TPU v7x, 512 devices: a whole 4x8x8 slice. The times are simulated.
512 devices in a mesh: rows: 32 (over x, y_hi, core), cols: 16 (over z, y_lo).
Axes of the slice: x: 4, y: 8 (y_hi: 4, y_lo: 2; y = y_hi * 2 + y_lo), z: 8, core: 2. Of those that a mesh axis runs over, the one named last changes fastest.
Arguments:
- greens: bfloat16 [512, 262144], P('cols', 'rows'), may hold values from -0.5 to 0.5
- slip_values: bfloat16 [8192, 128], P('cols'), may hold values from 0.5 to 4
- rupture_ids: int32 [8192, 128], P('cols'), may hold values from -1 to 511, as said below
- win_point: int32 [4096], P('rows'), may hold values from 0 to 1023, never falling along the last dimension, each value on 1 to 32 neighbouring positions
Outputs:
- window_peak: float32 [8192, 4096], P('cols', 'rows')
Inputs may be any that keep to these rules, and one draw needn't show every extreme that they name: `rupture_ids`: each row lists its sources as one run of consecutive source numbers in its first slots and -1 in the rest; some row fills all 128 slots. `win_point`: never falls along the windows; every point holds 1 to 32 consecutive windows and some point exactly 32.
All inputs are finite; a program needn't handle non-finite values.
Results may differ from a plain program's by a relative error of at most 0.0003.
Values may be sent and summed in bfloat16 or wider, within the bound.
No kernel may reach another device: no remote copies, remote signals or barrier semaphores. Data moves between devices by JAX's collectives and lax.ppermute only.
A program may use at most 64 MiB of HBM per device.

v0:
```python
import math

import jax
import jax.numpy as jnp
from jax import lax
from jax.sharding import Mesh
from jax.sharding import PartitionSpec as P

TSTEP = 64
COLS = ("cols_0", "cols_1")


def gathered_by_axis(value, axes, dim):
    for axis in reversed(axes):
        value = lax.all_gather(value, axis, axis=dim, tiled=True)
    return value


def extended(cells, sides, width):
    for axis, dim in sides:
        count = lax.axis_size(axis)
        ends = count - 1
        head = lax.slice_in_dim(cells, 0, width, axis=dim)
        tail = lax.slice_in_dim(cells, cells.shape[dim] - width, cells.shape[dim], axis=dim)
        cells = jnp.concatenate(
            [
                lax.ppermute(tail, axis, [(i, (i + 1) % count) for i in range(ends)]),
                cells,
                lax.ppermute(head, axis, [((i + 1) % count, i) for i in range(ends)]),
            ],
            axis=dim,
        )
    return cells


def spread_slips(slip_values, source_ids, width):
    count = source_ids.shape[0]
    slots = source_ids.shape[1]
    group = math.gcd(count, 64)
    sources = jnp.arange(width, dtype=jnp.int32)[None, None, :]
    values_grouped = slip_values.reshape(count // group, group, slots)
    ids_grouped = source_ids.reshape(count // group, group, slots)

    def one_group(operands):
        values, ids = operands
        onehot = (ids[:, :, None] == sources).astype(jnp.bfloat16)
        return jnp.einsum("kl,kls->ks", values, onehot, preferred_element_type=jnp.float32).astype(
            jnp.bfloat16
        )

    return lax.map(one_group, (values_grouped, ids_grouped)).reshape(count, width)


def window_maxima(dense, panel):
    scenarios = dense.shape[0]
    windows = panel.shape[1] // TSTEP
    group = math.gcd(windows, max(1, 512 // TSTEP))
    turns = windows // group
    span = group * TSTEP

    def one_turn(turn):
        piece = lax.dynamic_slice_in_dim(panel, turn * span, span, 1)
        wave = jnp.dot(dense, piece, preferred_element_type=jnp.float32)
        return jnp.max(wave.reshape(scenarios, group, TSTEP), axis=2)

    stacked = lax.map(one_turn, jnp.arange(turns, dtype=jnp.int32))
    return jnp.transpose(stacked, (1, 0, 2)).reshape(scenarios, windows)


def combine(earlier, later):
    flag = jnp.logical_or(earlier[0], later[0])
    value = jnp.where(later[0], later[1], jnp.maximum(earlier[1], later[1]))
    return (flag, value)


def local(greens, slip_values, rupture_ids, win_point):
    width = greens.shape[0] * lax.axis_size(COLS)
    dense = spread_slips(slip_values, rupture_ids, width)
    whole_panel = gathered_by_axis(greens, COLS, 0)
    window_max = window_maxima(dense, whole_panel)
    windows = window_max.shape[1]
    begins = jnp.concatenate([jnp.ones((1,), bool), win_point[1:] != win_point[:-1]])
    finals = jnp.concatenate([win_point[:-1] != win_point[1:], jnp.ones((1,), bool)])
    begin_flags = jnp.broadcast_to(begins[None, :], window_max.shape)
    final_flags = jnp.broadcast_to(finals[None, :], window_max.shape)
    forward = lax.associative_scan(combine, (begin_flags, window_max), axis=1)[1]
    backward = lax.associative_scan(combine, (final_flags, window_max), reverse=True, axis=1)[1]
    local_peak = jnp.maximum(forward, backward)
    edge_values = jnp.stack([backward[:, 0], forward[:, windows - 1]], axis=1)
    edge_points = jnp.stack([win_point[0] + 1, win_point[windows - 1] + 1]).astype(jnp.float32)[
        None, :
    ]
    padded_values, padded_points = (
        extended(edge_values, (("rows", 1),), 1),
        extended(edge_points, (("rows", 1),), 1),
    )
    point_code = (win_point + 1).astype(jnp.float32)[None, :]
    from_left = jnp.maximum(local_peak, padded_values[:, 0:1])
    local_peak = jnp.where(point_code == padded_points[0, 0], from_left, local_peak)
    from_right = jnp.maximum(local_peak, padded_values[:, 3:4])
    local_peak = jnp.where(point_code == padded_points[0, 3], from_right, local_peak)
    return local_peak


def solution(mesh):
    split = Mesh(mesh.devices.reshape(mesh.shape["rows"], 8, 2), ("rows", "cols_0", "cols_1"))
    in_specs = (P(COLS, "rows"), P(COLS, None), P(COLS, None), P("rows"))
    out_specs = P(COLS, "rows")
    return jax.shard_map(local, mesh=split, in_specs=in_specs, out_specs=out_specs, check_vma=False)
```

profile of v0, /device:TPU:6, one launch (start us, length us, event | category | flops | bytes accessed | tf_op | source)
XLA Modules:
  0.0 215.0 jit_solution(18331634613393556245)
XLA Ops:
  6.5 0.7 all-gather.3.cloned.1.call-update
  7.3 35.9 %all-gather.3.cloned.1.call-done = bf16[64,8192]{1,0:T(8,128)(2,1)} async-done(((bf16[32,8192]{1,0:T(8,128)(2,1)}), bf16[64,8192]{1,0:T(8,128)(2,1)}) %all-gather.3.cloned.1.call-update) | async-done | bytes 1048592 | tf_op jit(solution)/shard_map/all_gather | solution.py:15
  43.2 1.3 fusion.19
  46.5 4.3 %collective-permute-start = (f32[1,1]{1,0:T(1,128)}, f32[1,1]{1,0:T(1,128)}, u32[]{:S(2)}, u32[]{:S(2)}) collective-permute-start(f32[1,1]{1,0:T(1,128)} %get-tuple-element.101), channel_id=1, source_target_pairs={{16,0},{32,16},{48,32},{64,48},{80,64},{96,80},{112,96},{128,112},... | collective-permute-start | bytes 20 | tf_op jit(solution)/shard_map/ppermute | solution.py:29
  50.8 1.9 collective-permute-start.1
  52.7 0.8 slice_compare_fusion.1
  58.8 37.9 %while.22 = (s32[]{:T(128)}, bf16[8,64,512]{2,1,0:T(8,128)(2,1)S(1)}, bf16[8,64,128]{2,1,0:T(8,128)(2,1)}, s32[8,64,128]{2,1,0:T(8,128)}, s32[]{:T(128)}) while((s32[]{:T(128)}, bf16[8,64,512]{2,1,0:T(8,128)(2,1)S(1)}, bf16[8,64,128]{2,1,0:T(8,128)(2,1)}, s32[8,64,128]{2,1,0:T(8,128)}, s32[]{:T(128)}) %tuple.55), condition=%wide.region_1.2_spmd.clone, body=%wide.region_0.1_spmd.clone.sunk | while | flops 12582914 | bytes 409681 | solution.py:51
  58.8 0.8 dynamic-slice_bitcast_fusion.4
  59.5 0.7 dynamic-slice_bitcast_fusion.5
  60.2 3.2 %fusion.29 = bf16[64,1,512]{2,1,0:T(2,128)(2,1)S(1)} fusion(s32[64,128]{1,0:T(8,128)S(1)} %dynamic-slice_bitcast_fusion.4, bf16[64,128,1]{1,0,2:T(8,128)(2,1)S(1)} %dynamic-slice_bitcast_fusion.5), kind=kOutput, calls=%fused_computation.7.clone.1 | convolution fusion | flops 12582912 | bytes 114688 | tf_op jit(solution)/shard_map/while/body/eval_jaxpr/kl,kls->ks/dot_general | solution.py:47
  63.5 0.8 dynamic-slice_bitcast_fusion.4
  64.3 0.7 dynamic-slice_bitcast_fusion.5
  65.0 3.2 %fusion.29 = bf16[64,1,512]{2,1,0:T(2,128)(2,1)S(1)} fusion(s32[64,128]{1,0:T(8,128)S(1)} %dynamic-slice_bitcast_fusion.4, bf16[64,128,1]{1,0,2:T(8,128)(2,1)S(1)} %dynamic-slice_bitcast_fusion.5), kind=kOutput, calls=%fused_computation.7.clone.1 | convolution fusion | flops 12582912 | bytes 114688 | tf_op jit(solution)/shard_map/while/body/eval_jaxpr/kl,kls->ks/dot_general | solution.py:47
  68.2 0.8 dynamic-slice_bitcast_fusion.4
  69.0 0.7 dynamic-slice_bitcast_fusion.5
  69.7 3.2 %fusion.29 = bf16[64,1,512]{2,1,0:T(2,128)(2,1)S(1)} fusion(s32[64,128]{1,0:T(8,128)S(1)} %dynamic-slice_bitcast_fusion.4, bf16[64,128,1]{1,0,2:T(8,128)(2,1)S(1)} %dynamic-slice_bitcast_fusion.5), kind=kOutput, calls=%fused_computation.7.clone.1 | convolution fusion | flops 12582912 | bytes 114688 | tf_op jit(solution)/shard_map/while/body/eval_jaxpr/kl,kls->ks/dot_general | solution.py:47
  73.0 0.8 dynamic-slice_bitcast_fusion.4
  73.7 0.7 dynamic-slice_bitcast_fusion.5
  74.4 3.2 %fusion.29 = bf16[64,1,512]{2,1,0:T(2,128)(2,1)S(1)} fusion(s32[64,128]{1,0:T(8,128)S(1)} %dynamic-slice_bitcast_fusion.4, bf16[64,128,1]{1,0,2:T(8,128)(2,1)S(1)} %dynamic-slice_bitcast_fusion.5), kind=kOutput, calls=%fused_computation.7.clone.1 | convolution fusion | flops 12582912 | bytes 114688 | tf_op jit(solution)/shard_map/while/body/eval_jaxpr/kl,kls->ks/dot_general | solution.py:47
  77.7 0.8 dynamic-slice_bitcast_fusion.4
  78.5 0.7 dynamic-slice_bitcast_fusion.5
  79.2 3.2 %fusion.29 = bf16[64,1,512]{2,1,0:T(2,128)(2,1)S(1)} fusion(s32[64,128]{1,0:T(8,128)S(1)} %dynamic-slice_bitcast_fusion.4, bf16[64,128,1]{1,0,2:T(8,128)(2,1)S(1)} %dynamic-slice_bitcast_fusion.5), kind=kOutput, calls=%fused_computation.7.clone.1 | convolution fusion | flops 12582912 | bytes 114688 | tf_op jit(solution)/shard_map/while/body/eval_jaxpr/kl,kls->ks/dot_general | solution.py:47
  82.4 0.8 dynamic-slice_bitcast_fusion.4
  83.2 0.7 dynamic-slice_bitcast_fusion.5
  83.9 3.2 %fusion.29 = bf16[64,1,512]{2,1,0:T(2,128)(2,1)S(1)} fusion(s32[64,128]{1,0:T(8,128)S(1)} %dynamic-slice_bitcast_fusion.4, bf16[64,128,1]{1,0,2:T(8,128)(2,1)S(1)} %dynamic-slice_bitcast_fusion.5), kind=kOutput, calls=%fused_computation.7.clone.1 | convolution fusion | flops 12582912 | bytes 114688 | tf_op jit(solution)/shard_map/while/body/eval_jaxpr/kl,kls->ks/dot_general | solution.py:47
  87.2 0.8 dynamic-slice_bitcast_fusion.4
  87.9 0.7 dynamic-slice_bitcast_fusion.5
  88.6 3.2 %fusion.29 = bf16[64,1,512]{2,1,0:T(2,128)(2,1)S(1)} fusion(s32[64,128]{1,0:T(8,128)S(1)} %dynamic-slice_bitcast_fusion.4, bf16[64,128,1]{1,0,2:T(8,128)(2,1)S(1)} %dynamic-slice_bitcast_fusion.5), kind=kOutput, calls=%fused_computation.7.clone.1 | convolution fusion | flops 12582912 | bytes 114688 | tf_op jit(solution)/shard_map/while/body/eval_jaxpr/kl,kls->ks/dot_general | solution.py:47
  91.9 0.8 dynamic-slice_bitcast_fusion.4
  92.7 0.7 dynamic-slice_bitcast_fusion.5
  93.4 3.2 %fusion.29 = bf16[64,1,512]{2,1,0:T(2,128)(2,1)S(1)} fusion(s32[64,128]{1,0:T(8,128)S(1)} %dynamic-slice_bitcast_fusion.4, bf16[64,128,1]{1,0,2:T(8,128)(2,1)S(1)} %dynamic-slice_bitcast_fusion.5), kind=kOutput, calls=%fused_computation.7.clone.1 | convolution fusion | flops 12582912 | bytes 114688 | tf_op jit(solution)/shard_map/while/body/eval_jaxpr/kl,kls->ks/dot_general | solution.py:47
  96.6 46.6 %all-gather.5.cloned.1.call-done = bf16[512,8192]{1,0:T(8,128)(2,1)} async-done(((bf16[64,8192]{1,0:T(8,128)(2,1)}), bf16[512,8192]{1,0:T(8,128)(2,1)}) %all-gather.5.cloned.1.call-update) | async-done | bytes 8388624 | tf_op jit(solution)/shard_map/all_gather | solution.py:15
  143.2 45.8 %while.21 = (s32[]{:T(128)}, f32[16,512,8]{1,2,0:T(8,128)S(1)}, s32[16]{0:T(128)S(1)}, bf16[512,8192]{1,0:T(8,128)(2,1)}, bf16[512,512]{1,0:T(8,128)(2,1)S(1)}, ...) while((s32[]{:T(128)}, f32[16,512,8]{1,2,0:T(8,128)S(1)}, s32[16]{0:T(128)S(1)}, ...), condition=%wide.region_4.5_spmd, body=%wide.region_2.4_spmd.sunk | while | flops 268693504 | bytes 1097895 | solution.py:66
  144.5 1.5 bitcast_reduce_fusion.2
  146.1 0.7 dynamic_slice.28
  147.4 1.5 bitcast_reduce_fusion.2
  149.0 0.7 dynamic_slice.28
  150.2 1.5 bitcast_reduce_fusion.2
  151.8 0.7 dynamic_slice.28
  153.1 1.5 bitcast_reduce_fusion.2
  154.7 0.7 dynamic_slice.28
  156.0 1.5 bitcast_reduce_fusion.2
  157.5 0.7 dynamic_slice.28
  158.8 1.5 bitcast_reduce_fusion.2
  160.4 0.7 dynamic_slice.28
  161.7 1.5 bitcast_reduce_fusion.2
  163.3 0.7 dynamic_slice.28
  164.5 1.5 bitcast_reduce_fusion.2
  166.1 0.7 dynamic_slice.28
  167.4 1.5 bitcast_reduce_fusion.2
  169.0 0.7 dynamic_slice.28
  170.3 1.5 bitcast_reduce_fusion.2
  171.8 0.7 dynamic_slice.28
  173.1 1.5 bitcast_reduce_fusion.2
  176.0 1.5 bitcast_reduce_fusion.2
  178.8 1.5 bitcast_reduce_fusion.2
  181.7 1.5 bitcast_reduce_fusion.2
  184.6 1.5 bitcast_reduce_fusion.2
  187.4 1.5 bitcast_reduce_fusion.2
  194.1 5.2 %collective-permute-start.3 = (f32[512,1]{0,1:T(1,128)S(1)}, f32[512,1]{0,1:T(1,128)S(1)}, u32[]{:S(2)}, u32[]{:S(2)}) collective-permute-start(f32[512,1]{0,1:T(1,128)S(1)} %slice_add_fusion), channel_id=1, source_target_pairs={{16,0},{32,16},{48,32},{64,48},{80,64},{96,80},{112,96},{128,112},... | collective-permute-start | bytes 6152 | tf_op jit(solution)/shard_map/ppermute | solution.py:29
  199.3 1.9 collective-permute-start.2
  201.3 1.2 convert_compare_fusion.1
  202.7 4.5 %collective-permute-done.2 = f32[512,1]{0,1:T(1,128)S(1)} collective-permute-done((f32[512,1]{0,1:T(1,128)S(1)}, f32[512,1]{0,1:T(1,128)S(1)}, u32[]{:S(2)}, u32[]{:S(2)}) %collective-permute-start.2) | collective-permute-done | bytes 2080 | tf_op jit(solution)/shard_map/ppermute | solution.py:27
  207.3 0.8 copy.6
  (220 shorter events, 14.9 us)
Async XLA Ops:
  6.5 36.7 %all-gather.3.cloned.1.call-start = ((), (), s32[]{:S(2)}) async-start(), calls=%async_computation | async-start | bytes 1572864 | tf_op jit(solution)/shard_map/all_gather | solution.py:15
  7.3 136.0 %all-gather.5.cloned.1.call-start = ((), (), s32[]{:S(2)}) async-start(), calls=%async_computation.1 | async-start | bytes 9437184 | tf_op jit(solution)/shard_map/all_gather | solution.py:15
  46.5 154.8 %collective-permute-start = (f32[1,1]{1,0:T(1,128)}, f32[1,1]{1,0:T(1,128)}, u32[]{:S(2)}, u32[]{:S(2)}) collective-permute-start(f32[1,1]{1,0:T(1,128)} %get-tuple-element.101), channel_id=1, source_target_pairs={{16,0},{32,16},{48,32},{64,48},{80,64},{96,80},{112,96},{128,112},... | collective-permute-start | bytes 20 | tf_op jit(solution)/shard_map/ppermute | solution.py:29
  50.8 150.5 %collective-permute-start.1 = (f32[1,1]{1,0:T(1,128)}, f32[1,1]{1,0:T(1,128)}, u32[]{:S(2)}, u32[]{:S(2)}) collective-permute-start(f32[1,1]{1,0:T(1,128)} %get-tuple-element.102), channel_id=1, source_target_pairs={{0,16},{16,32},{32,48},{48,64},{64,80},{80,96},{96,112},{112,128},... | collective-permute-start | bytes 20 | tf_op jit(solution)/shard_map/ppermute | solution.py:27
  189.0 12.2 %copy-start = (s32[128]{0:T(128)S(1)}, s32[128]{0:T(128)}, u32[]{:S(2)}) copy-start(s32[128]{0:T(128)} %param.11) | copy-start | bytes 1540
  194.1 8.5 %collective-permute-start.3 = (f32[512,1]{0,1:T(1,128)S(1)}, f32[512,1]{0,1:T(1,128)S(1)}, u32[]{:S(2)}, u32[]{:S(2)}) collective-permute-start(f32[512,1]{0,1:T(1,128)S(1)} %slice_add_fusion), channel_id=1, source_target_pairs={{16,0},{32,16},{48,32},{64,48},{80,64},{96,80},{112,96},{128,112},... | collective-permute-start | bytes 6152 | tf_op jit(solution)/shard_map/ppermute | solution.py:29
  199.3 7.9 %collective-permute-start.2 = (f32[512,1]{0,1:T(1,128)S(1)}, f32[512,1]{0,1:T(1,128)S(1)}, u32[]{:S(2)}, u32[]{:S(2)}) collective-permute-start(f32[512,1]{0,1:T(1,128)S(1)} %slice_add_fusion.1), channel_id=1, source_target_pairs={{0,16},{16,32},{32,48},{48,64},{64,80},{80,96},{96,112},{112,128},... | collective-permute-start | bytes 6152 | tf_op jit(solution)/shard_map/ppermute | solution.py:27
Sparse Core Ops, SparseCore 0:
  9.4 33.7 all-gather.2
  45.3 97.9 all-gather.4
where the time goes:
time: 217 us; the launch traced here: 215 us
  waiting for transfers between devices  87.8 us (40%)
  matrix products  50.3 us (23%)
  local copies, waits for them, and re-layouts  32.3 us (15%)
  between operations  15.4 us (7%)
  starting transfers between devices  13.3 us (6%)
  loops' own time  10.8 us (5%)
  other arithmetic  5.05 us (2%)
    all_gather x2, waiting for transfers between devices, gathered_by_axis(): value = lax.all_gather(value, axis, axis=dim, tiled=True)  82.5 us
    dot_general x8, matrix products, one_group(): jnp.einsum('kl,kls->ks', values, onehot, preferred_element_type=jnp.float32)  25.7 us
    dot_general x16, matrix products, one_turn(): wave = jnp.dot(dense, piece, preferred_element_type=jnp.float32)  24.6 us
    another operation x1, loops' own time, window_maxima(): stacked = lax.map(one_turn, jnp.arange(turns, dtype=jnp.int32))  10.6 us
    dynamic_slice x16, local copies, waits for them, and re-layouts, window_maxima(): stacked = lax.map(one_turn, jnp.arange(turns, dtype=jnp.int32))  10.4 us
    ppermute x2, starting transfers between devices, extended(): lax.ppermute(head, axis, [((i + 1) % count, i) for i in range(ends)])  9.42 us
    eq x8, local copies, waits for them, and re-layouts, one_group(): onehot = (ids[:, :, None] == sources).astype(jnp.bfloat16)  6.11 us
    squeeze x8, local copies, waits for them, and re-layouts, spread_slips(): lax.map(one_group, (values_grouped, ids_grouped)).reshape(count, width)  5.75 us
  transfers between devices with their start and end apart: 6, of which 3 were waited for; matrix products, arithmetic and copies ran while one was open for 40% of the time, Pallas kernels for 0%

commit v1 on v0

v1 whole, which is shorter than its diff:
```python
import jax
import jax.numpy as jnp
from jax import lax
from jax.sharding import Mesh
from jax.sharding import PartitionSpec as P

TSTEP = 64
COLS = ("cols_0", "cols_1")
SPLIT = "cols_0"
SHARE = "cols_1"


def extended(cells, sides, width):
    for axis, dim in sides:
        count = lax.axis_size(axis)
        ends = count - 1
        head = lax.slice_in_dim(cells, 0, width, axis=dim)
        tail = lax.slice_in_dim(cells, cells.shape[dim] - width, cells.shape[dim], axis=dim)
        cells = jnp.concatenate(
            [
                lax.ppermute(tail, axis, [(i, (i + 1) % count) for i in range(ends)]),
                cells,
                lax.ppermute(head, axis, [((i + 1) % count, i) for i in range(ends)]),
            ],
            axis=dim,
        )
    return cells


def shifted_slips(values, starts, width):
    count, slots = values.shape
    dense = jnp.concatenate([values, jnp.zeros((count, width - slots), values.dtype)], axis=1)
    bits = max(1, (width - 1).bit_length())
    for bit in range(bits):
        step = 1 << bit
        rolled = jnp.concatenate([dense[:, width - step:], dense[:, : width - step]], axis=1)
        dense = jnp.where(((starts >> bit) & 1)[:, None] == 1, rolled, dense)
    return dense


def combine(earlier, later):
    flag = jnp.logical_or(earlier[0], later[0])
    value = jnp.where(later[0], later[1], jnp.maximum(earlier[1], later[1]))
    return (flag, value)


def point_peaks(window_max, win_point):
    windows = window_max.shape[1]
    begins = jnp.concatenate([jnp.ones((1,), bool), win_point[1:] != win_point[:-1]])
    finals = jnp.concatenate([win_point[:-1] != win_point[1:], jnp.ones((1,), bool)])
    begin_flags = jnp.broadcast_to(begins[None, :], window_max.shape)
    final_flags = jnp.broadcast_to(finals[None, :], window_max.shape)
    forward = lax.associative_scan(combine, (begin_flags, window_max), axis=1)[1]
    backward = lax.associative_scan(combine, (final_flags, window_max), reverse=True, axis=1)[1]
    local_peak = jnp.maximum(forward, backward)
    edge_values = jnp.stack([backward[:, 0], forward[:, windows - 1]], axis=1)
    edge_points = jnp.stack([win_point[0] + 1, win_point[windows - 1] + 1]).astype(jnp.float32)[
        None, :
    ]
    padded_values, padded_points = (
        extended(edge_values, (("rows", 1),), 1),
        extended(edge_points, (("rows", 1),), 1),
    )
    point_code = (win_point + 1).astype(jnp.float32)[None, :]
    from_left = jnp.maximum(local_peak, padded_values[:, 0:1])
    local_peak = jnp.where(point_code == padded_points[0, 0], from_left, local_peak)
    from_right = jnp.maximum(local_peak, padded_values[:, 3:4])
    local_peak = jnp.where(point_code == padded_points[0, 3], from_right, local_peak)
    return local_peak


def local(greens, slip_values, rupture_ids, win_point):
    parts = lax.axis_size(SPLIT)
    shares = lax.axis_size(SHARE)
    own_sources, rows = greens.shape
    width = own_sources * parts * shares
    scen = slip_values.shape[0]
    block = rows // parts

    listed = rupture_ids >= 0
    values = jnp.where(listed, slip_values, jnp.zeros_like(slip_values))
    starts = jnp.maximum(rupture_ids[:, 0], 0)
    all_values = lax.all_gather(values, SPLIT, axis=0, tiled=True)
    all_starts = lax.all_gather(starts, SPLIT, axis=0, tiled=True)

    pieces = greens.reshape(own_sources, parts, block)
    pieces = lax.all_to_all(pieces, SPLIT, 1, 0, tiled=True)
    pieces = pieces.reshape(parts, own_sources, block)
    pieces = lax.all_gather(pieces, SHARE, axis=0, tiled=False)
    panel_t = jnp.transpose(pieces, (3, 1, 0, 2)).reshape(block, width)

    dense = shifted_slips(all_values, all_starts, width)
    wave_t = lax.dot_general(
        panel_t, dense, (((1,), (1,)), ((), ())), preferred_element_type=jnp.float32
    )
    win_block = block // TSTEP
    maxima = jnp.max(wave_t.reshape(win_block, TSTEP, parts * scen), axis=1)
    maxima = maxima.reshape(win_block, parts, scen)
    maxima = lax.all_to_all(maxima, SPLIT, 1, 0, tiled=True)
    window_max = maxima.reshape(parts * win_block, scen).T
    return point_peaks(window_max, win_point)


def solution(mesh):
    split = Mesh(mesh.devices.reshape(mesh.shape["rows"], 8, 2), ("rows", "cols_0", "cols_1"))
    in_specs = (P(COLS, "rows"), P(COLS, None), P(COLS, None), P("rows"))
    out_specs = P(COLS, "rows")
    return jax.shard_map(local, mesh=split, in_specs=in_specs, out_specs=out_specs, check_vma=False)
```

time: 217 us -> 164 us (0.76)
  the two profiles are of different devices: /device:TPU:6 before, /device:TPU:21 now
where the time goes in v1:
time: 164 us
  other arithmetic  42.9 us (26%)
  blocking collectives  40.5 us (25%)
  starting transfers between devices  31.8 us (19%)
  local copies, waits for them, and re-layouts  22.3 us (14%)
  between operations  15.6 us (10%)
  matrix products  6.99 us (4%)
  waiting for transfers between devices  3.65 us (2%)
    all_gather x1, blocking collectives, local(): all_starts = lax.all_gather(starts, SPLIT, axis=0, tiled=True)  40.5 us
    select_n x8, other arithmetic, shifted_slips(): dense = jnp.where((starts >> bit & 1)[:, None] == 1, rolled, dense)  30.8 us
    all_to_all x1, starting transfers between devices, local(): pieces = lax.all_to_all(pieces, SPLIT, 1, 0, tiled=True)  10 us
    ppermute x2, starting transfers between devices, extended(): lax.ppermute(head, axis, [((i + 1) % count, i) for i in range(ends)])  8.94 us
    ppermute x2, starting transfers between devices, extended(): lax.ppermute(tail, axis, [(i, (i + 1) % count) for i in range(ends)])  7.7 us
    dot_general x1, matrix products, local(): lax.dot_general(panel_t, dense, (((1,), (1,)), ((), ())), preferred_eleme...  6.99 us
    eq x1, other arithmetic, shifted_slips(): dense = jnp.where((starts >> bit & 1)[:, None] == 1, rolled, dense)  5.06 us
    all_to_all x1, starting transfers between devices, local(): maxima = lax.all_to_all(maxima, SPLIT, 1, 0, tiled=True)  5.05 us
  transfers between devices with their start and end apart: 8, of which 1 were waited for; matrix products, arithmetic and copies ran while one was open for 35% of the time, Pallas kernels for 0%

profile of v1, /device:TPU:21, one launch (start us, length us, event | category | flops | bytes accessed | tf_op | source)
XLA Modules:
  0.0 163.6 jit_solution(4431919119020084951)
XLA Ops:
  6.5 1.7 %compare_select_fusion = bf16[512,128]{1,0:T(8,128)(2,1)} fusion(bf16[512,128]{1,0:T(8,128)(2,1)} %param.5, s32[512,128]{1,0:T(8,128)} %param.6), kind=kLoop, calls=%fused_computation.38 | loop fusion | flops 131072 | bytes 524288 | tf_op jit(solution)/shard_map/jit(_where)/select_n | solution.py:81
  8.3 1.9 %copy.27 = bf16[4,8,8,1024]{3,2,0,1:T(8,128)(2,1)} copy(bf16[4,8,8,1024]{3,2,1,0:T(8,128)(2,1)} %bitcast.57) | data formatting | bytes 1048576 | tf_op jit(solution)/shard_map/reshape | solution.py:86
  10.2 10.0 %all-to-all-start = ((bf16[32,8,1024]{2,0,1:T(8,128)(2,1)}), bf16[32,8,1024]{2,0,1:T(8,128)(2,1)S(1)}, u32[]{:S(2)}, u32[]{:S(2)}) async-start(bf16[32,8,1024]{2,0,1:T(8,128)(2,1)} %bitcast.35), calls=%async_computation | async-start | bytes 1048576 | tf_op jit(solution)/shard_map/all_to_all | solution.py:87
  20.3 1.3 fusion.22
  22.8 1.0 slice_maximum_fusion
  23.8 40.5 %all-gather = s32[4096,1]{1,0:T(8,128)S(1)} all-gather(s32[512,1]{1,0:T(8,128)S(1)} %slice_maximum_fusion), channel_id=2, replica_groups=mesh['rows'=32,'cols_0'=8,'cols_1'=2] {'cols_0'}, dimensions={0}, use_global_device_ids=true | all-gather | bytes 18432 | tf_op jit(solution)/shard_map/all_gather | solution.py:84
  64.4 5.1 %fusion.4 = (pred[4096]{0:T(1024)(128)(4,1)S(1)}, pred[4096]{0:T(1024)(128)(4,1)S(1)}, pred[4096]{0:T(1024)(128)(4,1)S(1)}, pred[4096]{0:T(1024)(128)(4,1)S(1)},...) fusion(s32[4096,1]{1,0:T(8,128)S(1)} %all-gather), kind=kLoop, calls=%fused_computation.24 | loop fusion | flops 110592 | bytes 53248 | tf_op jit(solution)/shard_map/eq | solution.py:37
  69.4 0.8 copy-done.2
  70.3 1.7 %pad_slice_fusion = bf16[4096,511]{1,0:T(8,128)(2,1)S(1)} fusion(bf16[4096,128]{1,0:T(8,128)(2,1)} %all-gather.5.cloned.1.call-done), kind=kLoop, calls=%fused_computation.2 | loop fusion | bytes 5234688 | tf_op jit(solution)/shard_map/slice | solution.py:36
  72.0 4.1 %pad_select_fusion = bf16[4096,512]{1,0:T(8,128)(2,1)S(1)} fusion(bf16[4096,128]{1,0:T(8,128)(2,1)S(1)} %copy-done.1, bf16[4096,511]{1,0:T(8,128)(2,1)S(1)} %pad_slice_fusion, pred[4096]{0:T(1024)(128)(4,1)S(1)} %get-tuple-element.13), kind=kLoop, calls=%fused_computation.1 | loop fusion | flops 2097152 | bytes 9433088 | tf_op jit(solution)/shard_map/jit(_where)/select_n | solution.py:37
  76.1 0.4 slice.575
  76.4 4.0 %maximum_select_fusion = bf16[4096,512]{1,0:T(8,128)(2,1)S(1)} fusion(bf16[4096,512]{1,0:T(8,128)(2,1)S(1)} %pad_select_fusion, bf16[4096,510]{1,0:T(8,128)(2,1)S(1)} %bitcast.43, bf16[4096,2]{1,0:T(8,128)(2,1)S(1)} %slice.575, pred[4096]{0:T(1024)(128)(4,1)S(1)} %get-tuple-element.6), kind=kLoop, calls=%fused_computation.3 | loop fusion | flops 10485760 | bytes 12587008 | tf_op jit(solution)/shard_map/jit(_where)/select_n | solution.py:37
  80.5 0.4 slice.577
  80.8 4.0 %maximum_select_fusion.1 = bf16[4096,512]{1,0:T(8,128)(2,1)S(1)} fusion(bf16[4096,512]{1,0:T(8,128)(2,1)S(1)} %maximum_select_fusion, bf16[4096,508]{1,0:T(8,128)(2,1)S(1)} %bitcast.44, bf16[4096,4]{1,0:T(8,128)(2,1)S(1)} %slice.577, pred[4096]{0:T(1024)(128)(4,1)S(1)} %get-tuple-element.7), kind=kLoop, calls=%fused_computation.4 | loop fusion | flops 10485760 | bytes 12587008 | tf_op jit(solution)/shard_map/jit(_where)/select_n | solution.py:37
  84.9 0.4 slice.579
  85.2 4.0 %maximum_select_fusion.2 = bf16[4096,512]{1,0:T(8,128)(2,1)S(1)} fusion(bf16[4096,512]{1,0:T(8,128)(2,1)S(1)} %maximum_select_fusion.1, bf16[4096,504]{1,0:T(8,128)(2,1)S(1)} %bitcast.45, bf16[4096,8]{1,0:T(8,128)(2,1)S(1)} %slice.579, pred[4096]{0:T(1024)(128)(4,1)S(1)} %get-tuple-element.8), kind=kLoop, calls=%fused_computation.5 | loop fusion | flops 10485760 | bytes 12587008 | tf_op jit(solution)/shard_map/jit(_where)/select_n | solution.py:37
  89.3 0.4 slice.581
  89.6 4.0 %maximum_select_fusion.3 = bf16[4096,512]{1,0:T(8,128)(2,1)S(1)} fusion(bf16[4096,512]{1,0:T(8,128)(2,1)S(1)} %maximum_select_fusion.2, bf16[4096,496]{1,0:T(8,128)(2,1)S(1)} %bitcast.46, bf16[4096,16]{1,0:T(8,128)(2,1)S(1)} %slice.581, pred[4096]{0:T(1024)(128)(4,1)S(1)} %get-tuple-element.9), kind=kLoop, calls=%fused_computation.6 | loop fusion | flops 10485760 | bytes 12587008 | tf_op jit(solution)/shard_map/jit(_where)/select_n | solution.py:37
  93.7 0.4 slice.583
  94.0 4.0 %maximum_select_fusion.4 = bf16[4096,512]{1,0:T(8,128)(2,1)S(1)} fusion(bf16[4096,512]{1,0:T(8,128)(2,1)S(1)} %maximum_select_fusion.3, bf16[4096,480]{1,0:T(8,128)(2,1)S(1)} %bitcast.47, bf16[4096,32]{1,0:T(8,128)(2,1)S(1)} %slice.583, pred[4096]{0:T(1024)(128)(4,1)S(1)} %get-tuple-element.10), kind=kLoop, calls=%fused_computation.7 | loop fusion | flops 10485760 | bytes 12587008 | tf_op jit(solution)/shard_map/jit(_where)/select_n | solution.py:37
  98.1 0.4 slice.585
  98.4 4.2 %maximum_select_fusion.5 = bf16[4096,512]{1,0:T(8,128)(2,1)S(1)} fusion(bf16[4096,512]{1,0:T(8,128)(2,1)S(1)} %maximum_select_fusion.4, bf16[4096,448]{1,0:T(8,128)(2,1)S(1)} %bitcast.48, bf16[4096,64]{1,0:T(8,128)(2,1)S(1)} %slice.585, pred[4096]{0:T(1024)(128)(4,1)S(1)} %get-tuple-element.11), kind=kLoop, calls=%fused_computation.8 | loop fusion | flops 10485760 | bytes 12587008 | tf_op jit(solution)/shard_map/jit(_where)/select_n | solution.py:37
  102.7 0.3 slice.588
  103.0 0.1 slice.587
  103.1 2.2 %maximum_select_fusion.6 = bf16[4096,512]{1,0:T(8,128)(2,1)S(1)} fusion(bf16[4096,512]{1,0:T(8,128)(2,1)S(1)} %maximum_select_fusion.5, bf16[4096,384]{1,0:T(8,128)(2,1)S(1)} %slice.588, bf16[4096,128]{1,0:T(8,128)(2,1)S(1)} %slice.587, pred[4096]{0:T(1024)(128)(4,1)S(1)} %get-tuple-element.12), kind=kLoop, calls=%fused_computation.9 | loop fusion | flops 10485760 | bytes 12587008 | tf_op jit(solution)/shard_map/jit(_where)/select_n | solution.py:37
  105.4 1.9 %copy-done = bf16[4096,512]{1,0:T(8,128)(2,1)} copy-done((bf16[4096,512]{1,0:T(8,128)(2,1)}, bf16[4096,512]{1,0:T(8,128)(2,1)S(1)}, u32[]{:S(2)}) %copy-start) | copy-done | bytes 4194328
  107.3 1.6 fusion.17
  108.9 1.3 copy.20
  110.2 7.0 %bitcast_reduce_fusion = f32[16,4096]{1,0:T(8,128)S(1)} fusion(bf16[1024,512]{0,1:T(8,128)(2,1)S(1)} %bitcast.56, bf16[4096,512]{1,0:T(8,128)(2,1)} %copy-done, bf16[4096,256]{1,0:T(8,128)(2,1)} %get-tuple-element.15, bf16[4096,256]{1,0:T(8,128)(2,1)S(1)} %get-tuple-element.14, pred[4096]{0:T(1024)(128)(4,1)S(1)} %get-tuple-element.5), kind=kOutput, calls=%fused_computation | convolution fusion | flops 4309581824 | bytes 9703424 | tf_op jit(solution)/shard_map/dot_general | solution.py:93
  117.2 0.7 copy.28
  118.0 5.1 %all-to-all-start.1 = ((f32[16,8,512]{2,0,1:T(8,128)}), f32[16,8,512]{2,0,1:T(8,128)S(1)}, u32[]{:S(2)}, u32[]{:S(2)}) async-start(f32[16,8,512]{2,0,1:T(8,128)} %bitcast.36), calls=%async_computation.1 | async-start | bytes 524288 | tf_op jit(solution)/shard_map/all_to_all | solution.py:99
  123.0 0.6 fusion.21
  123.6 7.0 %collective-permute-start = (f32[1,1]{1,0:T(1,128)}, f32[1,1]{1,0:T(1,128)}, u32[]{:S(2)}, u32[]{:S(2)}) collective-permute-start(f32[1,1]{1,0:T(1,128)} %get-tuple-element.28), channel_id=1, source_target_pairs={{16,0},{32,16},{48,32},{64,48},{80,64},{96,80},{112,96},{128,112},... | collective-permute-start | bytes 20 | tf_op jit(solution)/shard_map/ppermute | solution.py:23
  130.6 5.1 %collective-permute-start.1 = (f32[1,1]{1,0:T(1,128)}, f32[1,1]{1,0:T(1,128)}, u32[]{:S(2)}, u32[]{:S(2)}) collective-permute-start(f32[1,1]{1,0:T(1,128)} %get-tuple-element.29), channel_id=1, source_target_pairs={{0,16},{16,32},{32,48},{48,64},{64,80},{80,96},{96,112},{112,128},... | collective-permute-start | bytes 20 | tf_op jit(solution)/shard_map/ppermute | solution.py:21
  136.0 0.2 slice.468
  136.1 0.2 slice.472
  136.3 0.1 slice.475
  136.4 0.1 slice.479
  136.6 0.1 slice.482
  136.7 0.1 slice.486
  137.4 0.6 slice.501
  138.2 0.1 slice.480
  138.3 0.1 slice.473
  138.5 0.2 slice.466
  138.7 0.2 slice.523
  138.9 0.2 slice.528
  139.1 0.1 slice.524
  139.4 0.1 slice.529
  140.1 0.2 slice.519
  140.3 0.6 slice.509
  141.0 0.2 slice.520
  142.2 0.2 slice.467
  142.4 0.1 slice.525
  142.5 0.1 slice.526
  143.4 0.6 broadcast_select_fusion
  144.0 0.6 fusion.19
  145.5 2.6 %collective-permute-start.2 = (f32[512,1]{0,1:T(1,128)S(1)}, f32[512,1]{0,1:T(1,128)S(1)}, u32[]{:S(2)}, u32[]{:S(2)}) collective-permute-start(f32[512,1]{0,1:T(1,128)S(1)} %slice_add_fusion.1), channel_id=1, source_target_pairs={{0,16},{16,32},{32,48},{48,64},{64,80},{80,96},{96,112},{112,128},... | collective-permute-start | bytes 6152 | tf_op jit(solution)/shard_map/ppermute | solution.py:21
  148.5 0.2 slice.522
  148.8 1.9 %collective-permute-start.3 = (f32[512,1]{0,1:T(1,128)S(1)}, f32[512,1]{0,1:T(1,128)S(1)}, u32[]{:S(2)}, u32[]{:S(2)}) collective-permute-start(f32[512,1]{0,1:T(1,128)S(1)} %slice_add_fusion), channel_id=1, source_target_pairs={{16,0},{32,16},{48,32},{64,48},{80,64},{96,80},{112,96},{128,112},... | collective-permute-start | bytes 6152 | tf_op jit(solution)/shard_map/ppermute | solution.py:23
  150.8 1.3 convert_compare_fusion.1
  152.1 0.1 rev.2
  152.3 3.6 %collective-permute-done.3 = f32[512,1]{0,1:T(1,128)S(1)} collective-permute-done((f32[512,1]{0,1:T(1,128)S(1)}, f32[512,1]{0,1:T(1,128)S(1)}, u32[]{:S(2)}, u32[]{:S(2)}) %collective-permute-start.3) | collective-permute-done | bytes 2080 | tf_op jit(solution)/shard_map/ppermute | solution.py:23
  155.8 0.1 maximum_select_fusion.11
  156.0 0.8 copy.22
  (172 shorter events, 4.8 us)
Async XLA Ops:
  6.5 63.7 %all-gather.5.cloned.1.call-start = ((), (), s32[]{:S(2)}) async-start(), calls=%async_computation.2 | async-start | bytes 1179648 | tf_op jit(solution)/shard_map/all_gather | solution.py:83
  10.2 59.3 %all-to-all-start = ((bf16[32,8,1024]{2,0,1:T(8,128)(2,1)}), bf16[32,8,1024]{2,0,1:T(8,128)(2,1)S(1)}, u32[]{:S(2)}, u32[]{:S(2)}) async-start(bf16[32,8,1024]{2,0,1:T(8,128)(2,1)} %bitcast.35), calls=%async_computation | async-start | bytes 1048576 | tf_op jit(solution)/shard_map/all_to_all | solution.py:87
  20.2 88.7 %all-gather.7.cloned.1.call-start = ((), (), s32[]{:S(2)}) async-start(), calls=%async_computation.3 | async-start | bytes 1572864 | tf_op jit(solution)/shard_map/all_gather | solution.py:89
  69.4 0.8 copy-start.2
  70.3 1.7 %copy-start.1 = (bf16[4096,128]{1,0:T(8,128)(2,1)S(1)}, bf16[4096,128]{1,0:T(8,128)(2,1)}, u32[]{:S(2)}) copy-start(bf16[4096,128]{1,0:T(8,128)(2,1)} %all-gather.5.cloned.1.call-done) | copy-start | bytes 3145732
  105.4 1.9 %copy-start = (bf16[4096,512]{1,0:T(8,128)(2,1)}, bf16[4096,512]{1,0:T(8,128)(2,1)S(1)}, u32[]{:S(2)}) copy-start(bf16[4096,512]{1,0:T(8,128)(2,1)S(1)} %maximum_select_fusion.6) | copy-start | bytes 12582916
  110.2 25.6 %copy-start.3 = (s32[128]{0:T(128)S(1)}, s32[128]{0:T(128)}, u32[]{:S(2)}) copy-start(s32[128]{0:T(128)} %param.7) | copy-start | bytes 1540
  118.0 23.2 %all-to-all-start.1 = ((f32[16,8,512]{2,0,1:T(8,128)}), f32[16,8,512]{2,0,1:T(8,128)S(1)}, u32[]{:S(2)}, u32[]{:S(2)}) async-start(f32[16,8,512]{2,0,1:T(8,128)} %bitcast.36), calls=%async_computation.1 | async-start | bytes 524288 | tf_op jit(solution)/shard_map/all_to_all | solution.py:99
  123.6 27.2 %collective-permute-start = (f32[1,1]{1,0:T(1,128)}, f32[1,1]{1,0:T(1,128)}, u32[]{:S(2)}, u32[]{:S(2)}) collective-permute-start(f32[1,1]{1,0:T(1,128)} %get-tuple-element.28), channel_id=1, source_target_pairs={{16,0},{32,16},{48,32},{64,48},{80,64},{96,80},{112,96},{128,112},... | collective-permute-start | bytes 20 | tf_op jit(solution)/shard_map/ppermute | solution.py:23
  130.6 20.1 %collective-permute-start.1 = (f32[1,1]{1,0:T(1,128)}, f32[1,1]{1,0:T(1,128)}, u32[]{:S(2)}, u32[]{:S(2)}) collective-permute-start(f32[1,1]{1,0:T(1,128)} %get-tuple-element.29), channel_id=1, source_target_pairs={{0,16},{16,32},{32,48},{48,64},{64,80},{80,96},{96,112},{112,128},... | collective-permute-start | bytes 20 | tf_op jit(solution)/shard_map/ppermute | solution.py:21
  145.5 6.8 %collective-permute-start.2 = (f32[512,1]{0,1:T(1,128)S(1)}, f32[512,1]{0,1:T(1,128)S(1)}, u32[]{:S(2)}, u32[]{:S(2)}) collective-permute-start(f32[512,1]{0,1:T(1,128)S(1)} %slice_add_fusion.1), channel_id=1, source_target_pairs={{0,16},{16,32},{32,48},{48,64},{64,80},{80,96},{96,112},{112,128},... | collective-permute-start | bytes 6152 | tf_op jit(solution)/shard_map/ppermute | solution.py:21
  148.8 7.0 %collective-permute-start.3 = (f32[512,1]{0,1:T(1,128)S(1)}, f32[512,1]{0,1:T(1,128)S(1)}, u32[]{:S(2)}, u32[]{:S(2)}) collective-permute-start(f32[512,1]{0,1:T(1,128)S(1)} %slice_add_fusion), channel_id=1, source_target_pairs={{16,0},{32,16},{48,32},{64,48},{80,64},{96,80},{112,96},{128,112},... | collective-permute-start | bytes 6152 | tf_op jit(solution)/shard_map/ppermute | solution.py:23
Sparse Core Ops, SparseCore 0:
  9.4 47.3 all-gather.4
  70.4 32.4 all-gather.6

commit v2 on v1

--- a/solution.py
+++ b/solution.py
@@ -1,6 +1,8 @@
 import jax
 import jax.numpy as jnp
 from jax import lax
+from jax.experimental import pallas as pl
+from jax.experimental.pallas import tpu as pltpu
 from jax.sharding import Mesh
 from jax.sharding import PartitionSpec as P
 
@@ -8,6 +10,7 @@
 COLS = ("cols_0", "cols_1")
 SPLIT = "cols_0"
 SHARE = "cols_1"
+CODE = 32
 
 
 def extended(cells, sides, width):
@@ -27,15 +30,36 @@
     return cells
 
 
-def shifted_slips(values, starts, width):
-    count, slots = values.shape
-    dense = jnp.concatenate([values, jnp.zeros((count, width - slots), values.dtype)], axis=1)
-    bits = max(1, (width - 1).bit_length())
-    for bit in range(bits):
-        step = 1 << bit
-        rolled = jnp.concatenate([dense[:, width - step:], dense[:, : width - step]], axis=1)
-        dense = jnp.where(((starts >> bit) & 1)[:, None] == 1, rolled, dense)
-    return dense
+def wave_kernel(gt_ref, a_ref, o_ref):
+    slots = a_ref.shape[0] - 16
+    width = gt_ref.shape[1]
+    lanes = a_ref.shape[1]
+    code = a_ref[slots:slots + 16, :].astype(jnp.float32)
+    start = (code[0:1] * CODE + code[1:2]).astype(jnp.int32)
+    dense = jnp.concatenate(
+        [a_ref[0:slots, :].astype(jnp.float32), jnp.zeros((width - slots, lanes), jnp.float32)], axis=0
+    )
+    for bit in range(max(1, (width - 1).bit_length())):
+        rolled = pltpu.roll(dense, 1 << bit, 0)
+        dense = jnp.where(((start >> bit) & 1) == 1, rolled, dense)
+    wave = jnp.dot(gt_ref[...], dense.astype(jnp.bfloat16), preferred_element_type=jnp.float32)
+    rows = wave.shape[0]
+    o_ref[...] = jnp.max(wave.reshape(rows // TSTEP, TSTEP, lanes), axis=1)
+
+
+def wave_maxima(panel_t, coded):
+    parts, height, lanes = coded.shape
+    rows, width = panel_t.shape
+    return pl.pallas_call(
+        wave_kernel,
+        grid=(parts,),
+        in_specs=[
+            pl.BlockSpec((rows, width), lambda p: (0, 0)),
+            pl.BlockSpec((None, height, lanes), lambda p: (p, 0, 0)),
+        ],
+        out_specs=pl.BlockSpec((None, rows // TSTEP, lanes), lambda p: (p, 0, 0)),
+        out_shape=jax.ShapeDtypeStruct((parts, rows // TSTEP, lanes), jnp.float32),
+    )(panel_t, coded)
 
 
 def combine(earlier, later):
@@ -80,8 +104,9 @@
     listed = rupture_ids >= 0
     values = jnp.where(listed, slip_values, jnp.zeros_like(slip_values))
     starts = jnp.maximum(rupture_ids[:, 0], 0)
-    all_values = lax.all_gather(values, SPLIT, axis=0, tiled=True)
-    all_starts = lax.all_gather(starts, SPLIT, axis=0, tiled=True)
+    code = jnp.stack([starts // CODE, starts % CODE]).astype(jnp.bfloat16)
+    coded = jnp.concatenate([values.T, code, jnp.zeros((14, scen), jnp.bfloat16)], axis=0)
+    coded = lax.all_gather(coded, SPLIT, axis=0, tiled=False)
 
     pieces = greens.reshape(own_sources, parts, block)
     pieces = lax.all_to_all(pieces, SPLIT, 1, 0, tiled=True)
@@ -89,15 +114,9 @@
     pieces = lax.all_gather(pieces, SHARE, axis=0, tiled=False)
     panel_t = jnp.transpose(pieces, (3, 1, 0, 2)).reshape(block, width)
 
-    dense = shifted_slips(all_values, all_starts, width)
-    wave_t = lax.dot_general(
-        panel_t, dense, (((1,), (1,)), ((), ())), preferred_element_type=jnp.float32
-    )
-    win_block = block // TSTEP
-    maxima = jnp.max(wave_t.reshape(win_block, TSTEP, parts * scen), axis=1)
-    maxima = maxima.reshape(win_block, parts, scen)
-    maxima = lax.all_to_all(maxima, SPLIT, 1, 0, tiled=True)
-    window_max = maxima.reshape(parts * win_block, scen).T
+    maxima = wave_maxima(panel_t, coded)
+    maxima = lax.all_to_all(maxima, SPLIT, 0, 0, tiled=True)
+    window_max = maxima.reshape(-1, scen).T
     return point_peaks(window_max, win_point)
 
 

time: 164 us -> 158 us (0.963)
  the two profiles are of different devices: /device:TPU:21 before, /device:TPU:6 now
where the time goes in v2:
time: 158 us; the launch traced here: 157 us
  waiting for transfers between devices  68.6 us (43%)
  blocking collectives  27.8 us (18%)
  starting transfers between devices  16.3 us (10%)
  between operations  15.5 us (10%)
  local copies, waits for them, and re-layouts  13.2 us (8%)
  Pallas kernels  9.87 us (6%)
  other arithmetic  5.63 us (4%)
    all_gather x1, waiting for transfers between devices, local(): coded = lax.all_gather(coded, SPLIT, axis=0, tiled=False)  42 us
    all_to_all x1, blocking collectives, local(): pieces = lax.all_to_all(pieces, SPLIT, 1, 0, tiled=True)  27.8 us
    all_gather x1, waiting for transfers between devices, local(): pieces = lax.all_gather(pieces, SHARE, axis=0, tiled=False)  21.9 us
    pallas_call x1, Pallas kernels, wave_maxima(): pl.pallas_call(wave_kernel, grid=(parts,), in_specs=[pl.BlockSpec((rows,...  9.87 us
    ppermute x2, starting transfers between devices, extended(): lax.ppermute(head, axis, [((i + 1) % count, i) for i in range(ends)])  7.93 us
    ppermute x2, waiting for transfers between devices, extended(): lax.ppermute(tail, axis, [(i, (i + 1) % count) for i in range(ends)])  4.49 us
    ppermute x2, starting transfers between devices, extended(): lax.ppermute(tail, axis, [(i, (i + 1) % count) for i in range(ends)])  4.33 us
    all_to_all x1, starting transfers between devices, local(): maxima = lax.all_to_all(maxima, SPLIT, 0, 0, tiled=True)  4.01 us
  transfers between devices with their start and end apart: 7, of which 4 were waited for; matrix products, arithmetic and copies ran while one was open for 11% of the time, Pallas kernels for 0%

profile of v2, /device:TPU:6, one launch (start us, length us, event | category | flops | bytes accessed | tf_op | source)
XLA Modules:
  0.0 157.0 jit_solution(7277538674197251738)
XLA Ops:
  6.5 1.1 copy.37
  7.7 27.8 %all_to_all.20 = bf16[32,8,1024]{2,0,1:T(8,128)(2,1)} all-to-all(bf16[32,8,1024]{2,0,1:T(8,128)(2,1)S(1)} %bitcast.36), channel_id=1, replica_groups=mesh['rows'=32,'cols_0'=8,'cols_1'=2] {'cols_0'}, dimensions={1} | all-to-all | bytes 1048576 | tf_op jit(solution)/shard_map/all_to_all | solution.py:112
  35.6 0.1 copy.32
  35.7 0.1 copy.31
  36.0 0.2 fusion
  36.1 0.2 shift-right-logical_reduce_fusion
  36.4 0.8 maximum_maximum_fusion
  37.2 0.6 fusion.11
  39.1 21.9 %all-gather.5.cloned.1.call-done = bf16[16,32,1,1024]{3,1,2,0:T(8,128)(2,1)} async-done(((bf16[8,32,1,1024]{3,1,2,0:T(8,128)(2,1)}), bf16[16,32,1,1024]{3,1,2,0:T(8,128)(2,1)}) %all-gather.5.cloned.1.call-update) | async-done | bytes 1048592 | tf_op jit(solution)/shard_map/all_gather | solution.py:114
  61.0 1.3 copy.30
  62.3 1.3 copy.33.gt_ref
  63.6 42.0 %all-gather.7.cloned.1.call-done = bf16[1152,512]{1,0:T(8,128)(2,1)} async-done(((bf16[144,512]{1,0:T(8,128)(2,1)}), bf16[1152,512]{1,0:T(8,128)(2,1)}) %all-gather.7.cloned.1.call-update) | async-done | bytes 1179664 | tf_op jit(solution)/shard_map/all_gather | solution.py:109
  105.7 9.9 %shard_map.46 = f32[8,16,512]{2,1,0:T(8,128)} custom-call(bf16[1024,512]{1,0:T(8,128)(2,1)} %copy.33.gt_ref, bf16[8,144,512]{2,1,0:T(8,128)(2,1)} %bitcast.37), custom_call_target="tpu_custom_call" | custom-call | tf_op jit(solution)/shard_map/pallas_call | solution.py:53
  115.5 4.0 %all-to-all-start.1 = ((f32[8,16,512]{2,1,0:T(8,128)}), f32[8,16,512]{2,1,0:T(8,128)S(1)}, u32[]{:S(2)}, u32[]{:S(2)}) async-start(f32[8,16,512]{2,1,0:T(8,128)} %shard_map.46), calls=%async_computation.1 | async-start | bytes 524288 | tf_op jit(solution)/shard_map/all_to_all | solution.py:118
  119.5 0.6 fusion.10
  120.1 1.9 %collective-permute-start = (f32[1,1]{1,0:T(1,128)}, f32[1,1]{1,0:T(1,128)}, u32[]{:S(2)}, u32[]{:S(2)}) collective-permute-start(f32[1,1]{1,0:T(1,128)} %get-tuple-element.21), channel_id=1, source_target_pairs={{16,0},{32,16},{48,32},{64,48},{80,64},{96,80},{112,96},{128,112},... | collective-permute-start | bytes 20 | tf_op jit(solution)/shard_map/ppermute | solution.py:26
  122.0 2.4 %collective-permute-start.1 = (f32[1,1]{1,0:T(1,128)}, f32[1,1]{1,0:T(1,128)}, u32[]{:S(2)}, u32[]{:S(2)}) collective-permute-start(f32[1,1]{1,0:T(1,128)} %get-tuple-element.22), channel_id=1, source_target_pairs={{0,16},{16,32},{32,48},{48,64},{64,80},{80,96},{96,112},{112,128},... | collective-permute-start | bytes 20 | tf_op jit(solution)/shard_map/ppermute | solution.py:24
  124.5 0.1 pad_add_fusion.3
  124.6 0.2 slice.450
  124.8 0.2 slice.459
  124.9 0.2 slice.454
  125.1 0.1 broadcast_in_dim.80
  125.2 0.1 slice.460
  125.4 0.1 slice.455
  126.2 0.2 slice.399
  126.4 0.2 slice.403
  126.6 0.1 slice.406
  126.7 0.1 slice.410
  126.8 0.1 slice.413
  127.0 0.1 slice.417
  127.1 0.1 slice.420
  127.2 0.1 slice.424
  127.3 0.1 slice.431
  127.4 0.1 slice.427
  127.5 0.1 slice.439
  127.6 0.1 slice.435
  127.7 0.6 slice.432
  128.3 0.1 slice.425
  128.4 0.1 slice.418
  128.5 0.1 slice.411
  128.6 0.1 slice.404
  128.8 0.2 slice.397
  128.9 0.1 broadcast_in_dim.78
  129.0 0.2 slice.451
  129.2 0.6 slice.440
  129.9 0.2 all-to-all-done.1
  130.0 0.1 slice.452
  130.1 0.1 slice.401
  130.2 0.1 slice.400
  130.4 0.1 slice.456
  130.5 0.1 slice.457
  131.2 0.2 slice.398
  131.4 0.1 maximum_select_fusion.5
  132.1 0.2 slice.453
  133.0 0.6 broadcast_select_fusion
  133.7 0.6 fusion.8
  135.0 0.1 maximum_select_fusion.4
  135.2 6.0 %collective-permute-start.3 = (f32[512,1]{0,1:T(1,128)S(1)}, f32[512,1]{0,1:T(1,128)S(1)}, u32[]{:S(2)}, u32[]{:S(2)}) collective-permute-start(f32[512,1]{0,1:T(1,128)S(1)} %slice_add_fusion), channel_id=1, source_target_pairs={{16,0},{32,16},{48,32},{64,48},{80,64},{96,80},{112,96},{128,112},... | collective-permute-start | bytes 6152 | tf_op jit(solution)/shard_map/ppermute | solution.py:26
  141.3 1.9 %collective-permute-start.2 = (f32[512,1]{0,1:T(1,128)S(1)}, f32[512,1]{0,1:T(1,128)S(1)}, u32[]{:S(2)}, u32[]{:S(2)}) collective-permute-start(f32[512,1]{0,1:T(1,128)S(1)} %slice_add_fusion.1), channel_id=1, source_target_pairs={{0,16},{16,32},{32,48},{48,64},{64,80},{80,96},{96,112},{112,128},... | collective-permute-start | bytes 6152 | tf_op jit(solution)/shard_map/ppermute | solution.py:24
  143.2 1.3 convert_compare_fusion.1
  144.5 0.1 rev.2
  144.7 4.5 %collective-permute-done.2 = f32[512,1]{0,1:T(1,128)S(1)} collective-permute-done((f32[512,1]{0,1:T(1,128)S(1)}, f32[512,1]{0,1:T(1,128)S(1)}, u32[]{:S(2)}, u32[]{:S(2)}) %collective-permute-start.2) | collective-permute-done | bytes 2080 | tf_op jit(solution)/shard_map/ppermute | solution.py:24
  149.2 0.1 maximum_select_fusion
  149.3 0.8 copy.34
  (171 shorter events, 3.4 us)
Async XLA Ops:
  6.5 54.4 %all-gather.5.cloned.1.call-start = ((), (), s32[]{:S(2)}) async-start(), calls=%async_computation.2 | async-start | bytes 1572864 | tf_op jit(solution)/shard_map/all_gather | solution.py:114
  6.5 29.1 %copy-start.5 = (bf16[512,128]{1,0:T(8,128)(2,1)S(1)}, bf16[512,128]{1,0:T(8,128)(2,1)}, u32[]{:S(2)}) copy-start(bf16[512,128]{1,0:T(8,128)(2,1)} %param.5) | copy-start | bytes 393220
  7.7 28.1 %copy-start = (s32[512,128]{1,0:T(8,128)S(1)}, s32[512,128]{1,0:T(8,128)}, u32[]{:S(2)}) copy-start(s32[512,128]{1,0:T(8,128)} %param.6) | copy-start | bytes 786436
  35.5 1.7 %copy-start.7 = (s32[128]{0:T(128)S(1)}, s32[128]{0:T(128)}, u32[]{:S(2)}) copy-start(s32[128]{0:T(128)} %param.7) | copy-start | bytes 1540
  35.6 70.1 %all-gather.7.cloned.1.call-start = ((), (), s32[]{:S(2)}) async-start(), calls=%async_computation.3 | async-start | bytes 1327104 | tf_op jit(solution)/shard_map/all_gather | solution.py:109
  115.5 14.5 %all-to-all-start.1 = ((f32[8,16,512]{2,1,0:T(8,128)}), f32[8,16,512]{2,1,0:T(8,128)S(1)}, u32[]{:S(2)}, u32[]{:S(2)}) async-start(f32[8,16,512]{2,1,0:T(8,128)} %shard_map.46), calls=%async_computation.1 | async-start | bytes 524288 | tf_op jit(solution)/shard_map/all_to_all | solution.py:118
  120.1 23.1 %collective-permute-start = (f32[1,1]{1,0:T(1,128)}, f32[1,1]{1,0:T(1,128)}, u32[]{:S(2)}, u32[]{:S(2)}) collective-permute-start(f32[1,1]{1,0:T(1,128)} %get-tuple-element.21), channel_id=1, source_target_pairs={{16,0},{32,16},{48,32},{64,48},{80,64},{96,80},{112,96},{128,112},... | collective-permute-start | bytes 20 | tf_op jit(solution)/shard_map/ppermute | solution.py:26
  122.0 21.2 %collective-permute-start.1 = (f32[1,1]{1,0:T(1,128)}, f32[1,1]{1,0:T(1,128)}, u32[]{:S(2)}, u32[]{:S(2)}) collective-permute-start(f32[1,1]{1,0:T(1,128)} %get-tuple-element.22), channel_id=1, source_target_pairs={{0,16},{16,32},{32,48},{48,64},{64,80},{80,96},{96,112},{112,128},... | collective-permute-start | bytes 20 | tf_op jit(solution)/shard_map/ppermute | solution.py:24
  130.6 1.0 copy-start.1
  131.4 1.2 copy-start.2
  131.6 1.1 copy-start.3
  131.7 1.0 slice-start
  131.8 0.9 copy-start.4
  131.9 0.9 copy-start.6
  132.8 1.9 %slice-start.3 = ((f32[512,16]{0,1:T(8,128)}), f32[512,1]{0,1:T(1,128)S(1)}, s32[]{:S(2)}) async-start(f32[512,16]{0,1:T(8,128)} %copy-done.4), calls=%async_computation.7 | async-start | bytes 4096 | tf_op jit(solution)/shard_map/slice | solution.py:77
  132.8 1.7 %slice-start.4 = ((f32[512,8]{0,1:T(8,128)}), f32[512,1]{0,1:T(1,128)S(1)}, s32[]{:S(2)}) async-start(f32[512,8]{0,1:T(8,128)} %copy-done.6), calls=%async_computation.8 | async-start | bytes 4096 | tf_op jit(solution)/shard_map/slice | solution.py:77
  132.8 2.0 %slice-start.2 = ((f32[512,32]{0,1:T(8,128)}), f32[512,1]{0,1:T(1,128)S(1)}, s32[]{:S(2)}) async-start(f32[512,32]{0,1:T(8,128)} %copy-done.3), calls=%async_computation.6 | async-start | bytes 4096 | tf_op jit(solution)/shard_map/slice | solution.py:77
  132.9 2.1 %slice-start.1 = ((f32[512,64]{0,1:T(8,128)}), f32[512,1]{0,1:T(1,128)S(1)}, s32[]{:S(2)}) async-start(f32[512,64]{0,1:T(8,128)} %copy-done.2), calls=%async_computation.5 | async-start | bytes 4096 | tf_op jit(solution)/shard_map/slice | solution.py:77
  135.2 9.5 %collective-permute-start.3 = (f32[512,1]{0,1:T(1,128)S(1)}, f32[512,1]{0,1:T(1,128)S(1)}, u32[]{:S(2)}, u32[]{:S(2)}) collective-permute-start(f32[512,1]{0,1:T(1,128)S(1)} %slice_add_fusion), channel_id=1, source_target_pairs={{16,0},{32,16},{48,32},{64,48},{80,64},{96,80},{112,96},{128,112},... | collective-permute-start | bytes 6152 | tf_op jit(solution)/shard_map/ppermute | solution.py:26
  141.3 7.9 %collective-permute-start.2 = (f32[512,1]{0,1:T(1,128)S(1)}, f32[512,1]{0,1:T(1,128)S(1)}, u32[]{:S(2)}, u32[]{:S(2)}) collective-permute-start(f32[512,1]{0,1:T(1,128)S(1)} %slice_add_fusion.1), channel_id=1, source_target_pairs={{0,16},{16,32},{32,48},{48,64},{64,80},{80,96},{96,112},{112,128},... | collective-permute-start | bytes 6152 | tf_op jit(solution)/shard_map/ppermute | solution.py:24
Sparse Core Ops, SparseCore 0:
  35.7 25.2 all-gather.4
  63.0 42.5 all-gather.6

commit v3 on v2

v3 whole, which is shorter than its diff:
```python
import jax
import jax.numpy as jnp
from jax import lax
from jax.experimental import pallas as pl
from jax.experimental.pallas import tpu as pltpu
from jax.sharding import Mesh
from jax.sharding import PartitionSpec as P

TSTEP = 64
COLS = ("cols_0", "cols_1")
SPLIT = "cols_0"
SHARE = "cols_1"
CODE = 32
MOST = 32


def wave_kernel(offset_ref, gt_ref, a_ref, o_ref):
    slots = a_ref.shape[0] - 16
    width = gt_ref.shape[1]
    lanes = a_ref.shape[1]
    code = a_ref[slots:slots + 16, :].astype(jnp.float32)
    start = (code[0:1] * CODE + code[1:2]).astype(jnp.int32)
    start = (start - offset_ref[0]) & (width - 1)
    dense = jnp.concatenate(
        [a_ref[0:slots, :].astype(jnp.float32), jnp.zeros((width - slots, lanes), jnp.float32)], axis=0
    )
    for bit in range(max(1, (width - 1).bit_length())):
        rolled = pltpu.roll(dense, 1 << bit, 0)
        dense = jnp.where(((start >> bit) & 1) == 1, rolled, dense)
    wave = jnp.dot(gt_ref[...], dense.astype(jnp.bfloat16), preferred_element_type=jnp.float32)
    rows = wave.shape[0]
    o_ref[...] = jnp.max(wave.reshape(rows // TSTEP, TSTEP, lanes), axis=1)


def wave_maxima(offset, panel_t, coded):
    parts, height, lanes = coded.shape
    rows, width = panel_t.shape
    assert width & (width - 1) == 0
    grid_spec = pltpu.PrefetchScalarGridSpec(
        num_scalar_prefetch=1,
        grid=(parts,),
        in_specs=[
            pl.BlockSpec((rows, width), lambda p, o: (0, 0)),
            pl.BlockSpec((None, height, lanes), lambda p, o: (p, 0, 0)),
        ],
        out_specs=pl.BlockSpec((None, rows // TSTEP, lanes), lambda p, o: (p, 0, 0)),
    )
    return pl.pallas_call(
        wave_kernel,
        grid_spec=grid_spec,
        out_shape=jax.ShapeDtypeStruct((parts, rows // TSTEP, lanes), jnp.float32),
    )(offset, panel_t, coded)


def shifted(values, step, fill):
    pad = jnp.full((abs(step),) + values.shape[1:], fill, values.dtype)
    if step > 0:
        return jnp.concatenate([pad, values[:-step]], axis=0)
    return jnp.concatenate([values[-step:], pad], axis=0)


def run_max(values, codes, reach, sign):
    step = 1
    while step < reach:
        other = shifted(values, sign * step, -jnp.inf)
        same = shifted(codes, sign * step, 0.0) == codes
        values = jnp.where(same, jnp.maximum(values, other), values)
        step *= 2
    return values


def point_peaks(window_max_t, win_point, reach):
    windows, scen = window_max_t.shape
    codes = (win_point + 1).astype(jnp.float32)[:, None]
    forward = run_max(window_max_t, codes, reach, 1)
    backward = run_max(window_max_t, codes, reach, -1)
    peak = jnp.maximum(forward, backward)
    count = lax.axis_size("rows")
    to_right = jnp.concatenate([forward[windows - 1:], jnp.broadcast_to(codes[windows - 1:], (1, scen))], axis=0)
    to_left = jnp.concatenate([backward[:1], jnp.broadcast_to(codes[:1], (1, scen))], axis=0)
    from_left = lax.ppermute(to_right, "rows", [(i, i + 1) for i in range(count - 1)])
    from_right = lax.ppermute(to_left, "rows", [(i + 1, i) for i in range(count - 1)])
    peak = jnp.where(codes == from_left[1:2], jnp.maximum(peak, from_left[0:1]), peak)
    peak = jnp.where(codes == from_right[1:2], jnp.maximum(peak, from_right[0:1]), peak)
    return peak.T


def local(greens, slip_values, rupture_ids, win_point):
    parts = lax.axis_size(SPLIT)
    shares = lax.axis_size(SHARE)
    own_sources, rows = greens.shape
    width = own_sources * parts * shares
    scen = slip_values.shape[0]
    block = rows // parts

    listed = rupture_ids >= 0
    values = jnp.where(listed, slip_values, jnp.zeros_like(slip_values))
    starts = jnp.maximum(rupture_ids[:, 0], 0)
    code = jnp.stack([starts // CODE, starts % CODE]).astype(jnp.bfloat16)
    coded = jnp.concatenate([values.T, code, jnp.zeros((14, scen), jnp.bfloat16)], axis=0)
    coded = lax.all_gather(coded, SPLIT, axis=0, tiled=False)

    count = parts * shares
    here = lax.axis_index(COLS)
    pieces = greens.reshape(own_sources, parts, block)
    received = []
    for distance in range(count):
        target = lax.rem(here + distance, count) // shares
        piece = lax.dynamic_index_in_dim(pieces, target, axis=1, keepdims=False)
        if distance > 0:
            piece = lax.ppermute(piece, COLS, [(i, (i + distance) % count) for i in range(count)])
        received.append(piece)
    ordered = [received[(count - u) % count] for u in range(count)]
    panel_t = jnp.stack(ordered).reshape(width, block).T
    offset = (here * own_sources).astype(jnp.int32).reshape(1)

    maxima = wave_maxima(offset, panel_t, coded)
    maxima = lax.all_to_all(maxima, SPLIT, 0, 0, tiled=True)
    return point_peaks(maxima.reshape(-1, scen), win_point, MOST)


def solution(mesh):
    split = Mesh(mesh.devices.reshape(mesh.shape["rows"], 8, 2), ("rows", "cols_0", "cols_1"))
    in_specs = (P(COLS, "rows"), P(COLS, None), P(COLS, None), P("rows"))
    out_specs = P(COLS, "rows")
    return jax.shard_map(local, mesh=split, in_specs=in_specs, out_specs=out_specs, check_vma=False)
```

time: 158 us -> 143 us (0.905)
  starting transfers between devices: 16.3 us -> 74.8 us
  waiting for transfers between devices: 68.6 us -> 29.6 us
  blocking collectives: 27.8 us -> 0 us
  local copies, waits for them, and re-layouts: 13.2 us -> 9.99 us
  other arithmetic: 5.63 us -> 3.85 us
    ppermute x4 -> x17, starting transfers between devices: 12.3 us -> 70.4 us  [the longest x15 65.5 us: local(): lax.ppermute(piece, COLS, [(i, (i + distance) % count) for i in range(cou...]
    all_gather x1, waiting for transfers between devices: 42 us -> 5.39 us  [local(): coded = lax.all_gather(coded, SPLIT, axis=0, tiled=False)]
    all_to_all x1 -> x0, blocking collectives: 27.8 us -> none  [local(): pieces = lax.all_to_all(pieces, SPLIT, 1, 0, tiled=True)]
    all_gather x1 -> x0, waiting for transfers between devices: 21.9 us -> none  [local(): pieces = lax.all_gather(pieces, SHARE, axis=0, tiled=False)]
    ppermute x4 -> x17, waiting for transfers between devices: 4.5 us -> 14.4 us  [the longest x1 7.99 us: point_peaks(): lax.ppermute(to_right, 'rows', [(i, i + 1) for i in range(count - 1)])]
    all_to_all x1, waiting for transfers between devices: 0.15 us -> 9.74 us  [local(): maxima = lax.all_to_all(maxima, SPLIT, 0, 0, tiled=True)]
    slice x90 -> x14, local copies, waits for them, and re-layouts: 7.41 us -> 2.3 us  [the longest x10 0.99 us: shifted(): return jnp.concatenate([values[-step:], pad], axis=0)]
    dynamic_slice x0 -> x1, local copies, waits for them, and re-layouts: none -> 3.03 us  [local(): piece = lax.dynamic_index_in_dim(pieces, target, axis=1, keepdims=False)]
  transfers between devices with their start and end apart: 7 -> 19, of which waited for: 4 -> 6; matrix products, arithmetic and copies ran while one was open for 11% -> 4% of each run, Pallas kernels for 0% -> 0%
where the time goes in v3:
time: 143 us; the launch traced here: 142 us
  starting transfers between devices  74.8 us (52%)
  waiting for transfers between devices  29.6 us (21%)
  between operations  14.2 us (10%)
  local copies, waits for them, and re-layouts  9.99 us (7%)
  Pallas kernels  9.87 us (7%)
  other arithmetic  3.85 us (3%)
    ppermute x15, starting transfers between devices, local(): lax.ppermute(piece, COLS, [(i, (i + distance) % count) for i in range(cou...  65.5 us
    pallas_call x1, Pallas kernels, wave_maxima(): pl.pallas_call(wave_kernel, grid_spec=grid_spec, out_shape=jax.ShapeDtype...  9.87 us
    all_to_all x1, waiting for transfers between devices, local(): maxima = lax.all_to_all(maxima, SPLIT, 0, 0, tiled=True)  9.74 us
    ppermute x1, waiting for transfers between devices, point_peaks(): lax.ppermute(to_right, 'rows', [(i, i + 1) for i in range(count - 1)])  7.99 us
    all_gather x1, waiting for transfers between devices, local(): coded = lax.all_gather(coded, SPLIT, axis=0, tiled=False)  5.39 us
    ppermute x15, waiting for transfers between devices, local(): lax.ppermute(piece, COLS, [(i, (i + distance) % count) for i in range(cou...  4.85 us
    all_to_all x1, starting transfers between devices, local(): maxima = lax.all_to_all(maxima, SPLIT, 0, 0, tiled=True)  4.37 us
    ppermute x1, starting transfers between devices, point_peaks(): lax.ppermute(to_left, 'rows', [(i + 1, i) for i in range(count - 1)])  3.05 us
  transfers between devices with their start and end apart: 19, of which 6 were waited for; matrix products, arithmetic and copies ran while one was open for 4% of the time, Pallas kernels for 0%

profile of v3, /device:TPU:6, one launch (start us, length us, event | category | flops | bytes accessed | tf_op | source)
XLA Modules:
  0.0 142.3 jit_solution(1502469455446402424)
XLA Ops:
  6.5 1.3 copy.86
  8.0 3.0 %constant_dynamic-slice_fusion = (bf16[32,1,1024]{2,1,0:T(2,128)(2,1)S(1)}, bf16[32,1,1024]{2,1,0:T(2,128)(2,1)S(1)}, bf16[32,1,1024]{2,1,0:T(2,128)(2,1)S(1)}, ...) fusion(bf16[32,8,1024]{2,1,0:T(8,128)(2,1)S(1)} %bitcast.137, ...), kind=kLoop, calls=%fused_computation.59 | loop fusion | bytes 2097216 | tf_op jit(solution)/shard_map/jit(dynamic_index_in_dim)/dynamic_slice | solution.py:109
  11.0 0.0 copy-start
  11.0 0.0 copy-start.1
  11.1 12.1 %collective-permute-start = (bf16[32,1024]{1,0:T(8,128)(2,1)S(1)}, bf16[32,1024]{1,0:T(8,128)(2,1)S(1)}, u32[]{:S(2)}, u32[]{:S(2)}) collective-permute-start(bf16[32,1024]{1,0:T(8,128)(2,1)S(1)} %bitcast.157), channel_id=1, source_target_pairs={{0,15},{1,0},{2,1},{3,2},{4,3},{5,4},{6,5},{7,6},{8,7},{9,8},{10,9... | collective-permute-start | bytes 196616 | tf_op jit(solution)/shard_map/ppermute | solution.py:111
  23.2 2.5 %collective-permute-start.1 = (bf16[32,1024]{1,0:T(8,128)(2,1)S(1)}, bf16[32,1024]{1,0:T(8,128)(2,1)S(1)}, u32[]{:S(2)}, u32[]{:S(2)}) collective-permute-start(bf16[32,1024]{1,0:T(8,128)(2,1)S(1)} %bitcast.156), channel_id=1, source_target_pairs={{0,14},{1,15},{2,0},{3,1},{4,2},{5,3},{6,4},{7,5},{8,6},{9,7},{10,... | collective-permute-start | bytes 196616 | tf_op jit(solution)/shard_map/ppermute | solution.py:111
  25.7 2.3 %collective-permute-start.2 = (bf16[32,1024]{1,0:T(8,128)(2,1)S(1)}, bf16[32,1024]{1,0:T(8,128)(2,1)S(1)}, u32[]{:S(2)}, u32[]{:S(2)}) collective-permute-start(bf16[32,1024]{1,0:T(8,128)(2,1)S(1)} %bitcast.154), channel_id=1, source_target_pairs={{0,13},{1,14},{2,15},{3,0},{4,1},{5,2},{6,3},{7,4},{8,5},{9,6},{10... | collective-permute-start | bytes 196616 | tf_op jit(solution)/shard_map/ppermute | solution.py:111
  28.1 2.0 %collective-permute-start.3 = (bf16[32,1024]{1,0:T(8,128)(2,1)S(1)}, bf16[32,1024]{1,0:T(8,128)(2,1)S(1)}, u32[]{:S(2)}, u32[]{:S(2)}) collective-permute-start(bf16[32,1024]{1,0:T(8,128)(2,1)S(1)} %bitcast.153), channel_id=1, source_target_pairs={{0,12},{1,13},{2,14},{3,15},{4,0},{5,1},{6,2},{7,3},{8,4},{9,5},{1... | collective-permute-start | bytes 196616 | tf_op jit(solution)/shard_map/ppermute | solution.py:111
  30.2 1.9 %collective-permute-start.4 = (bf16[32,1024]{1,0:T(8,128)(2,1)S(1)}, bf16[32,1024]{1,0:T(8,128)(2,1)S(1)}, u32[]{:S(2)}, u32[]{:S(2)}) collective-permute-start(bf16[32,1024]{1,0:T(8,128)(2,1)S(1)} %bitcast.151), channel_id=1, source_target_pairs={{0,11},{1,12},{2,13},{3,14},{4,15},{5,0},{6,1},{7,2},{8,3},{9,4},{... | collective-permute-start | bytes 196616 | tf_op jit(solution)/shard_map/ppermute | solution.py:111
  32.1 0.2 shift-right-logical_reduce_fusion
  32.3 0.2 fusion.1
  32.5 0.1 copy.62
  32.6 0.1 copy.63
  32.8 0.1 pad.25.clone
  32.9 0.8 maximum_maximum_fusion
  33.6 0.0 all-gather.3.cloned.1.call-update
  33.7 0.1 fusion.7
  33.8 0.1 slice_bitcast_fusion.7
  33.8 0.1 slice_bitcast_fusion.6
  33.9 0.1 slice_bitcast_fusion.5
  34.0 0.1 slice_bitcast_fusion.4
  34.4 9.3 %collective-permute-start.5 = (bf16[32,1024]{1,0:T(8,128)(2,1)S(1)}, bf16[32,1024]{1,0:T(8,128)(2,1)S(1)}, u32[]{:S(2)}, u32[]{:S(2)}) collective-permute-start(bf16[32,1024]{1,0:T(8,128)(2,1)S(1)} %bitcast.161), channel_id=1, source_target_pairs={{0,10},{1,11},{2,12},{3,13},{4,14},{5,15},{6,0},{7,1},{8,2},{9,3},... | collective-permute-start | bytes 196616 | tf_op jit(solution)/shard_map/ppermute | solution.py:111
  43.7 1.9 %collective-permute-start.6 = (bf16[32,1024]{1,0:T(8,128)(2,1)S(1)}, bf16[32,1024]{1,0:T(8,128)(2,1)S(1)}, u32[]{:S(2)}, u32[]{:S(2)}) collective-permute-start(bf16[32,1024]{1,0:T(8,128)(2,1)S(1)} %bitcast.160), channel_id=1, source_target_pairs={{0,9},{1,10},{2,11},{3,12},{4,13},{5,14},{6,15},{7,0},{8,1},{9,2},... | collective-permute-start | bytes 196616 | tf_op jit(solution)/shard_map/ppermute | solution.py:111
  45.7 7.7 %collective-permute-start.7 = (bf16[32,1024]{1,0:T(8,128)(2,1)S(1)}, bf16[32,1024]{1,0:T(8,128)(2,1)S(1)}, u32[]{:S(2)}, u32[]{:S(2)}) collective-permute-start(bf16[32,1024]{1,0:T(8,128)(2,1)S(1)} %bitcast.159), channel_id=1, source_target_pairs={{0,8},{1,9},{2,10},{3,11},{4,12},{5,13},{6,14},{7,15},{8,0},{9,1},... | collective-permute-start | bytes 196616 | tf_op jit(solution)/shard_map/ppermute | solution.py:111
  53.5 1.9 %collective-permute-start.8 = (bf16[32,1024]{1,0:T(8,128)(2,1)S(1)}, bf16[32,1024]{1,0:T(8,128)(2,1)S(1)}, u32[]{:S(2)}, u32[]{:S(2)}) collective-permute-start(bf16[32,1024]{1,0:T(8,128)(2,1)S(1)} %bitcast.158), channel_id=1, source_target_pairs={{0,7},{1,8},{2,9},{3,10},{4,11},{5,12},{6,13},{7,14},{8,15},{9,0},... | collective-permute-start | bytes 196616 | tf_op jit(solution)/shard_map/ppermute | solution.py:111
  55.4 5.8 %collective-permute-start.9 = (bf16[32,1024]{1,0:T(8,128)(2,1)S(1)}, bf16[32,1024]{1,0:T(8,128)(2,1)S(1)}, u32[]{:S(2)}, u32[]{:S(2)}) collective-permute-start(bf16[32,1024]{1,0:T(8,128)(2,1)S(1)} %bitcast.155), channel_id=1, source_target_pairs={{0,6},{1,7},{2,8},{3,9},{4,10},{5,11},{6,12},{7,13},{8,14},{9,15},... | collective-permute-start | bytes 196616 | tf_op jit(solution)/shard_map/ppermute | solution.py:111
  61.2 6.3 %collective-permute-start.10 = (bf16[32,1024]{1,0:T(8,128)(2,1)S(1)}, bf16[32,1024]{1,0:T(8,128)(2,1)S(1)}, u32[]{:S(2)}, u32[]{:S(2)}) collective-permute-start(bf16[32,1024]{1,0:T(8,128)(2,1)S(1)} %bitcast.152), channel_id=1, source_target_pairs={{0,5},{1,6},{2,7},{3,8},{4,9},{5,10},{6,11},{7,12},{8,13},{9,14},{... | collective-permute-start | bytes 196616 | tf_op jit(solution)/shard_map/ppermute | solution.py:111
  67.6 1.9 %collective-permute-start.11 = (bf16[32,1024]{1,0:T(8,128)(2,1)S(1)}, bf16[32,1024]{1,0:T(8,128)(2,1)S(1)}, u32[]{:S(2)}, u32[]{:S(2)}) collective-permute-start(bf16[32,1024]{1,0:T(8,128)(2,1)S(1)} %bitcast.150), channel_id=1, source_target_pairs={{0,4},{1,5},{2,6},{3,7},{4,8},{5,9},{6,10},{7,11},{8,12},{9,13},{1... | collective-permute-start | bytes 196616 | tf_op jit(solution)/shard_map/ppermute | solution.py:111
  69.5 3.5 %collective-permute-start.12 = (bf16[32,1024]{1,0:T(8,128)(2,1)S(1)}, bf16[32,1024]{1,0:T(8,128)(2,1)S(1)}, u32[]{:S(2)}, u32[]{:S(2)}) collective-permute-start(bf16[32,1024]{1,0:T(8,128)(2,1)S(1)} %bitcast.149), channel_id=1, source_target_pairs={{0,3},{1,4},{2,5},{3,6},{4,7},{5,8},{6,9},{7,10},{8,11},{9,12},{10... | collective-permute-start | bytes 196616 | tf_op jit(solution)/shard_map/ppermute | solution.py:111
  73.1 2.5 %collective-permute-start.13 = (bf16[32,1024]{1,0:T(8,128)(2,1)S(1)}, bf16[32,1024]{1,0:T(8,128)(2,1)S(1)}, u32[]{:S(2)}, u32[]{:S(2)}) collective-permute-start(bf16[32,1024]{1,0:T(8,128)(2,1)S(1)} %bitcast.148), channel_id=1, source_target_pairs={{0,2},{1,3},{2,4},{3,5},{4,6},{5,7},{6,8},{7,9},{8,10},{9,11},{10,... | collective-permute-start | bytes 196616 | tf_op jit(solution)/shard_map/ppermute | solution.py:111
  75.6 3.8 %collective-permute-start.14 = (bf16[32,1024]{1,0:T(8,128)(2,1)S(1)}, bf16[32,1024]{1,0:T(8,128)(2,1)S(1)}, u32[]{:S(2)}, u32[]{:S(2)}) collective-permute-start(bf16[32,1024]{1,0:T(8,128)(2,1)S(1)} %bitcast.147), channel_id=1, source_target_pairs={{0,1},{1,2},{2,3},{3,4},{4,5},{5,6},{6,7},{7,8},{8,9},{9,10},{10,1... | collective-permute-start | bytes 196616 | tf_op jit(solution)/shard_map/ppermute | solution.py:111
  79.4 1.9 %collective-permute-done.11 = bf16[32,1024]{1,0:T(8,128)(2,1)S(1)} collective-permute-done((bf16[32,1024]{1,0:T(8,128)(2,1)S(1)}, bf16[32,1024]{1,0:T(8,128)(2,1)S(1)}, u32[]{:S(2)}, u32[]{:S(2)}) %collective-permute-start.11) | collective-permute-done | bytes 65568 | tf_op jit(solution)/shard_map/ppermute | solution.py:111
  81.3 2.9 %collective-permute-done.13 = bf16[32,1024]{1,0:T(8,128)(2,1)S(1)} collective-permute-done((bf16[32,1024]{1,0:T(8,128)(2,1)S(1)}, bf16[32,1024]{1,0:T(8,128)(2,1)S(1)}, u32[]{:S(2)}, u32[]{:S(2)}) %collective-permute-start.13) | collective-permute-done | bytes 65568 | tf_op jit(solution)/shard_map/ppermute | solution.py:111
  84.3 1.3 copy.61
  85.6 5.4 %all-gather.3.cloned.1.call-done = bf16[1152,512]{1,0:T(8,128)(2,1)} async-done(((bf16[144,512]{1,0:T(8,128)(2,1)}), bf16[1152,512]{1,0:T(8,128)(2,1)}) %all-gather.3.cloned.1.call-update) | async-done | bytes 1179664 | tf_op jit(solution)/shard_map/all_gather | solution.py:101
  91.0 9.9 %shard_map.46 = f32[8,16,512]{2,1,0:T(8,128)} custom-call(s32[1]{0:T(128)} %bitcast.9.offset_ref, bf16[1024,512]{1,0:T(8,128)(2,1)} %bitcast.138, bf16[8,144,512]{2,1,0:T(8,128)(2,1)} %bitcast.144), custom_call_target="tpu_custom_call" | custom-call | tf_op jit(solution)/shard_map/pallas_call | solution.py:48
  100.8 4.4 %all-to-all-start = ((f32[8,16,512]{2,1,0:T(8,128)}), f32[8,16,512]{2,1,0:T(8,128)S(1)}, u32[]{:S(2)}, u32[]{:S(2)}) async-start(f32[8,16,512]{2,1,0:T(8,128)} %shard_map.46), calls=%async_computation | async-start | bytes 524288 | tf_op jit(solution)/shard_map/all_to_all | solution.py:118
  105.2 0.6 fusion.6
  105.8 0.1 maximum_compare_fusion
  105.9 0.1 compare_bitcast_fusion.7
  105.9 9.7 %all-to-all-done = f32[8,16,512]{2,1,0:T(8,128)S(1)} async-done(((f32[8,16,512]{2,1,0:T(8,128)}), f32[8,16,512]{2,1,0:T(8,128)S(1)}, u32[]{:S(2)}, u32[]{:S(2)}) %all-to-all-start) | async-done | bytes 262176 | tf_op jit(solution)/shard_map/all_to_all | solution.py:118
  115.7 0.1 copy.65
  115.8 0.1 fusion.5
  115.9 0.1 maximum_select_fusion.11
  116.1 0.1 slice.154
  116.3 0.1 slice.155
  116.4 0.1 slice.156
  116.6 0.0 copy-start.3
  116.6 0.1 slice.157
  116.8 0.4 copy-done.3
  117.2 0.6 slice_select_fusion
  117.9 3.1 %collective-permute-start.15 = (f32[2,512]{0,1:T(8,128)S(1)}, f32[2,512]{0,1:T(8,128)S(1)}, u32[]{:S(2)}, u32[]{:S(2)}) collective-permute-start(f32[2,512]{0,1:T(8,128)S(1)} %slice_select_fusion), channel_id=1, source_target_pairs={{16,0},{32,16},{48,32},{64,48},{80,64},{96,80},{112,96},{128,112},... | collective-permute-start | bytes 12296 | tf_op jit(solution)/shard_map/ppermute | solution.py:82
  120.9 0.1 maximum_select_fusion.5
  121.1 0.1 maximum_select_fusion.4
  121.2 0.1 maximum_select_fusion.3
  121.4 0.1 maximum_select_fusion.2
  121.5 0.1 slice.165
  121.6 0.6 concatenate.94
  122.2 1.9 %collective-permute-start.16 = (f32[2,512]{0,1:T(8,128)S(1)}, f32[2,512]{0,1:T(8,128)S(1)}, u32[]{:S(2)}, u32[]{:S(2)}) collective-permute-start(f32[2,512]{0,1:T(8,128)S(1)} %concatenate.94), channel_id=1, source_target_pairs={{0,16},{16,32},{32,48},{48,64},{64,80},{80,96},{96,112},{112,128},... | collective-permute-start | bytes 12296 | tf_op jit(solution)/shard_map/ppermute | solution.py:81
  124.2 1.6 %collective-permute-done.15 = f32[2,512]{0,1:T(8,128)S(1)} collective-permute-done((f32[2,512]{0,1:T(8,128)S(1)}, f32[2,512]{0,1:T(8,128)S(1)}, u32[]{:S(2)}, u32[]{:S(2)}) %collective-permute-start.15) | collective-permute-done | bytes 4128 | tf_op jit(solution)/shard_map/ppermute | solution.py:82
  125.8 0.3 slice_reduce_fusion.3
  126.1 8.0 %collective-permute-done.16 = f32[2,512]{0,1:T(8,128)S(1)} collective-permute-done((f32[2,512]{0,1:T(8,128)S(1)}, f32[2,512]{0,1:T(8,128)S(1)}, u32[]{:S(2)}, u32[]{:S(2)}) %collective-permute-start.16) | collective-permute-done | bytes 4128 | tf_op jit(solution)/shard_map/ppermute | solution.py:81
  134.1 0.3 slice_reduce_fusion.2
  134.4 1.0 fusion
  (57 shorter events, 0.8 us)
Async XLA Ops:
  6.5 84.4 %all-gather.3.cloned.1.call-start = ((), (), s32[]{:S(2)}) async-start(), calls=%async_computation.1 | async-start | bytes 1327104 | tf_op jit(solution)/shard_map/all_gather | solution.py:101
  11.0 21.1 %copy-start = (s32[512,128]{1,0:T(8,128)S(1)}, s32[512,128]{1,0:T(8,128)}, u32[]{:S(2)}) copy-start(s32[512,128]{1,0:T(8,128)} %param.6) | copy-start | bytes 786436
  11.0 21.6 %copy-start.1 = (bf16[512,128]{1,0:T(8,128)(2,1)S(1)}, bf16[512,128]{1,0:T(8,128)(2,1)}, u32[]{:S(2)}) copy-start(bf16[512,128]{1,0:T(8,128)(2,1)} %param.5) | copy-start | bytes 393220
  11.1 23.4 %collective-permute-start = (bf16[32,1024]{1,0:T(8,128)(2,1)S(1)}, bf16[32,1024]{1,0:T(8,128)(2,1)S(1)}, u32[]{:S(2)}, u32[]{:S(2)}) collective-permute-start(bf16[32,1024]{1,0:T(8,128)(2,1)S(1)} %bitcast.157), channel_id=1, source_target_pairs={{0,15},{1,0},{2,1},{3,2},{4,3},{5,4},{6,5},{7,6},{8,7},{9,8},{10,9... | collective-permute-start | bytes 196616 | tf_op jit(solution)/shard_map/ppermute | solution.py:111
  23.2 20.5 %collective-permute-start.1 = (bf16[32,1024]{1,0:T(8,128)(2,1)S(1)}, bf16[32,1024]{1,0:T(8,128)(2,1)S(1)}, u32[]{:S(2)}, u32[]{:S(2)}) collective-permute-start(bf16[32,1024]{1,0:T(8,128)(2,1)S(1)} %bitcast.156), channel_id=1, source_target_pairs={{0,14},{1,15},{2,0},{3,1},{4,2},{5,3},{6,4},{7,5},{8,6},{9,7},{10,... | collective-permute-start | bytes 196616 | tf_op jit(solution)/shard_map/ppermute | solution.py:111
  25.7 20.0 %collective-permute-start.2 = (bf16[32,1024]{1,0:T(8,128)(2,1)S(1)}, bf16[32,1024]{1,0:T(8,128)(2,1)S(1)}, u32[]{:S(2)}, u32[]{:S(2)}) collective-permute-start(bf16[32,1024]{1,0:T(8,128)(2,1)S(1)} %bitcast.154), channel_id=1, source_target_pairs={{0,13},{1,14},{2,15},{3,0},{4,1},{5,2},{6,3},{7,4},{8,5},{9,6},{10... | collective-permute-start | bytes 196616 | tf_op jit(solution)/shard_map/ppermute | solution.py:111
  28.1 25.4 %collective-permute-start.3 = (bf16[32,1024]{1,0:T(8,128)(2,1)S(1)}, bf16[32,1024]{1,0:T(8,128)(2,1)S(1)}, u32[]{:S(2)}, u32[]{:S(2)}) collective-permute-start(bf16[32,1024]{1,0:T(8,128)(2,1)S(1)} %bitcast.153), channel_id=1, source_target_pairs={{0,12},{1,13},{2,14},{3,15},{4,0},{5,1},{6,2},{7,3},{8,4},{9,5},{1... | collective-permute-start | bytes 196616 | tf_op jit(solution)/shard_map/ppermute | solution.py:111
  30.1 3.5 %copy-start.2 = (s32[128]{0:T(128)S(1)}, s32[128]{0:T(128)}, u32[]{:S(2)}) copy-start(s32[128]{0:T(128)} %param.7) | copy-start | bytes 1540
  30.2 25.2 %collective-permute-start.4 = (bf16[32,1024]{1,0:T(8,128)(2,1)S(1)}, bf16[32,1024]{1,0:T(8,128)(2,1)S(1)}, u32[]{:S(2)}, u32[]{:S(2)}) collective-permute-start(bf16[32,1024]{1,0:T(8,128)(2,1)S(1)} %bitcast.151), channel_id=1, source_target_pairs={{0,11},{1,12},{2,13},{3,14},{4,15},{5,0},{6,1},{7,2},{8,3},{9,4},{... | collective-permute-start | bytes 196616 | tf_op jit(solution)/shard_map/ppermute | solution.py:111
  34.4 26.8 %collective-permute-start.5 = (bf16[32,1024]{1,0:T(8,128)(2,1)S(1)}, bf16[32,1024]{1,0:T(8,128)(2,1)S(1)}, u32[]{:S(2)}, u32[]{:S(2)}) collective-permute-start(bf16[32,1024]{1,0:T(8,128)(2,1)S(1)} %bitcast.161), channel_id=1, source_target_pairs={{0,10},{1,11},{2,12},{3,13},{4,14},{5,15},{6,0},{7,1},{8,2},{9,3},... | collective-permute-start | bytes 196616 | tf_op jit(solution)/shard_map/ppermute | solution.py:111
  43.7 23.8 %collective-permute-start.6 = (bf16[32,1024]{1,0:T(8,128)(2,1)S(1)}, bf16[32,1024]{1,0:T(8,128)(2,1)S(1)}, u32[]{:S(2)}, u32[]{:S(2)}) collective-permute-start(bf16[32,1024]{1,0:T(8,128)(2,1)S(1)} %bitcast.160), channel_id=1, source_target_pairs={{0,9},{1,10},{2,11},{3,12},{4,13},{5,14},{6,15},{7,0},{8,1},{9,2},... | collective-permute-start | bytes 196616 | tf_op jit(solution)/shard_map/ppermute | solution.py:111
  45.7 23.8 %collective-permute-start.7 = (bf16[32,1024]{1,0:T(8,128)(2,1)S(1)}, bf16[32,1024]{1,0:T(8,128)(2,1)S(1)}, u32[]{:S(2)}, u32[]{:S(2)}) collective-permute-start(bf16[32,1024]{1,0:T(8,128)(2,1)S(1)} %bitcast.159), channel_id=1, source_target_pairs={{0,8},{1,9},{2,10},{3,11},{4,12},{5,13},{6,14},{7,15},{8,0},{9,1},... | collective-permute-start | bytes 196616 | tf_op jit(solution)/shard_map/ppermute | solution.py:111
  53.5 19.6 %collective-permute-start.8 = (bf16[32,1024]{1,0:T(8,128)(2,1)S(1)}, bf16[32,1024]{1,0:T(8,128)(2,1)S(1)}, u32[]{:S(2)}, u32[]{:S(2)}) collective-permute-start(bf16[32,1024]{1,0:T(8,128)(2,1)S(1)} %bitcast.158), channel_id=1, source_target_pairs={{0,7},{1,8},{2,9},{3,10},{4,11},{5,12},{6,13},{7,14},{8,15},{9,0},... | collective-permute-start | bytes 196616 | tf_op jit(solution)/shard_map/ppermute | solution.py:111
  55.4 20.1 %collective-permute-start.9 = (bf16[32,1024]{1,0:T(8,128)(2,1)S(1)}, bf16[32,1024]{1,0:T(8,128)(2,1)S(1)}, u32[]{:S(2)}, u32[]{:S(2)}) collective-permute-start(bf16[32,1024]{1,0:T(8,128)(2,1)S(1)} %bitcast.155), channel_id=1, source_target_pairs={{0,6},{1,7},{2,8},{3,9},{4,10},{5,11},{6,12},{7,13},{8,14},{9,15},... | collective-permute-start | bytes 196616 | tf_op jit(solution)/shard_map/ppermute | solution.py:111
  61.2 18.1 %collective-permute-start.10 = (bf16[32,1024]{1,0:T(8,128)(2,1)S(1)}, bf16[32,1024]{1,0:T(8,128)(2,1)S(1)}, u32[]{:S(2)}, u32[]{:S(2)}) collective-permute-start(bf16[32,1024]{1,0:T(8,128)(2,1)S(1)} %bitcast.152), channel_id=1, source_target_pairs={{0,5},{1,6},{2,7},{3,8},{4,9},{5,10},{6,11},{7,12},{8,13},{9,14},{... | collective-permute-start | bytes 196616 | tf_op jit(solution)/shard_map/ppermute | solution.py:111
  67.6 13.7 %collective-permute-start.11 = (bf16[32,1024]{1,0:T(8,128)(2,1)S(1)}, bf16[32,1024]{1,0:T(8,128)(2,1)S(1)}, u32[]{:S(2)}, u32[]{:S(2)}) collective-permute-start(bf16[32,1024]{1,0:T(8,128)(2,1)S(1)} %bitcast.150), channel_id=1, source_target_pairs={{0,4},{1,5},{2,6},{3,7},{4,8},{5,9},{6,10},{7,11},{8,12},{9,13},{1... | collective-permute-start | bytes 196616 | tf_op jit(solution)/shard_map/ppermute | solution.py:111
  69.5 11.8 %collective-permute-start.12 = (bf16[32,1024]{1,0:T(8,128)(2,1)S(1)}, bf16[32,1024]{1,0:T(8,128)(2,1)S(1)}, u32[]{:S(2)}, u32[]{:S(2)}) collective-permute-start(bf16[32,1024]{1,0:T(8,128)(2,1)S(1)} %bitcast.149), channel_id=1, source_target_pairs={{0,3},{1,4},{2,5},{3,6},{4,7},{5,8},{6,9},{7,10},{8,11},{9,12},{10... | collective-permute-start | bytes 196616 | tf_op jit(solution)/shard_map/ppermute | solution.py:111
  73.1 11.2 %collective-permute-start.13 = (bf16[32,1024]{1,0:T(8,128)(2,1)S(1)}, bf16[32,1024]{1,0:T(8,128)(2,1)S(1)}, u32[]{:S(2)}, u32[]{:S(2)}) collective-permute-start(bf16[32,1024]{1,0:T(8,128)(2,1)S(1)} %bitcast.148), channel_id=1, source_target_pairs={{0,2},{1,3},{2,4},{3,5},{4,6},{5,7},{6,8},{7,9},{8,10},{9,11},{10,... | collective-permute-start | bytes 196616 | tf_op jit(solution)/shard_map/ppermute | solution.py:111
  75.6 8.7 %collective-permute-start.14 = (bf16[32,1024]{1,0:T(8,128)(2,1)S(1)}, bf16[32,1024]{1,0:T(8,128)(2,1)S(1)}, u32[]{:S(2)}, u32[]{:S(2)}) collective-permute-start(bf16[32,1024]{1,0:T(8,128)(2,1)S(1)} %bitcast.147), channel_id=1, source_target_pairs={{0,1},{1,2},{2,3},{3,4},{4,5},{5,6},{6,7},{7,8},{8,9},{9,10},{10,1... | collective-permute-start | bytes 196616 | tf_op jit(solution)/shard_map/ppermute | solution.py:111
  100.8 14.9 %all-to-all-start = ((f32[8,16,512]{2,1,0:T(8,128)}), f32[8,16,512]{2,1,0:T(8,128)S(1)}, u32[]{:S(2)}, u32[]{:S(2)}) async-start(f32[8,16,512]{2,1,0:T(8,128)} %shard_map.46), calls=%async_computation | async-start | bytes 524288 | tf_op jit(solution)/shard_map/all_to_all | solution.py:118
  116.6 0.7 copy-start.3
  117.9 7.9 %collective-permute-start.15 = (f32[2,512]{0,1:T(8,128)S(1)}, f32[2,512]{0,1:T(8,128)S(1)}, u32[]{:S(2)}, u32[]{:S(2)}) collective-permute-start(f32[2,512]{0,1:T(8,128)S(1)} %slice_select_fusion), channel_id=1, source_target_pairs={{16,0},{32,16},{48,32},{64,48},{80,64},{96,80},{112,96},{128,112},... | collective-permute-start | bytes 12296 | tf_op jit(solution)/shard_map/ppermute | solution.py:82
  122.2 11.8 %collective-permute-start.16 = (f32[2,512]{0,1:T(8,128)S(1)}, f32[2,512]{0,1:T(8,128)S(1)}, u32[]{:S(2)}, u32[]{:S(2)}) collective-permute-start(f32[2,512]{0,1:T(8,128)S(1)} %concatenate.94), channel_id=1, source_target_pairs={{0,16},{16,32},{32,48},{48,64},{64,80},{80,96},{96,112},{112,128},... | collective-permute-start | bytes 12296 | tf_op jit(solution)/shard_map/ppermute | solution.py:81
Sparse Core Ops, SparseCore 0:
  33.8 57.1 all-gather.2

commit v4 on v3

--- a/solution.py
+++ b/solution.py
@@ -98,21 +98,19 @@
     starts = jnp.maximum(rupture_ids[:, 0], 0)
     code = jnp.stack([starts // CODE, starts % CODE]).astype(jnp.bfloat16)
     coded = jnp.concatenate([values.T, code, jnp.zeros((14, scen), jnp.bfloat16)], axis=0)
-    coded = lax.all_gather(coded, SPLIT, axis=0, tiled=False)
+    core = lax.rem(lax.axis_index("rows"), 2)
+    half = scen // 2
+    mine = lax.dynamic_slice_in_dim(coded, core * half, half, axis=1)
+    mine = lax.all_gather(mine, SPLIT, axis=0, tiled=False)
+    count_rows = lax.axis_size("rows")
+    theirs = lax.ppermute(mine, "rows", [(i, i ^ 1) for i in range(count_rows)])
+    coded = jnp.where(core == 0, jnp.concatenate([mine, theirs], axis=2), jnp.concatenate([theirs, mine], axis=2))
 
-    count = parts * shares
-    here = lax.axis_index(COLS)
-    pieces = greens.reshape(own_sources, parts, block)
-    received = []
-    for distance in range(count):
-        target = lax.rem(here + distance, count) // shares
-        piece = lax.dynamic_index_in_dim(pieces, target, axis=1, keepdims=False)
-        if distance > 0:
-            piece = lax.ppermute(piece, COLS, [(i, (i + distance) % count) for i in range(count)])
-        received.append(piece)
-    ordered = [received[(count - u) % count] for u in range(count)]
-    panel_t = jnp.stack(ordered).reshape(width, block).T
-    offset = (here * own_sources).astype(jnp.int32).reshape(1)
+    pieces = greens.reshape(own_sources, parts, 1, block)
+    pieces = jnp.broadcast_to(pieces, (own_sources, parts, shares, block)).reshape(own_sources, parts * shares, block)
+    pieces = lax.all_to_all(pieces, COLS, 1, 0, tiled=True)
+    panel_t = pieces.reshape(width, block).T
+    offset = jnp.zeros((1,), jnp.int32)
 
     maxima = wave_maxima(offset, panel_t, coded)
     maxima = lax.all_to_all(maxima, SPLIT, 0, 0, tiled=True)

time: 143 us -> 116 us (0.81)
  starting transfers between devices: 74.8 us -> 24.1 us
  blocking collectives: 0 us -> 45.4 us
  between operations: 14.2 us -> 0.3 us
  waiting for transfers between devices: 29.6 us -> 24.3 us
  local copies, waits for them, and re-layouts: 9.99 us -> 7.39 us
    ppermute x15 -> x1, starting transfers between devices: 65.5 us -> 1.91 us  [local(): theirs = lax.ppermute(mine, 'rows', [(i, i ^ 1) for i in range(count_rows)])]
    all_gather x0 -> x1, blocking collectives: none -> 45.4 us  [local(): mine = lax.all_gather(mine, SPLIT, axis=0, tiled=False)]
    all_to_all x0 -> x1, starting transfers between devices: none -> 11.6 us  [local(): pieces = lax.all_to_all(pieces, COLS, 1, 0, tiled=True)]
    all_gather x1 -> x0, waiting for transfers between devices: 5.39 us -> none  [local(): coded = lax.all_gather(coded, SPLIT, axis=0, tiled=False)]
    ppermute x15 -> x1, waiting for transfers between devices: 4.85 us -> 1.58 us  [local(): theirs = lax.ppermute(mine, 'rows', [(i, i ^ 1) for i in range(count_rows)])]
    dynamic_slice x1 -> x0, local copies, waits for them, and re-layouts: 3.03 us -> none  [local(): piece = lax.dynamic_index_in_dim(pieces, target, axis=1, keepdims=False)]
    broadcast_in_dim x0 -> x2, local copies, waits for them, and re-layouts: none -> 2.22 us  [local(): jnp.broadcast_to(pieces, (own_sources, parts, shares, block))]
    unnamed x41 -> x10, local copies, waits for them, and re-layouts: 2.55 us -> 0.7 us
  transfers between devices with their start and end apart: 19 -> 5, of which waited for: 6 -> 4; matrix products, arithmetic and copies ran while one was open for 4% -> 4% of each run, Pallas kernels for 0% -> 0%
where the time goes in v4:
time: 116 us
  blocking collectives  45.4 us (39%)
  waiting for transfers between devices  24.3 us (21%)
  starting transfers between devices  24.1 us (21%)
  Pallas kernels  9.86 us (8%)
  local copies, waits for them, and re-layouts  7.39 us (6%)
  other arithmetic  4.41 us (4%)
    all_gather x1, blocking collectives, local(): mine = lax.all_gather(mine, SPLIT, axis=0, tiled=False)  45.4 us
    all_to_all x1, starting transfers between devices, local(): pieces = lax.all_to_all(pieces, COLS, 1, 0, tiled=True)  11.6 us
    all_to_all x1, waiting for transfers between devices, local(): maxima = lax.all_to_all(maxima, SPLIT, 0, 0, tiled=True)  11.4 us
    pallas_call x1, Pallas kernels, wave_maxima(): pl.pallas_call(wave_kernel, grid_spec=grid_spec, out_shape=jax.ShapeDtype...  9.86 us
    ppermute x1, waiting for transfers between devices, point_peaks(): lax.ppermute(to_right, 'rows', [(i, i + 1) for i in range(count - 1)])  9.09 us
    all_to_all x1, starting transfers between devices, local(): maxima = lax.all_to_all(maxima, SPLIT, 0, 0, tiled=True)  4.75 us
    ppermute x1, starting transfers between devices, point_peaks(): lax.ppermute(to_left, 'rows', [(i + 1, i) for i in range(count - 1)])  3.91 us
  transfers between devices with their start and end apart: 5, of which 4 were waited for; matrix products, arithmetic and copies ran while one was open for 4% of the time, Pallas kernels for 0%

profile of v4, /device:TPU:6, one launch (start us, length us, event | category | flops | bytes accessed | tf_op | source)
XLA Modules:
  0.0 115.7 jit_solution(2867983726727924191)
XLA Ops:
  0.0 1.1 copy.44
  1.1 1.1 broadcast_in_dim.106
  2.2 0.0 copy-start
  2.2 0.0 copy-start.1
  2.2 11.6 %all-to-all-start = ((bf16[32,16,1024]{2,0,1:T(8,128)(2,1)}), bf16[32,16,1024]{2,0,1:T(8,128)(2,1)S(1)}, u32[]{:S(2)}, u32[]{:S(2)}) async-start(bf16[32,16,1024]{2,0,1:T(8,128)(2,1)} %bitcast.9), calls=%async_computation | async-start | bytes 2097152 | tf_op jit(solution)/shard_map/all_to_all | solution.py:111
  13.8 0.0 copy-done
  13.8 0.2 and_reduce_fusion
  14.0 0.2 fusion.1
  14.2 0.0 copy-start.2
  14.2 0.1 copy.34
  14.4 0.0 copy-done.1
  14.4 0.1 copy.35
  14.5 0.1 pad.29.clone
  14.6 0.1 fusion.5
  14.7 45.4 %all-gather = bf16[1152,256]{1,0:T(8,128)(2,1)S(1)} all-gather(bf16[144,256]{1,0:T(8,128)(2,1)S(1)} %fusion.5), channel_id=2, replica_groups=mesh['rows'=32,'cols_0'=8,'cols_1'=2] {'cols_0'}, dimensions={0}, use_global_device_ids=true | all-gather | bytes 663552 | tf_op jit(solution)/shard_map/all_gather | solution.py:104
  60.1 1.9 %collective-permute-start = (bf16[8,144,256]{2,1,0:T(8,128)(2,1)S(1)}, bf16[8,144,256]{2,1,0:T(8,128)(2,1)S(1)}, u32[]{:S(2)}, u32[]{:S(2)}) collective-permute-start(bf16[8,144,256]{2,1,0:T(8,128)(2,1)S(1)} %bitcast.68), channel_id=1, source_target_pairs={{0,16},{16,0},{32,48},{48,32},{64,80},{80,64},{96,112},{112,96},{1... | collective-permute-start | bytes 1769480 | tf_op jit(solution)/shard_map/ppermute | solution.py:106
  62.1 0.0 copy-done.2
  62.1 0.1 fusion.10
  62.2 0.1 slice_bitcast_fusion.7
  62.2 0.1 slice_bitcast_fusion.6
  62.3 0.1 slice_bitcast_fusion.5
  62.4 0.1 slice_bitcast_fusion.4
  62.4 1.6 %collective-permute-done = bf16[8,144,256]{2,1,0:T(8,128)(2,1)S(1)} collective-permute-done((bf16[8,144,256]{2,1,0:T(8,128)(2,1)S(1)}, bf16[8,144,256]{2,1,0:T(8,128)(2,1)S(1)}, u32[]{:S(2)}, u32[]{:S(2)}) %collective-permute-start) | collective-permute-done | bytes 589856 | tf_op jit(solution)/shard_map/ppermute | solution.py:106
  64.0 1.3 %maximum_select_fusion.a_ref = bf16[8,144,512]{2,1,0:T(8,128)(2,1)} fusion(bf16[8,144,256]{2,1,0:T(8,128)(2,1)S(1)} %collective-permute-done, bf16[8,144,256]{2,1,0:T(8,128)(2,1)S(1)} %bitcast.69, pred[]{:T(512)S(6)} %eq.71), kind=kLoop, calls=%fused_computation | loop fusion | flops 5308416 | bytes 2359297 | tf_op jit(solution)/shard_map/jit(_where)/select_n | solution.py:107
  65.3 0.0 all-to-all-done
  65.3 1.3 %copy.33 = bf16[512,1024]{0,1:T(8,128)(2,1)} copy(bf16[512,1024]{1,0:T(8,128)(2,1)S(1)} %bitcast.66) | data formatting | bytes 2097152 | tf_op jit(solution)/shard_map/reshape | solution.py:112
  66.7 9.9 %shard_map.46 = f32[8,16,512]{2,1,0:T(8,128)} custom-call(s32[1]{0:T(128)} %constant.58.clone.1.offset_ref, bf16[1024,512]{1,0:T(8,128)(2,1)} %bitcast.67, bf16[8,144,512]{2,1,0:T(8,128)(2,1)} %maximum_select_fusion.a_ref), custom_call_target="tpu_custom_call" | custom-call | tf_op jit(solution)/shard_map/pallas_call | solution.py:48
  76.5 4.7 %all-to-all-start.1 = ((f32[8,16,512]{2,1,0:T(8,128)}), f32[8,16,512]{2,1,0:T(8,128)S(1)}, u32[]{:S(2)}, u32[]{:S(2)}) async-start(f32[8,16,512]{2,1,0:T(8,128)} %shard_map.46), calls=%async_computation.1 | async-start | bytes 524288 | tf_op jit(solution)/shard_map/all_to_all | solution.py:116
  81.3 0.6 fusion.9
  81.9 0.1 maximum_compare_fusion
  81.9 0.1 compare_bitcast_fusion.7
  82.0 11.4 %all-to-all-done.1 = f32[8,16,512]{2,1,0:T(8,128)S(1)} async-done(((f32[8,16,512]{2,1,0:T(8,128)}), f32[8,16,512]{2,1,0:T(8,128)S(1)}, u32[]{:S(2)}, u32[]{:S(2)}) %all-to-all-start.1) | async-done | bytes 262176 | tf_op jit(solution)/shard_map/all_to_all | solution.py:116
  93.4 0.1 copy.37
  93.6 0.1 fusion.8
  93.7 0.1 maximum_select_fusion.12
  93.9 0.1 slice.154
  94.0 0.1 slice.155
  94.2 0.1 slice.156
  94.3 0.0 copy-start.3
  94.4 0.1 slice.157
  94.6 0.4 copy-done.3
  95.0 0.6 slice_select_fusion
  95.6 3.9 %collective-permute-start.1 = (f32[2,512]{0,1:T(8,128)S(1)}, f32[2,512]{0,1:T(8,128)S(1)}, u32[]{:S(2)}, u32[]{:S(2)}) collective-permute-start(f32[2,512]{0,1:T(8,128)S(1)} %slice_select_fusion), channel_id=1, source_target_pairs={{16,0},{32,16},{48,32},{64,48},{80,64},{96,80},{112,96},{128,112},... | collective-permute-start | bytes 12296 | tf_op jit(solution)/shard_map/ppermute | solution.py:82
  99.5 0.1 maximum_select_fusion.6
  99.7 0.1 maximum_select_fusion.5
  99.8 0.1 maximum_select_fusion.4
  99.9 0.1 maximum_select_fusion.3
  100.1 0.1 slice.165
  100.2 0.6 concatenate.102
  100.9 1.9 %collective-permute-start.2 = (f32[2,512]{0,1:T(8,128)S(1)}, f32[2,512]{0,1:T(8,128)S(1)}, u32[]{:S(2)}, u32[]{:S(2)}) collective-permute-start(f32[2,512]{0,1:T(8,128)S(1)} %concatenate.102), channel_id=1, source_target_pairs={{0,16},{16,32},{32,48},{48,64},{64,80},{80,96},{96,112},{112,128},... | collective-permute-start | bytes 12296 | tf_op jit(solution)/shard_map/ppermute | solution.py:81
  102.8 2.2 %collective-permute-done.1 = f32[2,512]{0,1:T(8,128)S(1)} collective-permute-done((f32[2,512]{0,1:T(8,128)S(1)}, f32[2,512]{0,1:T(8,128)S(1)}, u32[]{:S(2)}, u32[]{:S(2)}) %collective-permute-start.1) | collective-permute-done | bytes 4128 | tf_op jit(solution)/shard_map/ppermute | solution.py:82
  105.0 0.3 slice_reduce_fusion.3
  105.3 9.1 %collective-permute-done.2 = f32[2,512]{0,1:T(8,128)S(1)} collective-permute-done((f32[2,512]{0,1:T(8,128)S(1)}, f32[2,512]{0,1:T(8,128)S(1)}, u32[]{:S(2)}, u32[]{:S(2)}) %collective-permute-start.2) | collective-permute-done | bytes 4128 | tf_op jit(solution)/shard_map/ppermute | solution.py:81
  114.4 0.3 slice_reduce_fusion.2
  114.7 1.0 fusion
  (8 shorter events, 0.2 us)
Async XLA Ops:
  2.2 11.6 %copy-start = (s32[512,128]{1,0:T(8,128)S(1)}, s32[512,128]{1,0:T(8,128)}, u32[]{:S(2)}) copy-start(s32[512,128]{1,0:T(8,128)} %param.6) | copy-start | bytes 786436
  2.2 12.1 %copy-start.1 = (bf16[512,128]{1,0:T(8,128)(2,1)S(1)}, bf16[512,128]{1,0:T(8,128)(2,1)}, u32[]{:S(2)}) copy-start(bf16[512,128]{1,0:T(8,128)(2,1)} %param.5) | copy-start | bytes 393220
  2.2 63.1 %all-to-all-start = ((bf16[32,16,1024]{2,0,1:T(8,128)(2,1)}), bf16[32,16,1024]{2,0,1:T(8,128)(2,1)S(1)}, u32[]{:S(2)}, u32[]{:S(2)}) async-start(bf16[32,16,1024]{2,0,1:T(8,128)(2,1)} %bitcast.9), calls=%async_computation | async-start | bytes 2097152 | tf_op jit(solution)/shard_map/all_to_all | solution.py:111
  14.2 47.9 %copy-start.2 = (s32[128]{0:T(128)S(1)}, s32[128]{0:T(128)}, u32[]{:S(2)}) copy-start(s32[128]{0:T(128)} %param.7) | copy-start | bytes 1540
  60.1 3.9 %collective-permute-start = (bf16[8,144,256]{2,1,0:T(8,128)(2,1)S(1)}, bf16[8,144,256]{2,1,0:T(8,128)(2,1)S(1)}, u32[]{:S(2)}, u32[]{:S(2)}) collective-permute-start(bf16[8,144,256]{2,1,0:T(8,128)(2,1)S(1)} %bitcast.68), channel_id=1, source_target_pairs={{0,16},{16,0},{32,48},{48,32},{64,80},{80,64},{96,112},{112,96},{1... | collective-permute-start | bytes 1769480 | tf_op jit(solution)/shard_map/ppermute | solution.py:106
  76.5 16.9 %all-to-all-start.1 = ((f32[8,16,512]{2,1,0:T(8,128)}), f32[8,16,512]{2,1,0:T(8,128)S(1)}, u32[]{:S(2)}, u32[]{:S(2)}) async-start(f32[8,16,512]{2,1,0:T(8,128)} %shard_map.46), calls=%async_computation.1 | async-start | bytes 524288 | tf_op jit(solution)/shard_map/all_to_all | solution.py:116
  94.3 0.7 copy-start.3
  95.6 9.4 %collective-permute-start.1 = (f32[2,512]{0,1:T(8,128)S(1)}, f32[2,512]{0,1:T(8,128)S(1)}, u32[]{:S(2)}, u32[]{:S(2)}) collective-permute-start(f32[2,512]{0,1:T(8,128)S(1)} %slice_select_fusion), channel_id=1, source_target_pairs={{16,0},{32,16},{48,32},{64,48},{80,64},{96,80},{112,96},{128,112},... | collective-permute-start | bytes 12296 | tf_op jit(solution)/shard_map/ppermute | solution.py:82
  100.9 13.5 %collective-permute-start.2 = (f32[2,512]{0,1:T(8,128)S(1)}, f32[2,512]{0,1:T(8,128)S(1)}, u32[]{:S(2)}, u32[]{:S(2)}) collective-permute-start(f32[2,512]{0,1:T(8,128)S(1)} %concatenate.102), channel_id=1, source_target_pairs={{0,16},{16,32},{32,48},{48,64},{64,80},{80,96},{96,112},{112,128},... | collective-permute-start | bytes 12296 | tf_op jit(solution)/shard_map/ppermute | solution.py:81

commit v5 on v4

--- a/solution.py
+++ b/solution.py
@@ -12,44 +12,45 @@
 SHARE = "cols_1"
 CODE = 32
 MOST = 32
+HALVES = 2
 
 
-def wave_kernel(offset_ref, gt_ref, a_ref, o_ref):
+def wave_kernel(gt_ref, a_ref, o_ref):
     slots = a_ref.shape[0] - 16
     width = gt_ref.shape[1]
     lanes = a_ref.shape[1]
     code = a_ref[slots:slots + 16, :].astype(jnp.float32)
     start = (code[0:1] * CODE + code[1:2]).astype(jnp.int32)
-    start = (start - offset_ref[0]) & (width - 1)
-    dense = jnp.concatenate(
-        [a_ref[0:slots, :].astype(jnp.float32), jnp.zeros((width - slots, lanes), jnp.float32)], axis=0
-    )
+    dense = a_ref[0:slots, :].astype(jnp.float32)
+    reach = slots
     for bit in range(max(1, (width - 1).bit_length())):
-        rolled = pltpu.roll(dense, 1 << bit, 0)
+        step = 1 << bit
+        reach = reach + step
+        extent = min(width, -(-reach // 8) * 8)
+        if extent > dense.shape[0]:
+            dense = jnp.concatenate([dense, jnp.zeros((extent - dense.shape[0], lanes), jnp.float32)], axis=0)
+        rolled = pltpu.roll(dense, step, 0)
         dense = jnp.where(((start >> bit) & 1) == 1, rolled, dense)
+    if dense.shape[0] < width:
+        dense = jnp.concatenate([dense, jnp.zeros((width - dense.shape[0], lanes), jnp.float32)], axis=0)
     wave = jnp.dot(gt_ref[...], dense.astype(jnp.bfloat16), preferred_element_type=jnp.float32)
     rows = wave.shape[0]
     o_ref[...] = jnp.max(wave.reshape(rows // TSTEP, TSTEP, lanes), axis=1)
 
 
-def wave_maxima(offset, panel_t, coded):
+def wave_maxima(panel_t, coded):
     parts, height, lanes = coded.shape
     rows, width = panel_t.shape
-    assert width & (width - 1) == 0
-    grid_spec = pltpu.PrefetchScalarGridSpec(
-        num_scalar_prefetch=1,
+    return pl.pallas_call(
+        wave_kernel,
         grid=(parts,),
         in_specs=[
-            pl.BlockSpec((rows, width), lambda p, o: (0, 0)),
-            pl.BlockSpec((None, height, lanes), lambda p, o: (p, 0, 0)),
+            pl.BlockSpec((rows, width), lambda p: (0, 0)),
+            pl.BlockSpec((None, height, lanes), lambda p: (p, 0, 0)),
         ],
-        out_specs=pl.BlockSpec((None, rows // TSTEP, lanes), lambda p, o: (p, 0, 0)),
-    )
-    return pl.pallas_call(
-        wave_kernel,
-        grid_spec=grid_spec,
+        out_specs=pl.BlockSpec((None, rows // TSTEP, lanes), lambda p: (p, 0, 0)),
         out_shape=jax.ShapeDtypeStruct((parts, rows // TSTEP, lanes), jnp.float32),
-    )(offset, panel_t, coded)
+    )(panel_t, coded)
 
 
 def shifted(values, step, fill):
@@ -108,12 +109,15 @@
 
     pieces = greens.reshape(own_sources, parts, 1, block)
     pieces = jnp.broadcast_to(pieces, (own_sources, parts, shares, block)).reshape(own_sources, parts * shares, block)
-    pieces = lax.all_to_all(pieces, COLS, 1, 0, tiled=True)
-    panel_t = pieces.reshape(width, block).T
-    offset = jnp.zeros((1,), jnp.int32)
-
-    maxima = wave_maxima(offset, panel_t, coded)
-    maxima = lax.all_to_all(maxima, SPLIT, 0, 0, tiled=True)
+    piece = block // HALVES
+    outs = []
+    for half in range(HALVES):
+        sub = pieces[:, :, half * piece:(half + 1) * piece]
+        sub = lax.all_to_all(sub, COLS, 1, 0, tiled=True)
+        panel_t = sub.reshape(width, piece).T
+        maxima = wave_maxima(panel_t, coded)
+        outs.append(lax.all_to_all(maxima, SPLIT, 0, 0, tiled=True))
+    maxima = jnp.concatenate(outs, axis=1)
     return point_peaks(maxima.reshape(-1, scen), win_point, MOST)
 
 

time: 116 us -> 125 us (1.078)
  blocking collectives: 45.4 us -> 34.1 us
  starting transfers between devices: 24.1 us -> 35 us
  Pallas kernels: 9.86 us -> 15.9 us
  waiting for transfers between devices: 24.3 us -> 25.7 us
    all_to_all x2 -> x4, starting transfers between devices: 16.3 us -> 27.9 us  [the longest x2 17.4 us: local(): sub = lax.all_to_all(sub, COLS, 1, 0, tiled=True)]
    all_gather x1, blocking collectives: 45.4 us -> 34.1 us  [local(): mine = lax.all_gather(mine, SPLIT, axis=0, tiled=False)]
    pallas_call x1 -> x2, Pallas kernels: 9.86 us -> 15.9 us  [wave_maxima(): pl.pallas_call(wave_kernel, grid=(parts,), in_specs=[pl.BlockSpec((rows,...]
    all_to_all x2 -> x4, waiting for transfers between devices: 11.4 us -> 14.4 us  [the longest x2 8.47 us: local(): outs.append(lax.all_to_all(maxima, SPLIT, 0, 0, tiled=True))]
    ppermute x1, waiting for transfers between devices: 1.58 us -> 0.01 us  [local(): theirs = lax.ppermute(mine, 'rows', [(i, i ^ 1) for i in range(count_rows)])]
    ppermute x1, waiting for transfers between devices: 9.09 us -> 10.6 us  [point_peaks(): lax.ppermute(to_right, 'rows', [(i, i + 1) for i in range(count - 1)])]
    ppermute x1, waiting for transfers between devices: 2.18 us -> 0.72 us  [point_peaks(): lax.ppermute(to_left, 'rows', [(i + 1, i) for i in range(count - 1)])]
  transfers between devices with their start and end apart: 5 -> 7, of which waited for: 4 -> 5; matrix products, arithmetic and copies ran while one was open for 4% -> 6% of each run, Pallas kernels for 0% -> 13%
where the time goes in v5:
time: 125 us; the launch traced here: 124 us
  starting transfers between devices  35 us (28%)
  blocking collectives  34.1 us (27%)
  waiting for transfers between devices  25.7 us (21%)
  Pallas kernels  15.9 us (13%)
  local copies, waits for them, and re-layouts  8.32 us (7%)
  other arithmetic  4.51 us (4%)
    all_gather x1, blocking collectives, local(): mine = lax.all_gather(mine, SPLIT, axis=0, tiled=False)  34.1 us
    all_to_all x2, starting transfers between devices, local(): sub = lax.all_to_all(sub, COLS, 1, 0, tiled=True)  17.4 us
    pallas_call x2, Pallas kernels, wave_maxima(): pl.pallas_call(wave_kernel, grid=(parts,), in_specs=[pl.BlockSpec((rows,...  15.9 us
    ppermute x1, waiting for transfers between devices, point_peaks(): lax.ppermute(to_right, 'rows', [(i, i + 1) for i in range(count - 1)])  10.6 us
    all_to_all x2, starting transfers between devices, local(): outs.append(lax.all_to_all(maxima, SPLIT, 0, 0, tiled=True))  10.5 us
    all_to_all x2, waiting for transfers between devices, local(): outs.append(lax.all_to_all(maxima, SPLIT, 0, 0, tiled=True))  8.47 us
    all_to_all x2, waiting for transfers between devices, local(): sub = lax.all_to_all(sub, COLS, 1, 0, tiled=True)  5.93 us
    ppermute x1, starting transfers between devices, point_peaks(): lax.ppermute(to_left, 'rows', [(i + 1, i) for i in range(count - 1)])  3.26 us
  transfers between devices with their start and end apart: 7, of which 5 were waited for; matrix products, arithmetic and copies ran while one was open for 6% of the time, Pallas kernels for 13%

profile of v5, /device:TPU:6, one launch (start us, length us, event | category | flops | bytes accessed | tf_op | source)
XLA Modules:
  0.0 123.9 jit_solution(18058709175112935729)
XLA Ops:
  0.0 1.1 copy.47
  1.1 0.1 broadcast_in_dim.106
  1.2 0.0 copy-start
  1.2 1.2 fusion.8
  2.4 0.0 copy-start.1
  2.4 11.6 %all-to-all-start = ((bf16[32,16,512]{2,0,1:T(8,128)(2,1)}), bf16[32,16,512]{2,0,1:T(8,128)(2,1)S(1)}, u32[]{:S(2)}, u32[]{:S(2)}) async-start(bf16[32,16,512]{2,0,1:T(8,128)(2,1)} %get-tuple-element.11), calls=%async_computation | async-start | bytes 1048576 | tf_op jit(solution)/shard_map/all_to_all | solution.py:116
  14.0 0.0 copy-done
  14.0 0.2 and_reduce_fusion
  14.2 0.2 fusion.1
  14.4 0.0 copy-start.2
  14.4 0.1 copy.36
  14.5 0.0 copy-done.1
  14.5 0.1 copy.37
  14.7 0.1 pad.31.clone
  14.8 0.1 fusion.5
  14.9 34.1 %all-gather = bf16[1152,256]{1,0:T(8,128)(2,1)S(1)} all-gather(bf16[144,256]{1,0:T(8,128)(2,1)S(1)} %fusion.5), channel_id=2, replica_groups=mesh['rows'=32,'cols_0'=8,'cols_1'=2] {'cols_0'}, dimensions={0}, use_global_device_ids=true | all-gather | bytes 663552 | tf_op jit(solution)/shard_map/all_gather | solution.py:105
  49.0 1.9 %collective-permute-start = (bf16[8,144,256]{2,1,0:T(8,128)(2,1)S(1)}, bf16[8,144,256]{2,1,0:T(8,128)(2,1)S(1)}, u32[]{:S(2)}, u32[]{:S(2)}) collective-permute-start(bf16[8,144,256]{2,1,0:T(8,128)(2,1)S(1)} %bitcast.73), channel_id=1, source_target_pairs={{0,16},{16,0},{32,48},{48,32},{64,80},{80,64},{96,112},{112,96},{1... | collective-permute-start | bytes 1769480 | tf_op jit(solution)/shard_map/ppermute | solution.py:107
  50.9 0.0 copy-done.2
  50.9 0.0 all-to-all-done
  50.9 5.8 %all-to-all-start.2 = ((bf16[32,16,512]{2,0,1:T(8,128)(2,1)}), bf16[32,16,512]{2,0,1:T(8,128)(2,1)S(1)}, u32[]{:S(2)}, u32[]{:S(2)}) async-start(bf16[32,16,512]{2,0,1:T(8,128)(2,1)} %get-tuple-element.12), calls=%async_computation.2 | async-start | bytes 1048576 | tf_op jit(solution)/shard_map/all_to_all | solution.py:116
  56.8 0.1 fusion.11
  56.9 0.1 slice_bitcast_fusion.7
  56.9 0.1 slice_bitcast_fusion.6
  57.0 0.1 slice_bitcast_fusion.5
  57.1 0.0 collective-permute-done
  57.1 1.3 %maximum_select_fusion.a_ref = bf16[8,144,512]{2,1,0:T(8,128)(2,1)} fusion(bf16[8,144,256]{2,1,0:T(8,128)(2,1)S(1)} %collective-permute-done, bf16[8,144,256]{2,1,0:T(8,128)(2,1)S(1)} %bitcast.74, pred[]{:T(512)S(6)} %eq.71), kind=kLoop, calls=%fused_computation | loop fusion | flops 5308416 | bytes 2359297 | tf_op jit(solution)/shard_map/jit(_where)/select_n | solution.py:108
  58.4 1.0 copy.35
  59.4 8.0 %shard_map.46 = f32[8,8,512]{2,1,0:T(8,128)} custom-call(bf16[512,512]{1,0:T(8,128)(2,1)} %bitcast.80, bf16[8,144,512]{2,1,0:T(8,128)(2,1)} %maximum_select_fusion.a_ref), custom_call_target="tpu_custom_call" | custom-call | tf_op jit(solution)/shard_map/pallas_call | solution.py:44
  67.4 5.9 %all-to-all-done.2 = bf16[32,16,512]{2,0,1:T(8,128)(2,1)S(1)} async-done(((bf16[32,16,512]{2,0,1:T(8,128)(2,1)}), bf16[32,16,512]{2,0,1:T(8,128)(2,1)S(1)}, u32[]{:S(2)}, u32[]{:S(2)}) %all-to-all-start.2) | async-done | bytes 524320 | tf_op jit(solution)/shard_map/all_to_all | solution.py:116
  73.3 3.4 %all-to-all-start.1 = ((f32[8,8,512]{2,1,0:T(8,128)}), f32[8,8,512]{2,1,0:T(8,128)S(1)}, u32[]{:S(2)}, u32[]{:S(2)}) async-start(f32[8,8,512]{2,1,0:T(8,128)} %shard_map.46), calls=%async_computation.1 | async-start | bytes 262144 | tf_op jit(solution)/shard_map/all_to_all | solution.py:119
  76.7 0.1 slice_bitcast_fusion.4
  76.8 0.1 maximum_compare_fusion
  76.8 1.0 copy.38
  77.9 8.0 %shard_map.47 = f32[8,8,512]{2,1,0:T(8,128)} custom-call(bf16[512,512]{1,0:T(8,128)(2,1)} %bitcast.79, bf16[8,144,512]{2,1,0:T(8,128)(2,1)} %maximum_select_fusion.a_ref), custom_call_target="tpu_custom_call" | custom-call | tf_op jit(solution)/shard_map/pallas_call | solution.py:44
  85.8 0.1 all-to-all-done.1
  86.0 7.1 %all-to-all-start.3 = ((f32[8,8,512]{2,1,0:T(8,128)}), f32[8,8,512]{2,1,0:T(8,128)S(1)}, u32[]{:S(2)}, u32[]{:S(2)}) async-start(f32[8,8,512]{2,1,0:T(8,128)} %shard_map.47), calls=%async_computation.3 | async-start | bytes 262144 | tf_op jit(solution)/shard_map/all_to_all | solution.py:119
  93.1 0.6 fusion.10
  93.7 0.1 compare_bitcast_fusion.7
  93.8 8.4 %all-to-all-done.3 = f32[8,8,512]{2,1,0:T(8,128)S(1)} async-done(((f32[8,8,512]{2,1,0:T(8,128)}), f32[8,8,512]{2,1,0:T(8,128)S(1)}, u32[]{:S(2)}, u32[]{:S(2)}) %all-to-all-start.3) | async-done | bytes 131104 | tf_op jit(solution)/shard_map/all_to_all | solution.py:119
  102.2 0.1 copy.40
  102.3 0.1 fusion.9
  102.4 0.1 maximum_select_fusion.12
  102.6 0.1 slice.164
  102.8 0.1 slice.165
  102.9 0.1 slice.166
  103.1 0.0 copy-start.3
  103.1 0.1 slice.167
  103.3 0.4 copy-done.3
  103.7 0.7 slice_select_fusion
  104.4 3.3 %collective-permute-start.1 = (f32[2,512]{0,1:T(8,128)S(1)}, f32[2,512]{0,1:T(8,128)S(1)}, u32[]{:S(2)}, u32[]{:S(2)}) collective-permute-start(f32[2,512]{0,1:T(8,128)S(1)} %slice_select_fusion), channel_id=1, source_target_pairs={{16,0},{32,16},{48,32},{64,48},{80,64},{96,80},{112,96},{128,112},... | collective-permute-start | bytes 12296 | tf_op jit(solution)/shard_map/ppermute | solution.py:83
  107.6 0.1 maximum_select_fusion.6
  107.8 0.1 maximum_select_fusion.5
  107.9 0.1 maximum_select_fusion.4
  108.1 0.1 maximum_select_fusion.3
  108.2 0.1 slice.175
  108.3 0.7 concatenate.106
  109.0 1.9 %collective-permute-start.2 = (f32[2,512]{0,1:T(8,128)S(1)}, f32[2,512]{0,1:T(8,128)S(1)}, u32[]{:S(2)}, u32[]{:S(2)}) collective-permute-start(f32[2,512]{0,1:T(8,128)S(1)} %concatenate.106), channel_id=1, source_target_pairs={{0,16},{16,32},{32,48},{48,64},{64,80},{80,96},{96,112},{112,128},... | collective-permute-start | bytes 12296 | tf_op jit(solution)/shard_map/ppermute | solution.py:82
  110.9 0.7 collective-permute-done.1
  111.6 0.3 slice_reduce_fusion.3
  111.9 10.6 %collective-permute-done.2 = f32[2,512]{0,1:T(8,128)S(1)} collective-permute-done((f32[2,512]{0,1:T(8,128)S(1)}, f32[2,512]{0,1:T(8,128)S(1)}, u32[]{:S(2)}, u32[]{:S(2)}) %collective-permute-start.2) | collective-permute-done | bytes 4128 | tf_op jit(solution)/shard_map/ppermute | solution.py:82
  122.5 0.3 slice_reduce_fusion.2
  122.8 1.0 fusion
  (9 shorter events, 0.2 us)
Async XLA Ops:
  1.2 12.8 %copy-start = (s32[512,128]{1,0:T(8,128)S(1)}, s32[512,128]{1,0:T(8,128)}, u32[]{:S(2)}) copy-start(s32[512,128]{1,0:T(8,128)} %param.6) | copy-start | bytes 786436
  2.4 12.2 %copy-start.1 = (bf16[512,128]{1,0:T(8,128)(2,1)S(1)}, bf16[512,128]{1,0:T(8,128)(2,1)}, u32[]{:S(2)}) copy-start(bf16[512,128]{1,0:T(8,128)(2,1)} %param.5) | copy-start | bytes 393220
  2.4 48.5 %all-to-all-start = ((bf16[32,16,512]{2,0,1:T(8,128)(2,1)}), bf16[32,16,512]{2,0,1:T(8,128)(2,1)S(1)}, u32[]{:S(2)}, u32[]{:S(2)}) async-start(bf16[32,16,512]{2,0,1:T(8,128)(2,1)} %get-tuple-element.11), calls=%async_computation | async-start | bytes 1048576 | tf_op jit(solution)/shard_map/all_to_all | solution.py:116
  14.4 36.6 %copy-start.2 = (s32[128]{0:T(128)S(1)}, s32[128]{0:T(128)}, u32[]{:S(2)}) copy-start(s32[128]{0:T(128)} %param.7) | copy-start | bytes 1540
  49.0 8.1 %collective-permute-start = (bf16[8,144,256]{2,1,0:T(8,128)(2,1)S(1)}, bf16[8,144,256]{2,1,0:T(8,128)(2,1)S(1)}, u32[]{:S(2)}, u32[]{:S(2)}) collective-permute-start(bf16[8,144,256]{2,1,0:T(8,128)(2,1)S(1)} %bitcast.73), channel_id=1, source_target_pairs={{0,16},{16,0},{32,48},{48,32},{64,80},{80,64},{96,112},{112,96},{1... | collective-permute-start | bytes 1769480 | tf_op jit(solution)/shard_map/ppermute | solution.py:107
  50.9 22.4 %all-to-all-start.2 = ((bf16[32,16,512]{2,0,1:T(8,128)(2,1)}), bf16[32,16,512]{2,0,1:T(8,128)(2,1)S(1)}, u32[]{:S(2)}, u32[]{:S(2)}) async-start(bf16[32,16,512]{2,0,1:T(8,128)(2,1)} %get-tuple-element.12), calls=%async_computation.2 | async-start | bytes 1048576 | tf_op jit(solution)/shard_map/all_to_all | solution.py:116
  73.3 12.6 %all-to-all-start.1 = ((f32[8,8,512]{2,1,0:T(8,128)}), f32[8,8,512]{2,1,0:T(8,128)S(1)}, u32[]{:S(2)}, u32[]{:S(2)}) async-start(f32[8,8,512]{2,1,0:T(8,128)} %shard_map.46), calls=%async_computation.1 | async-start | bytes 262144 | tf_op jit(solution)/shard_map/all_to_all | solution.py:119
  86.0 16.2 %all-to-all-start.3 = ((f32[8,8,512]{2,1,0:T(8,128)}), f32[8,8,512]{2,1,0:T(8,128)S(1)}, u32[]{:S(2)}, u32[]{:S(2)}) async-start(f32[8,8,512]{2,1,0:T(8,128)} %shard_map.47), calls=%async_computation.3 | async-start | bytes 262144 | tf_op jit(solution)/shard_map/all_to_all | solution.py:119
  103.1 0.7 copy-start.3
  104.4 7.3 %collective-permute-start.1 = (f32[2,512]{0,1:T(8,128)S(1)}, f32[2,512]{0,1:T(8,128)S(1)}, u32[]{:S(2)}, u32[]{:S(2)}) collective-permute-start(f32[2,512]{0,1:T(8,128)S(1)} %slice_select_fusion), channel_id=1, source_target_pairs={{16,0},{32,16},{48,32},{64,48},{80,64},{96,80},{112,96},{128,112},... | collective-permute-start | bytes 12296 | tf_op jit(solution)/shard_map/ppermute | solution.py:83
  109.0 13.5 %collective-permute-start.2 = (f32[2,512]{0,1:T(8,128)S(1)}, f32[2,512]{0,1:T(8,128)S(1)}, u32[]{:S(2)}, u32[]{:S(2)}) collective-permute-start(f32[2,512]{0,1:T(8,128)S(1)} %concatenate.106), channel_id=1, source_target_pairs={{0,16},{16,32},{32,48},{48,64},{64,80},{80,96},{96,112},{112,128},... | collective-permute-start | bytes 12296 | tf_op jit(solution)/shard_map/ppermute | solution.py:82

commit v6 on v5

--- a/solution.py
+++ b/solution.py
@@ -12,7 +12,6 @@
 SHARE = "cols_1"
 CODE = 32
 MOST = 32
-HALVES = 2
 
 
 def wave_kernel(gt_ref, a_ref, o_ref):
@@ -29,7 +28,10 @@
         extent = min(width, -(-reach // 8) * 8)
         if extent > dense.shape[0]:
             dense = jnp.concatenate([dense, jnp.zeros((extent - dense.shape[0], lanes), jnp.float32)], axis=0)
-        rolled = pltpu.roll(dense, step, 0)
+        if step % 8 == 0:
+            rolled = jnp.concatenate([dense[extent - step:], dense[: extent - step]], axis=0)
+        else:
+            rolled = pltpu.roll(dense, step, 0)
         dense = jnp.where(((start >> bit) & 1) == 1, rolled, dense)
     if dense.shape[0] < width:
         dense = jnp.concatenate([dense, jnp.zeros((width - dense.shape[0], lanes), jnp.float32)], axis=0)
@@ -109,15 +111,11 @@
 
     pieces = greens.reshape(own_sources, parts, 1, block)
     pieces = jnp.broadcast_to(pieces, (own_sources, parts, shares, block)).reshape(own_sources, parts * shares, block)
-    piece = block // HALVES
-    outs = []
-    for half in range(HALVES):
-        sub = pieces[:, :, half * piece:(half + 1) * piece]
-        sub = lax.all_to_all(sub, COLS, 1, 0, tiled=True)
-        panel_t = sub.reshape(width, piece).T
-        maxima = wave_maxima(panel_t, coded)
-        outs.append(lax.all_to_all(maxima, SPLIT, 0, 0, tiled=True))
-    maxima = jnp.concatenate(outs, axis=1)
+    pieces = lax.all_to_all(pieces, COLS, 1, 0, tiled=True)
+    panel_t = pieces.reshape(width, block).T
+
+    maxima = wave_maxima(panel_t, coded)
+    maxima = lax.all_to_all(maxima, SPLIT, 0, 0, tiled=True)
     return point_peaks(maxima.reshape(-1, scen), win_point, MOST)
 
 

time: 125 us -> 116 us (0.928)
  blocking collectives: 34.1 us -> 45.4 us
  starting transfers between devices: 35 us -> 24 us
  Pallas kernels: 15.9 us -> 9.6 us
  waiting for transfers between devices: 25.7 us -> 24.3 us
    all_to_all x4 -> x2, starting transfers between devices: 27.9 us -> 16.3 us  [the longest x1 11.6 us: local(): pieces = lax.all_to_all(pieces, COLS, 1, 0, tiled=True)]
    all_gather x1, blocking collectives: 34.1 us -> 45.4 us  [local(): mine = lax.all_gather(mine, SPLIT, axis=0, tiled=False)]
    pallas_call x2 -> x1, Pallas kernels: 15.9 us -> 9.6 us  [wave_maxima(): pl.pallas_call(wave_kernel, grid=(parts,), in_specs=[pl.BlockSpec((rows,...]
    all_to_all x4 -> x2, waiting for transfers between devices: 14.4 us -> 11.4 us  [the longest x1 11.4 us: local(): maxima = lax.all_to_all(maxima, SPLIT, 0, 0, tiled=True)]
    ppermute x1, waiting for transfers between devices: 0.01 us -> 1.58 us  [local(): theirs = lax.ppermute(mine, 'rows', [(i, i ^ 1) for i in range(count_rows)])]
    ppermute x1, waiting for transfers between devices: 0.72 us -> 2.19 us  [point_peaks(): lax.ppermute(to_left, 'rows', [(i + 1, i) for i in range(count - 1)])]
    ppermute x1, waiting for transfers between devices: 10.6 us -> 9.09 us  [point_peaks(): lax.ppermute(to_right, 'rows', [(i, i + 1) for i in range(count - 1)])]
  transfers between devices with their start and end apart: 7 -> 5, of which waited for: 5 -> 4; matrix products, arithmetic and copies ran while one was open for 6% -> 4% of each run, Pallas kernels for 13% -> 0%
where the time goes in v6:
time: 116 us; the launch traced here: 115 us
  blocking collectives  45.4 us (39%)
  waiting for transfers between devices  24.3 us (21%)
  starting transfers between devices  24 us (21%)
  Pallas kernels  9.6 us (8%)
  local copies, waits for them, and re-layouts  7.39 us (6%)
  other arithmetic  4.41 us (4%)
    all_gather x1, blocking collectives, local(): mine = lax.all_gather(mine, SPLIT, axis=0, tiled=False)  45.4 us
    all_to_all x1, starting transfers between devices, local(): pieces = lax.all_to_all(pieces, COLS, 1, 0, tiled=True)  11.6 us
    all_to_all x1, waiting for transfers between devices, local(): maxima = lax.all_to_all(maxima, SPLIT, 0, 0, tiled=True)  11.4 us
    pallas_call x1, Pallas kernels, wave_maxima(): pl.pallas_call(wave_kernel, grid=(parts,), in_specs=[pl.BlockSpec((rows,...  9.6 us
    ppermute x1, waiting for transfers between devices, point_peaks(): lax.ppermute(to_right, 'rows', [(i, i + 1) for i in range(count - 1)])  9.09 us
    all_to_all x1, starting transfers between devices, local(): maxima = lax.all_to_all(maxima, SPLIT, 0, 0, tiled=True)  4.74 us
    ppermute x1, starting transfers between devices, point_peaks(): lax.ppermute(to_left, 'rows', [(i + 1, i) for i in range(count - 1)])  3.89 us
  transfers between devices with their start and end apart: 5, of which 4 were waited for; matrix products, arithmetic and copies ran while one was open for 4% of the time, Pallas kernels for 0%

profile of v6, /device:TPU:6, one launch (start us, length us, event | category | flops | bytes accessed | tf_op | source)
XLA Modules:
  0.0 115.4 jit_solution(498557814718575772)
XLA Ops:
  0.0 1.1 copy.44
  1.1 1.1 broadcast_in_dim.106
  2.2 0.0 copy-start
  2.2 0.0 copy-start.1
  2.2 11.6 %all-to-all-start = ((bf16[32,16,1024]{2,0,1:T(8,128)(2,1)}), bf16[32,16,1024]{2,0,1:T(8,128)(2,1)S(1)}, u32[]{:S(2)}, u32[]{:S(2)}) async-start(bf16[32,16,1024]{2,0,1:T(8,128)(2,1)} %bitcast.9), calls=%async_computation | async-start | bytes 2097152 | tf_op jit(solution)/shard_map/all_to_all | solution.py:114
  13.8 0.0 copy-done
  13.8 0.2 and_reduce_fusion
  14.0 0.2 fusion.1
  14.2 0.0 copy-start.2
  14.2 0.1 copy.34
  14.4 0.0 copy-done.1
  14.4 0.1 copy.35
  14.5 0.1 pad.29.clone
  14.6 0.1 fusion.5
  14.7 45.4 %all-gather = bf16[1152,256]{1,0:T(8,128)(2,1)S(1)} all-gather(bf16[144,256]{1,0:T(8,128)(2,1)S(1)} %fusion.5), channel_id=2, replica_groups=mesh['rows'=32,'cols_0'=8,'cols_1'=2] {'cols_0'}, dimensions={0}, use_global_device_ids=true | all-gather | bytes 663552 | tf_op jit(solution)/shard_map/all_gather | solution.py:107
  60.1 1.9 %collective-permute-start = (bf16[8,144,256]{2,1,0:T(8,128)(2,1)S(1)}, bf16[8,144,256]{2,1,0:T(8,128)(2,1)S(1)}, u32[]{:S(2)}, u32[]{:S(2)}) collective-permute-start(bf16[8,144,256]{2,1,0:T(8,128)(2,1)S(1)} %bitcast.68), channel_id=1, source_target_pairs={{0,16},{16,0},{32,48},{48,32},{64,80},{80,64},{96,112},{112,96},{1... | collective-permute-start | bytes 1769480 | tf_op jit(solution)/shard_map/ppermute | solution.py:109
  62.1 0.0 copy-done.2
  62.1 0.1 fusion.10
  62.2 0.1 slice_bitcast_fusion.7
  62.2 0.1 slice_bitcast_fusion.6
  62.3 0.1 slice_bitcast_fusion.5
  62.4 0.1 slice_bitcast_fusion.4
  62.4 1.6 %collective-permute-done = bf16[8,144,256]{2,1,0:T(8,128)(2,1)S(1)} collective-permute-done((bf16[8,144,256]{2,1,0:T(8,128)(2,1)S(1)}, bf16[8,144,256]{2,1,0:T(8,128)(2,1)S(1)}, u32[]{:S(2)}, u32[]{:S(2)}) %collective-permute-start) | collective-permute-done | bytes 589856 | tf_op jit(solution)/shard_map/ppermute | solution.py:109
  64.0 1.3 %maximum_select_fusion.a_ref = bf16[8,144,512]{2,1,0:T(8,128)(2,1)} fusion(bf16[8,144,256]{2,1,0:T(8,128)(2,1)S(1)} %collective-permute-done, bf16[8,144,256]{2,1,0:T(8,128)(2,1)S(1)} %bitcast.69, pred[]{:T(512)S(6)} %eq.71), kind=kLoop, calls=%fused_computation | loop fusion | flops 5308416 | bytes 2359297 | tf_op jit(solution)/shard_map/jit(_where)/select_n | solution.py:110
  65.3 0.0 all-to-all-done
  65.3 1.3 %copy.33 = bf16[512,1024]{0,1:T(8,128)(2,1)} copy(bf16[512,1024]{1,0:T(8,128)(2,1)S(1)} %bitcast.66) | data formatting | bytes 2097152 | tf_op jit(solution)/shard_map/reshape | solution.py:115
  66.7 9.6 %shard_map.46 = f32[8,16,512]{2,1,0:T(8,128)} custom-call(bf16[1024,512]{1,0:T(8,128)(2,1)} %bitcast.67, bf16[8,144,512]{2,1,0:T(8,128)(2,1)} %maximum_select_fusion.a_ref), custom_call_target="tpu_custom_call" | custom-call | tf_op jit(solution)/shard_map/pallas_call | solution.py:46
  76.3 4.7 %all-to-all-start.1 = ((f32[8,16,512]{2,1,0:T(8,128)}), f32[8,16,512]{2,1,0:T(8,128)S(1)}, u32[]{:S(2)}, u32[]{:S(2)}) async-start(f32[8,16,512]{2,1,0:T(8,128)} %shard_map.46), calls=%async_computation.1 | async-start | bytes 524288 | tf_op jit(solution)/shard_map/all_to_all | solution.py:118
  81.0 0.6 fusion.9
  81.6 0.1 maximum_compare_fusion
  81.7 0.1 compare_bitcast_fusion.7
  81.7 11.4 %all-to-all-done.1 = f32[8,16,512]{2,1,0:T(8,128)S(1)} async-done(((f32[8,16,512]{2,1,0:T(8,128)}), f32[8,16,512]{2,1,0:T(8,128)S(1)}, u32[]{:S(2)}, u32[]{:S(2)}) %all-to-all-start.1) | async-done | bytes 262176 | tf_op jit(solution)/shard_map/all_to_all | solution.py:118
  93.2 0.1 copy.37
  93.3 0.1 fusion.8
  93.4 0.1 maximum_select_fusion.12
  93.6 0.1 slice.154
  93.8 0.1 slice.155
  93.9 0.1 slice.156
  94.1 0.0 copy-start.3
  94.1 0.1 slice.157
  94.3 0.4 copy-done.3
  94.7 0.6 slice_select_fusion
  95.3 3.9 %collective-permute-start.1 = (f32[2,512]{0,1:T(8,128)S(1)}, f32[2,512]{0,1:T(8,128)S(1)}, u32[]{:S(2)}, u32[]{:S(2)}) collective-permute-start(f32[2,512]{0,1:T(8,128)S(1)} %slice_select_fusion), channel_id=1, source_target_pairs={{16,0},{32,16},{48,32},{64,48},{80,64},{96,80},{112,96},{128,112},... | collective-permute-start | bytes 12296 | tf_op jit(solution)/shard_map/ppermute | solution.py:85
  99.2 0.1 maximum_select_fusion.6
  99.4 0.1 maximum_select_fusion.5
  99.5 0.1 maximum_select_fusion.4
  99.6 0.1 maximum_select_fusion.3
  99.8 0.1 slice.165
  99.9 0.6 concatenate.102
  100.6 1.9 %collective-permute-start.2 = (f32[2,512]{0,1:T(8,128)S(1)}, f32[2,512]{0,1:T(8,128)S(1)}, u32[]{:S(2)}, u32[]{:S(2)}) collective-permute-start(f32[2,512]{0,1:T(8,128)S(1)} %concatenate.102), channel_id=1, source_target_pairs={{0,16},{16,32},{32,48},{48,64},{64,80},{80,96},{96,112},{112,128},... | collective-permute-start | bytes 12296 | tf_op jit(solution)/shard_map/ppermute | solution.py:84
  102.5 2.2 %collective-permute-done.1 = f32[2,512]{0,1:T(8,128)S(1)} collective-permute-done((f32[2,512]{0,1:T(8,128)S(1)}, f32[2,512]{0,1:T(8,128)S(1)}, u32[]{:S(2)}, u32[]{:S(2)}) %collective-permute-start.1) | collective-permute-done | bytes 4128 | tf_op jit(solution)/shard_map/ppermute | solution.py:85
  104.7 0.3 slice_reduce_fusion.3
  105.0 9.1 %collective-permute-done.2 = f32[2,512]{0,1:T(8,128)S(1)} collective-permute-done((f32[2,512]{0,1:T(8,128)S(1)}, f32[2,512]{0,1:T(8,128)S(1)}, u32[]{:S(2)}, u32[]{:S(2)}) %collective-permute-start.2) | collective-permute-done | bytes 4128 | tf_op jit(solution)/shard_map/ppermute | solution.py:84
  114.1 0.3 slice_reduce_fusion.2
  114.4 1.0 fusion
  (8 shorter events, 0.2 us)
Async XLA Ops:
  2.2 11.6 %copy-start = (s32[512,128]{1,0:T(8,128)S(1)}, s32[512,128]{1,0:T(8,128)}, u32[]{:S(2)}) copy-start(s32[512,128]{1,0:T(8,128)} %param.6) | copy-start | bytes 786436
  2.2 12.1 %copy-start.1 = (bf16[512,128]{1,0:T(8,128)(2,1)S(1)}, bf16[512,128]{1,0:T(8,128)(2,1)}, u32[]{:S(2)}) copy-start(bf16[512,128]{1,0:T(8,128)(2,1)} %param.5) | copy-start | bytes 393220
  2.2 63.1 %all-to-all-start = ((bf16[32,16,1024]{2,0,1:T(8,128)(2,1)}), bf16[32,16,1024]{2,0,1:T(8,128)(2,1)S(1)}, u32[]{:S(2)}, u32[]{:S(2)}) async-start(bf16[32,16,1024]{2,0,1:T(8,128)(2,1)} %bitcast.9), calls=%async_computation | async-start | bytes 2097152 | tf_op jit(solution)/shard_map/all_to_all | solution.py:114
  14.2 47.9 %copy-start.2 = (s32[128]{0:T(128)S(1)}, s32[128]{0:T(128)}, u32[]{:S(2)}) copy-start(s32[128]{0:T(128)} %param.7) | copy-start | bytes 1540
  60.1 3.9 %collective-permute-start = (bf16[8,144,256]{2,1,0:T(8,128)(2,1)S(1)}, bf16[8,144,256]{2,1,0:T(8,128)(2,1)S(1)}, u32[]{:S(2)}, u32[]{:S(2)}) collective-permute-start(bf16[8,144,256]{2,1,0:T(8,128)(2,1)S(1)} %bitcast.68), channel_id=1, source_target_pairs={{0,16},{16,0},{32,48},{48,32},{64,80},{80,64},{96,112},{112,96},{1... | collective-permute-start | bytes 1769480 | tf_op jit(solution)/shard_map/ppermute | solution.py:109
  76.3 16.9 %all-to-all-start.1 = ((f32[8,16,512]{2,1,0:T(8,128)}), f32[8,16,512]{2,1,0:T(8,128)S(1)}, u32[]{:S(2)}, u32[]{:S(2)}) async-start(f32[8,16,512]{2,1,0:T(8,128)} %shard_map.46), calls=%async_computation.1 | async-start | bytes 524288 | tf_op jit(solution)/shard_map/all_to_all | solution.py:118
  94.1 0.7 copy-start.3
  95.3 9.4 %collective-permute-start.1 = (f32[2,512]{0,1:T(8,128)S(1)}, f32[2,512]{0,1:T(8,128)S(1)}, u32[]{:S(2)}, u32[]{:S(2)}) collective-permute-start(f32[2,512]{0,1:T(8,128)S(1)} %slice_select_fusion), channel_id=1, source_target_pairs={{16,0},{32,16},{48,32},{64,48},{80,64},{96,80},{112,96},{128,112},... | collective-permute-start | bytes 12296 | tf_op jit(solution)/shard_map/ppermute | solution.py:85
  100.6 13.5 %collective-permute-start.2 = (f32[2,512]{0,1:T(8,128)S(1)}, f32[2,512]{0,1:T(8,128)S(1)}, u32[]{:S(2)}, u32[]{:S(2)}) collective-permute-start(f32[2,512]{0,1:T(8,128)S(1)} %concatenate.102), channel_id=1, source_target_pairs={{0,16},{16,32},{32,48},{48,64},{64,80},{80,96},{96,112},{112,128},... | collective-permute-start | bytes 12296 | tf_op jit(solution)/shard_map/ppermute | solution.py:84

commit v7 on v6

--- a/solution.py
+++ b/solution.py
@@ -104,7 +104,8 @@
     core = lax.rem(lax.axis_index("rows"), 2)
     half = scen // 2
     mine = lax.dynamic_slice_in_dim(coded, core * half, half, axis=1)
-    mine = lax.all_gather(mine, SPLIT, axis=0, tiled=False)
+    mine = jnp.broadcast_to(mine[None], (parts,) + mine.shape)
+    mine = lax.all_to_all(mine, SPLIT, 0, 0, tiled=True)
     count_rows = lax.axis_size("rows")
     theirs = lax.ppermute(mine, "rows", [(i, i ^ 1) for i in range(count_rows)])
     coded = jnp.where(core == 0, jnp.concatenate([mine, theirs], axis=2), jnp.concatenate([theirs, mine], axis=2))

time: 116 us -> 114 us (0.983)
  blocking collectives: 45.4 us -> 0 us
  waiting for transfers between devices: 24.3 us -> 65.3 us
  other arithmetic: 4.41 us -> 6.3 us
  starting transfers between devices: 24 us -> 25.3 us
    all_gather x1 -> x0, blocking collectives: 45.4 us -> none  [local(): mine = lax.all_gather(mine, SPLIT, axis=0, tiled=False)]
    all_to_all x1, waiting for transfers between devices: 0.01 us -> 22.7 us  [local(): pieces = lax.all_to_all(pieces, COLS, 1, 0, tiled=True)]
    all_to_all x0 -> x1, waiting for transfers between devices: none -> 18.9 us  [local(): mine = lax.all_to_all(mine, SPLIT, 0, 0, tiled=True)]
    all_to_all x0 -> x1, starting transfers between devices: none -> 10.3 us  [local(): mine = lax.all_to_all(mine, SPLIT, 0, 0, tiled=True)]
    all_to_all x1, starting transfers between devices: 11.6 us -> 3.78 us  [local(): pieces = lax.all_to_all(pieces, COLS, 1, 0, tiled=True)]
    all_to_all x1, starting transfers between devices: 4.74 us -> 3.41 us  [local(): maxima = lax.all_to_all(maxima, SPLIT, 0, 0, tiled=True)]
    ppermute x1, waiting for transfers between devices: 9.09 us -> 7.79 us  [point_peaks(): lax.ppermute(to_right, 'rows', [(i, i + 1) for i in range(count - 1)])]
    ppermute x1, waiting for transfers between devices: 2.19 us -> 3.49 us  [point_peaks(): lax.ppermute(to_left, 'rows', [(i + 1, i) for i in range(count - 1)])]
  transfers between devices with their start and end apart: 5 -> 6, of which waited for: 4 -> 6; matrix products, arithmetic and copies ran while one was open for 4% -> 4% of each run, Pallas kernels for 0% -> 0%
where the time goes in v7:
time: 114 us
  waiting for transfers between devices  65.3 us (57%)
  starting transfers between devices  25.3 us (22%)
  Pallas kernels  9.6 us (8%)
  local copies, waits for them, and re-layouts  6.98 us (6%)
  other arithmetic  6.3 us (6%)
    all_to_all x1, waiting for transfers between devices, local(): pieces = lax.all_to_all(pieces, COLS, 1, 0, tiled=True)  22.7 us
    all_to_all x1, waiting for transfers between devices, local(): mine = lax.all_to_all(mine, SPLIT, 0, 0, tiled=True)  18.9 us
    all_to_all x1, waiting for transfers between devices, local(): maxima = lax.all_to_all(maxima, SPLIT, 0, 0, tiled=True)  10.7 us
    all_to_all x1, starting transfers between devices, local(): mine = lax.all_to_all(mine, SPLIT, 0, 0, tiled=True)  10.3 us
    pallas_call x1, Pallas kernels, wave_maxima(): pl.pallas_call(wave_kernel, grid=(parts,), in_specs=[pl.BlockSpec((rows,...  9.6 us
    ppermute x1, waiting for transfers between devices, point_peaks(): lax.ppermute(to_right, 'rows', [(i, i + 1) for i in range(count - 1)])  7.79 us
    ppermute x1, starting transfers between devices, point_peaks(): lax.ppermute(to_left, 'rows', [(i + 1, i) for i in range(count - 1)])  3.91 us
    all_to_all x1, starting transfers between devices, local(): pieces = lax.all_to_all(pieces, COLS, 1, 0, tiled=True)  3.78 us
  transfers between devices with their start and end apart: 6, of which 6 were waited for; matrix products, arithmetic and copies ran while one was open for 4% of the time, Pallas kernels for 0%

profile of v7, /device:TPU:6, one launch (start us, length us, event | category | flops | bytes accessed | tf_op | source)
XLA Modules:
  0.0 113.7 jit_solution(14971963380292053454)
XLA Ops:
  0.0 1.2 %fusion.1 = (bf16[1,512]{0,1:T(8,128)(2,1)S(1)}, bf16[1,512]{0,1:T(8,128)(2,1)S(1)}) fusion(s32[512,128]{1,0:T(8,128)} %param.6), kind=kLoop, calls=%fused_computation.17 | loop fusion | flops 7680 | bytes 4096 | tf_op jit(solution)/shard_map/convert.1
  1.2 1.1 fusion.6
  2.3 0.1 pad.29.clone
  2.3 0.0 copy-start
  2.3 0.1 fusion.9
  2.4 0.1 copy.15
  2.5 0.9 broadcast_in_dim.115
  3.4 10.3 %all-to-all-start.1 = ((bf16[8,144,256]{2,1,0:T(8,128)(2,1)}), bf16[8,144,256]{2,1,0:T(8,128)(2,1)S(1)}, u32[]{:S(2)}, u32[]{:S(2)}) async-start(bf16[8,144,256]{2,1,0:T(8,128)(2,1)} %broadcast_in_dim.115), calls=%async_computation.1 | async-start | bytes 1179648 | tf_op jit(solution)/shard_map/all_to_all | solution.py:108
  13.7 0.0 copy-done
  13.8 18.9 %all-to-all-done.1 = bf16[8,144,256]{2,1,0:T(8,128)(2,1)S(1)} async-done(((bf16[8,144,256]{2,1,0:T(8,128)(2,1)}), bf16[8,144,256]{2,1,0:T(8,128)(2,1)S(1)}, u32[]{:S(2)}, u32[]{:S(2)}) %all-to-all-start.1) | async-done | bytes 589856 | tf_op jit(solution)/shard_map/all_to_all | solution.py:108
  32.6 1.1 broadcast_in_dim.112
  33.7 0.0 copy-start.1
  33.7 3.8 %all-to-all-start = ((bf16[32,16,1024]{2,0,1:T(8,128)(2,1)}), bf16[32,16,1024]{2,0,1:T(8,128)(2,1)S(1)}, u32[]{:S(2)}, u32[]{:S(2)}) async-start(bf16[32,16,1024]{2,0,1:T(8,128)(2,1)} %bitcast.9), calls=%async_computation | async-start | bytes 2097152 | tf_op jit(solution)/shard_map/all_to_all | solution.py:115
  37.5 0.0 copy-done.1
  37.5 0.1 fusion.12
  37.6 0.1 slice_bitcast_fusion.7
  37.7 1.9 %collective-permute-start = (bf16[8,144,256]{2,1,0:T(8,128)(2,1)S(1)}, bf16[8,144,256]{2,1,0:T(8,128)(2,1)S(1)}, u32[]{:S(2)}, u32[]{:S(2)}) collective-permute-start(bf16[8,144,256]{2,1,0:T(8,128)(2,1)S(1)} %all-to-all-done.1), channel_id=1, source_target_pairs={{0,16},{16,0},{32,48},{48,32},{64,80},{80,64},{96,112},{112,96},{1... | collective-permute-start | bytes 1769480 | tf_op jit(solution)/shard_map/ppermute | solution.py:110
  39.6 0.1 slice_bitcast_fusion.6
  39.7 0.1 slice_bitcast_fusion.5
  39.8 0.1 slice_bitcast_fusion.4
  39.8 1.7 %collective-permute-done = bf16[8,144,256]{2,1,0:T(8,128)(2,1)S(1)} collective-permute-done((bf16[8,144,256]{2,1,0:T(8,128)(2,1)S(1)}, bf16[8,144,256]{2,1,0:T(8,128)(2,1)S(1)}, u32[]{:S(2)}, u32[]{:S(2)}) %collective-permute-start) | collective-permute-done | bytes 589856 | tf_op jit(solution)/shard_map/ppermute | solution.py:110
  41.6 1.3 %maximum_select_fusion.a_ref = bf16[8,144,512]{2,1,0:T(8,128)(2,1)} fusion(bf16[8,144,256]{2,1,0:T(8,128)(2,1)S(1)} %collective-permute-done, bf16[8,144,256]{2,1,0:T(8,128)(2,1)S(1)} %all-to-all-done.1, pred[]{:T(512)S(6)} %eq.71), kind=kLoop, calls=%fused_computation | loop fusion | flops 5308416 | bytes 2359297 | tf_op jit(solution)/shard_map/jit(_where)/select_n | solution.py:111
  42.9 22.7 %all-to-all-done = bf16[32,16,1024]{2,0,1:T(8,128)(2,1)S(1)} async-done(((bf16[32,16,1024]{2,0,1:T(8,128)(2,1)}), bf16[32,16,1024]{2,0,1:T(8,128)(2,1)S(1)}, u32[]{:S(2)}, u32[]{:S(2)}) %all-to-all-start) | async-done | bytes 1048608 | tf_op jit(solution)/shard_map/all_to_all | solution.py:115
  65.5 1.3 %copy.14 = bf16[512,1024]{0,1:T(8,128)(2,1)} copy(bf16[512,1024]{1,0:T(8,128)(2,1)S(1)} %bitcast.83) | data formatting | bytes 2097152 | tf_op jit(solution)/shard_map/reshape | solution.py:116
  66.9 9.6 %shard_map.46 = f32[8,16,512]{2,1,0:T(8,128)} custom-call(bf16[1024,512]{1,0:T(8,128)(2,1)} %bitcast.84, bf16[8,144,512]{2,1,0:T(8,128)(2,1)} %maximum_select_fusion.a_ref), custom_call_target="tpu_custom_call" | custom-call | tf_op jit(solution)/shard_map/pallas_call | solution.py:46
  76.5 3.4 %all-to-all-start.2 = ((f32[8,16,512]{2,1,0:T(8,128)}), f32[8,16,512]{2,1,0:T(8,128)S(1)}, u32[]{:S(2)}, u32[]{:S(2)}) async-start(f32[8,16,512]{2,1,0:T(8,128)} %shard_map.46), calls=%async_computation.2 | async-start | bytes 524288 | tf_op jit(solution)/shard_map/all_to_all | solution.py:119
  79.9 0.6 fusion.11
  80.5 0.1 maximum_compare_fusion
  80.6 0.1 compare_bitcast_fusion.7
  80.6 10.7 %all-to-all-done.2 = f32[8,16,512]{2,1,0:T(8,128)S(1)} async-done(((f32[8,16,512]{2,1,0:T(8,128)}), f32[8,16,512]{2,1,0:T(8,128)S(1)}, u32[]{:S(2)}, u32[]{:S(2)}) %all-to-all-start.2) | async-done | bytes 262176 | tf_op jit(solution)/shard_map/all_to_all | solution.py:119
  91.4 0.1 copy.17
  91.5 0.1 fusion.10
  91.6 0.1 maximum_select_fusion.12
  91.8 0.1 slice.154
  92.0 0.1 slice.155
  92.1 0.1 slice.156
  92.3 0.0 copy-start.2
  92.3 0.1 slice.157
  92.5 0.4 copy-done.2
  92.9 0.6 slice_select_fusion
  93.6 3.9 %collective-permute-start.1 = (f32[2,512]{0,1:T(8,128)S(1)}, f32[2,512]{0,1:T(8,128)S(1)}, u32[]{:S(2)}, u32[]{:S(2)}) collective-permute-start(f32[2,512]{0,1:T(8,128)S(1)} %slice_select_fusion), channel_id=1, source_target_pairs={{16,0},{32,16},{48,32},{64,48},{80,64},{96,80},{112,96},{128,112},... | collective-permute-start | bytes 12296 | tf_op jit(solution)/shard_map/ppermute | solution.py:85
  97.5 0.1 maximum_select_fusion.6
  97.7 0.1 maximum_select_fusion.5
  97.8 0.1 maximum_select_fusion.4
  97.9 0.1 maximum_select_fusion.3
  98.1 0.1 slice.165
  98.2 0.6 concatenate.102
  98.8 1.9 %collective-permute-start.2 = (f32[2,512]{0,1:T(8,128)S(1)}, f32[2,512]{0,1:T(8,128)S(1)}, u32[]{:S(2)}, u32[]{:S(2)}) collective-permute-start(f32[2,512]{0,1:T(8,128)S(1)} %concatenate.102), channel_id=1, source_target_pairs={{0,16},{16,32},{32,48},{48,64},{64,80},{80,96},{96,112},{112,128},... | collective-permute-start | bytes 12296 | tf_op jit(solution)/shard_map/ppermute | solution.py:84
  100.7 3.5 %collective-permute-done.1 = f32[2,512]{0,1:T(8,128)S(1)} collective-permute-done((f32[2,512]{0,1:T(8,128)S(1)}, f32[2,512]{0,1:T(8,128)S(1)}, u32[]{:S(2)}, u32[]{:S(2)}) %collective-permute-start.1) | collective-permute-done | bytes 4128 | tf_op jit(solution)/shard_map/ppermute | solution.py:85
  104.2 0.3 slice_reduce_fusion.3
  104.5 7.8 %collective-permute-done.2 = f32[2,512]{0,1:T(8,128)S(1)} collective-permute-done((f32[2,512]{0,1:T(8,128)S(1)}, f32[2,512]{0,1:T(8,128)S(1)}, u32[]{:S(2)}, u32[]{:S(2)}) %collective-permute-start.2) | collective-permute-done | bytes 4128 | tf_op jit(solution)/shard_map/ppermute | solution.py:84
  112.3 0.3 slice_reduce_fusion.2
  112.6 1.0 fusion.2
  (7 shorter events, 0.2 us)
Async XLA Ops:
  2.3 11.4 %copy-start = (bf16[32,8192]{1,0:T(8,128)(2,1)S(1)}, bf16[32,8192]{1,0:T(8,128)(2,1)}, u32[]{:S(2)}) copy-start(bf16[32,8192]{1,0:T(8,128)(2,1)} %param.4) | copy-start | bytes 1572868
  3.4 29.2 %all-to-all-start.1 = ((bf16[8,144,256]{2,1,0:T(8,128)(2,1)}), bf16[8,144,256]{2,1,0:T(8,128)(2,1)S(1)}, u32[]{:S(2)}, u32[]{:S(2)}) async-start(bf16[8,144,256]{2,1,0:T(8,128)(2,1)} %broadcast_in_dim.115), calls=%async_computation.1 | async-start | bytes 1179648 | tf_op jit(solution)/shard_map/all_to_all | solution.py:108
  33.7 3.8 %copy-start.1 = (s32[128]{0:T(128)S(1)}, s32[128]{0:T(128)}, u32[]{:S(2)}) copy-start(s32[128]{0:T(128)} %param.7) | copy-start | bytes 1540
  33.7 31.8 %all-to-all-start = ((bf16[32,16,1024]{2,0,1:T(8,128)(2,1)}), bf16[32,16,1024]{2,0,1:T(8,128)(2,1)S(1)}, u32[]{:S(2)}, u32[]{:S(2)}) async-start(bf16[32,16,1024]{2,0,1:T(8,128)(2,1)} %bitcast.9), calls=%async_computation | async-start | bytes 2097152 | tf_op jit(solution)/shard_map/all_to_all | solution.py:115
  37.7 3.9 %collective-permute-start = (bf16[8,144,256]{2,1,0:T(8,128)(2,1)S(1)}, bf16[8,144,256]{2,1,0:T(8,128)(2,1)S(1)}, u32[]{:S(2)}, u32[]{:S(2)}) collective-permute-start(bf16[8,144,256]{2,1,0:T(8,128)(2,1)S(1)} %all-to-all-done.1), channel_id=1, source_target_pairs={{0,16},{16,0},{32,48},{48,32},{64,80},{80,64},{96,112},{112,96},{1... | collective-permute-start | bytes 1769480 | tf_op jit(solution)/shard_map/ppermute | solution.py:110
  76.5 14.9 %all-to-all-start.2 = ((f32[8,16,512]{2,1,0:T(8,128)}), f32[8,16,512]{2,1,0:T(8,128)S(1)}, u32[]{:S(2)}, u32[]{:S(2)}) async-start(f32[8,16,512]{2,1,0:T(8,128)} %shard_map.46), calls=%async_computation.2 | async-start | bytes 524288 | tf_op jit(solution)/shard_map/all_to_all | solution.py:119
  92.3 0.7 copy-start.2
  93.6 10.6 %collective-permute-start.1 = (f32[2,512]{0,1:T(8,128)S(1)}, f32[2,512]{0,1:T(8,128)S(1)}, u32[]{:S(2)}, u32[]{:S(2)}) collective-permute-start(f32[2,512]{0,1:T(8,128)S(1)} %slice_select_fusion), channel_id=1, source_target_pairs={{16,0},{32,16},{48,32},{64,48},{80,64},{96,80},{112,96},{128,112},... | collective-permute-start | bytes 12296 | tf_op jit(solution)/shard_map/ppermute | solution.py:85
  98.8 13.5 %collective-permute-start.2 = (f32[2,512]{0,1:T(8,128)S(1)}, f32[2,512]{0,1:T(8,128)S(1)}, u32[]{:S(2)}, u32[]{:S(2)}) collective-permute-start(f32[2,512]{0,1:T(8,128)S(1)} %concatenate.102), channel_id=1, source_target_pairs={{0,16},{16,32},{32,48},{48,64},{64,80},{80,96},{96,112},{112,128},... | collective-permute-start | bytes 12296 | tf_op jit(solution)/shard_map/ppermute | solution.py:84

commit v8 on v6

--- a/solution.py
+++ b/solution.py
@@ -102,17 +102,26 @@
     code = jnp.stack([starts // CODE, starts % CODE]).astype(jnp.bfloat16)
     coded = jnp.concatenate([values.T, code, jnp.zeros((14, scen), jnp.bfloat16)], axis=0)
     core = lax.rem(lax.axis_index("rows"), 2)
+    side = lax.axis_index(SHARE)
     half = scen // 2
     mine = lax.dynamic_slice_in_dim(coded, core * half, half, axis=1)
-    mine = lax.all_gather(mine, SPLIT, axis=0, tiled=False)
+    height = mine.shape[0]
+    outgoing = jnp.concatenate(
+        [
+            greens.reshape(own_sources, parts, block).transpose(1, 0, 2),
+            jnp.broadcast_to(mine.reshape(1, -1, block), (parts, height * half // block, block)),
+        ],
+        axis=1,
+    )
+    incoming = lax.all_to_all(outgoing, SPLIT, 0, 0, tiled=True)
+    near = incoming[:, :own_sources]
+    mine = incoming[:, own_sources:].reshape(parts, height, half)
     count_rows = lax.axis_size("rows")
+    far = lax.ppermute(near, SHARE, [(i, (i + 1) % shares) for i in range(shares)])
     theirs = lax.ppermute(mine, "rows", [(i, i ^ 1) for i in range(count_rows)])
     coded = jnp.where(core == 0, jnp.concatenate([mine, theirs], axis=2), jnp.concatenate([theirs, mine], axis=2))
-
-    pieces = greens.reshape(own_sources, parts, 1, block)
-    pieces = jnp.broadcast_to(pieces, (own_sources, parts, shares, block)).reshape(own_sources, parts * shares, block)
-    pieces = lax.all_to_all(pieces, COLS, 1, 0, tiled=True)
-    panel_t = pieces.reshape(width, block).T
+    panel = jnp.where(side == 0, jnp.stack([near, far], axis=1), jnp.stack([far, near], axis=1))
+    panel_t = panel.reshape(width, block).T
 
     maxima = wave_maxima(panel_t, coded)
     maxima = lax.all_to_all(maxima, SPLIT, 0, 0, tiled=True)

time: 116 us -> 112 us (0.966)
  blocking collectives: 45.4 us -> 0 us
  waiting for transfers between devices: 24.3 us -> 61.4 us
  other arithmetic: 4.41 us -> 7.61 us
    all_gather x1 -> x0, blocking collectives: 45.4 us -> none  [local(): mine = lax.all_gather(mine, SPLIT, axis=0, tiled=False)]
    all_to_all x1, waiting for transfers between devices: 0.01 us -> 31.4 us  [local(): incoming = lax.all_to_all(outgoing, SPLIT, 0, 0, tiled=True)]
    ppermute x0 -> x1, waiting for transfers between devices: none -> 9.89 us  [local(): lax.ppermute(near, SHARE, [(i, (i + 1) % shares) for i in range(shares)])]
    ppermute x0 -> x1, starting transfers between devices: none -> 3.47 us  [local(): lax.ppermute(near, SHARE, [(i, (i + 1) % shares) for i in range(shares)])]
    ppermute x1, waiting for transfers between devices: 9.09 us -> 6.04 us  [point_peaks(): lax.ppermute(to_right, 'rows', [(i, i + 1) for i in range(count - 1)])]
    broadcast_in_dim x2, local copies, waits for them, and re-layouts: 2.22 us -> 0.12 us  [local(): jnp.broadcast_to(mine.reshape(1, -1, block), (parts, height * half // blo...]
    ppermute x1, waiting for transfers between devices: 1.58 us -> 0.01 us  [local(): theirs = lax.ppermute(mine, 'rows', [(i, i ^ 1) for i in range(count_rows)])]
    select_n x0 -> x1, local copies, waits for them, and re-layouts: none -> 1.35 us  [local(): jnp.where(side == 0, jnp.stack([near, far], axis=1), jnp.stack([far, near...]
  transfers between devices with their start and end apart: 5 -> 6, of which waited for: 4 -> 5; matrix products, arithmetic and copies ran while one was open for 4% -> 4% of each run, Pallas kernels for 0% -> 0%
where the time goes in v8:
time: 112 us; the launch traced here: 111 us
  waiting for transfers between devices  61.4 us (55%)
  starting transfers between devices  25.1 us (22%)
  Pallas kernels  9.6 us (9%)
  other arithmetic  7.61 us (7%)
  local copies, waits for them, and re-layouts  7.04 us (6%)
    all_to_all x1, waiting for transfers between devices, local(): incoming = lax.all_to_all(outgoing, SPLIT, 0, 0, tiled=True)  31.4 us
    all_to_all x1, waiting for transfers between devices, local(): maxima = lax.all_to_all(maxima, SPLIT, 0, 0, tiled=True)  10.6 us
    all_to_all x1, starting transfers between devices, local(): incoming = lax.all_to_all(outgoing, SPLIT, 0, 0, tiled=True)  10.4 us
    ppermute x1, waiting for transfers between devices, local(): lax.ppermute(near, SHARE, [(i, (i + 1) % shares) for i in range(shares)])  9.89 us
    pallas_call x1, Pallas kernels, wave_maxima(): pl.pallas_call(wave_kernel, grid=(parts,), in_specs=[pl.BlockSpec((rows,...  9.6 us
    ppermute x1, waiting for transfers between devices, point_peaks(): lax.ppermute(to_right, 'rows', [(i, i + 1) for i in range(count - 1)])  6.04 us
    ppermute x1, starting transfers between devices, point_peaks(): lax.ppermute(to_left, 'rows', [(i + 1, i) for i in range(count - 1)])  3.9 us
    ppermute x1, starting transfers between devices, local(): lax.ppermute(near, SHARE, [(i, (i + 1) % shares) for i in range(shares)])  3.47 us
  transfers between devices with their start and end apart: 6, of which 5 were waited for; matrix products, arithmetic and copies ran while one was open for 4% of the time, Pallas kernels for 0%

profile of v8, /device:TPU:6, one launch (start us, length us, event | category | flops | bytes accessed | tf_op | source)
XLA Modules:
  0.0 111.0 jit_solution(1386292196581251948)
XLA Ops:
  0.0 0.0 copy-start
  0.0 1.2 %fusion.1 = (bf16[1,512]{0,1:T(8,128)(2,1)S(1)}, bf16[1,512]{0,1:T(8,128)(2,1)S(1)}) fusion(s32[512,128]{1,0:T(8,128)} %param.6), kind=kLoop, calls=%fused_computation.18 | loop fusion | flops 7680 | bytes 4096 | tf_op jit(solution)/shard_map/convert.1
  1.2 1.1 fusion.6
  2.3 0.1 pad.35.clone
  2.4 0.1 fusion.9
  2.5 0.1 copy.21
  2.6 0.1 broadcast_in_dim.107
  2.7 0.0 copy-done
  2.7 0.3 copy.30
  3.0 0.3 copy.22
  3.3 0.1 broadcast_in_dim.108
  3.4 1.2 %pad_maximum_fusion = bf16[8,68,1024]{2,1,0:T(8,128)(2,1)} fusion(bf16[8,36,1024]{2,1,0:T(8,128)(2,1)S(1)} %broadcast_in_dim.108, bf16[8,32,1024]{2,1,0:T(8,128)(2,1)S(1)} %copy.22), kind=kLoop, calls=%fused_computation | loop fusion | flops 2228224 | bytes 2228224 | tf_op jit(solution)/shard_map/concatenate | solution.py:109
  4.5 0.0 copy-start.1
  4.5 10.4 %all-to-all-start = ((bf16[8,68,1024]{2,1,0:T(8,128)(2,1)}), bf16[8,68,1024]{2,1,0:T(8,128)(2,1)S(1)}, u32[]{:S(2)}, u32[]{:S(2)}) async-start(bf16[8,68,1024]{2,1,0:T(8,128)(2,1)} %pad_maximum_fusion), calls=%async_computation | async-start | bytes 2359296 | tf_op jit(solution)/shard_map/all_to_all | solution.py:116
  15.0 0.0 copy-done.1
  15.0 0.1 fusion.12
  15.0 0.1 slice_bitcast_fusion.7
  15.1 31.4 %all-to-all-done = bf16[8,68,1024]{2,1,0:T(8,128)(2,1)S(1)} async-done(((bf16[8,68,1024]{2,1,0:T(8,128)(2,1)}), bf16[8,68,1024]{2,1,0:T(8,128)(2,1)S(1)}, u32[]{:S(2)}, u32[]{:S(2)}) %all-to-all-start) | async-done | bytes 1114144 | tf_op jit(solution)/shard_map/all_to_all | solution.py:116
  46.5 0.9 slice_bitcast_fusion.8
  47.5 3.5 %collective-permute-start = (bf16[8,32,1024]{2,1,0:T(8,128)(2,1)}, bf16[8,32,1024]{2,1,0:T(8,128)(2,1)S(1)}, u32[]{:S(2)}, u32[]{:S(2)}) collective-permute-start(bf16[8,32,1024]{2,1,0:T(8,128)(2,1)} %get-tuple-element.10), channel_id=1, source_target_pairs={{0,1},{1,0},{2,3},{3,2},{4,5},{5,4},{6,7},{7,6},{8,9},{9,8},{10,11... | collective-permute-start | bytes 1572872 | tf_op jit(solution)/shard_map/ppermute | solution.py:120
  51.0 0.4 reshape.107
  51.4 1.9 %collective-permute-start.1 = (bf16[8,144,256]{2,1,0:T(8,128)(2,1)S(1)}, bf16[8,144,256]{2,1,0:T(8,128)(2,1)S(1)}, u32[]{:S(2)}, u32[]{:S(2)}) collective-permute-start(bf16[8,144,256]{2,1,0:T(8,128)(2,1)S(1)} %reshape.107), channel_id=1, source_target_pairs={{0,16},{16,0},{32,48},{48,32},{64,80},{80,64},{96,112},{112,96},{1... | collective-permute-start | bytes 1769480 | tf_op jit(solution)/shard_map/ppermute | solution.py:121
  53.3 0.1 slice_bitcast_fusion.4
  53.4 0.1 slice_bitcast_fusion.5
  53.4 0.1 slice_bitcast_fusion.6
  53.5 9.9 %collective-permute-done = bf16[8,32,1024]{2,1,0:T(8,128)(2,1)S(1)} collective-permute-done((bf16[8,32,1024]{2,1,0:T(8,128)(2,1)}, bf16[8,32,1024]{2,1,0:T(8,128)(2,1)S(1)}, u32[]{:S(2)}, u32[]{:S(2)}) %collective-permute-start) | collective-permute-done | bytes 524320 | tf_op jit(solution)/shard_map/ppermute | solution.py:120
  63.4 0.1 maximum_select_fusion.1
  63.5 1.4 %copy.23 = bf16[512,1024]{0,1:T(8,128)(2,1)} copy(bf16[512,1024]{1,0:T(8,128)(2,1)S(1)} %bitcast.81) | data formatting | bytes 2097152 | tf_op jit(solution)/shard_map/jit(_where)/select_n | solution.py:123
  64.9 0.0 collective-permute-done.1
  64.9 1.3 %maximum_select_fusion.a_ref = bf16[8,144,512]{2,1,0:T(8,128)(2,1)} fusion(bf16[8,144,256]{2,1,0:T(8,128)(2,1)S(1)} %collective-permute-done.1, bf16[8,144,256]{2,1,0:T(8,128)(2,1)S(1)} %reshape.107, pred[]{:T(512)S(6)} %eq.75), kind=kLoop, calls=%fused_computation.1 | loop fusion | flops 5308416 | bytes 2359297 | tf_op jit(solution)/shard_map/jit(_where)/select_n | solution.py:122
  66.2 9.6 %shard_map.46 = f32[8,16,512]{2,1,0:T(8,128)} custom-call(bf16[1024,512]{1,0:T(8,128)(2,1)} %bitcast.82, bf16[8,144,512]{2,1,0:T(8,128)(2,1)} %maximum_select_fusion.a_ref), custom_call_target="tpu_custom_call" | custom-call | tf_op jit(solution)/shard_map/pallas_call | solution.py:46
  75.8 3.4 %all-to-all-start.1 = ((f32[8,16,512]{2,1,0:T(8,128)}), f32[8,16,512]{2,1,0:T(8,128)S(1)}, u32[]{:S(2)}, u32[]{:S(2)}) async-start(f32[8,16,512]{2,1,0:T(8,128)} %shard_map.46), calls=%async_computation.1 | async-start | bytes 524288 | tf_op jit(solution)/shard_map/all_to_all | solution.py:127
  79.2 0.6 fusion.11
  79.8 0.1 maximum_compare_fusion
  79.8 0.1 compare_bitcast_fusion.7
  79.9 10.6 %all-to-all-done.1 = f32[8,16,512]{2,1,0:T(8,128)S(1)} async-done(((f32[8,16,512]{2,1,0:T(8,128)}), f32[8,16,512]{2,1,0:T(8,128)S(1)}, u32[]{:S(2)}, u32[]{:S(2)}) %all-to-all-start.1) | async-done | bytes 262176 | tf_op jit(solution)/shard_map/all_to_all | solution.py:127
  90.6 0.1 copy.25
  90.7 0.1 fusion.10
  90.8 0.1 maximum_select_fusion.13
  91.0 0.1 slice.164
  91.2 0.1 slice.165
  91.3 0.1 slice.166
  91.5 0.0 copy-start.2
  91.5 0.1 slice.167
  91.7 0.4 copy-done.2
  92.1 0.6 slice_select_fusion
  92.8 3.9 %collective-permute-start.2 = (f32[2,512]{0,1:T(8,128)S(1)}, f32[2,512]{0,1:T(8,128)S(1)}, u32[]{:S(2)}, u32[]{:S(2)}) collective-permute-start(f32[2,512]{0,1:T(8,128)S(1)} %slice_select_fusion), channel_id=1, source_target_pairs={{16,0},{32,16},{48,32},{64,48},{80,64},{96,80},{112,96},{128,112},... | collective-permute-start | bytes 12296 | tf_op jit(solution)/shard_map/ppermute | solution.py:85
  96.7 0.1 maximum_select_fusion.7
  96.8 0.1 maximum_select_fusion.6
  97.0 0.1 maximum_select_fusion.5
  97.1 0.1 maximum_select_fusion.4
  97.3 0.1 slice.175
  97.4 0.6 concatenate.106
  98.0 1.9 %collective-permute-start.3 = (f32[2,512]{0,1:T(8,128)S(1)}, f32[2,512]{0,1:T(8,128)S(1)}, u32[]{:S(2)}, u32[]{:S(2)}) collective-permute-start(f32[2,512]{0,1:T(8,128)S(1)} %concatenate.106), channel_id=1, source_target_pairs={{0,16},{16,32},{32,48},{48,64},{64,80},{80,96},{96,112},{112,128},... | collective-permute-start | bytes 12296 | tf_op jit(solution)/shard_map/ppermute | solution.py:84
  99.9 3.4 %collective-permute-done.2 = f32[2,512]{0,1:T(8,128)S(1)} collective-permute-done((f32[2,512]{0,1:T(8,128)S(1)}, f32[2,512]{0,1:T(8,128)S(1)}, u32[]{:S(2)}, u32[]{:S(2)}) %collective-permute-start.2) | collective-permute-done | bytes 4128 | tf_op jit(solution)/shard_map/ppermute | solution.py:85
  103.3 0.3 slice_reduce_fusion.3
  103.6 6.0 %collective-permute-done.3 = f32[2,512]{0,1:T(8,128)S(1)} collective-permute-done((f32[2,512]{0,1:T(8,128)S(1)}, f32[2,512]{0,1:T(8,128)S(1)}, u32[]{:S(2)}, u32[]{:S(2)}) %collective-permute-start.3) | collective-permute-done | bytes 4128 | tf_op jit(solution)/shard_map/ppermute | solution.py:84
  109.7 0.3 slice_reduce_fusion.2
  110.0 1.0 fusion.2
  (7 shorter events, 0.2 us)
Async XLA Ops:
  0.0 2.7 %copy-start = (bf16[32,8192]{1,0:T(8,128)(2,1)S(1)}, bf16[32,8192]{1,0:T(8,128)(2,1)}, u32[]{:S(2)}) copy-start(bf16[32,8192]{1,0:T(8,128)(2,1)} %param.4) | copy-start | bytes 1572868
  4.5 10.5 %copy-start.1 = (s32[128]{0:T(128)S(1)}, s32[128]{0:T(128)}, u32[]{:S(2)}) copy-start(s32[128]{0:T(128)} %param.7) | copy-start | bytes 1540
  4.5 42.0 %all-to-all-start = ((bf16[8,68,1024]{2,1,0:T(8,128)(2,1)}), bf16[8,68,1024]{2,1,0:T(8,128)(2,1)S(1)}, u32[]{:S(2)}, u32[]{:S(2)}) async-start(bf16[8,68,1024]{2,1,0:T(8,128)(2,1)} %pad_maximum_fusion), calls=%async_computation | async-start | bytes 2359296 | tf_op jit(solution)/shard_map/all_to_all | solution.py:116
  47.5 15.9 %collective-permute-start = (bf16[8,32,1024]{2,1,0:T(8,128)(2,1)}, bf16[8,32,1024]{2,1,0:T(8,128)(2,1)S(1)}, u32[]{:S(2)}, u32[]{:S(2)}) collective-permute-start(bf16[8,32,1024]{2,1,0:T(8,128)(2,1)} %get-tuple-element.10), channel_id=1, source_target_pairs={{0,1},{1,0},{2,3},{3,2},{4,5},{5,4},{6,7},{7,6},{8,9},{9,8},{10,11... | collective-permute-start | bytes 1572872 | tf_op jit(solution)/shard_map/ppermute | solution.py:120
  51.4 13.5 %collective-permute-start.1 = (bf16[8,144,256]{2,1,0:T(8,128)(2,1)S(1)}, bf16[8,144,256]{2,1,0:T(8,128)(2,1)S(1)}, u32[]{:S(2)}, u32[]{:S(2)}) collective-permute-start(bf16[8,144,256]{2,1,0:T(8,128)(2,1)S(1)} %reshape.107), channel_id=1, source_target_pairs={{0,16},{16,0},{32,48},{48,32},{64,80},{80,64},{96,112},{112,96},{1... | collective-permute-start | bytes 1769480 | tf_op jit(solution)/shard_map/ppermute | solution.py:121
  75.8 14.8 %all-to-all-start.1 = ((f32[8,16,512]{2,1,0:T(8,128)}), f32[8,16,512]{2,1,0:T(8,128)S(1)}, u32[]{:S(2)}, u32[]{:S(2)}) async-start(f32[8,16,512]{2,1,0:T(8,128)} %shard_map.46), calls=%async_computation.1 | async-start | bytes 524288 | tf_op jit(solution)/shard_map/all_to_all | solution.py:127
  91.5 0.7 copy-start.2
  92.8 10.5 %collective-permute-start.2 = (f32[2,512]{0,1:T(8,128)S(1)}, f32[2,512]{0,1:T(8,128)S(1)}, u32[]{:S(2)}, u32[]{:S(2)}) collective-permute-start(f32[2,512]{0,1:T(8,128)S(1)} %slice_select_fusion), channel_id=1, source_target_pairs={{16,0},{32,16},{48,32},{64,48},{80,64},{96,80},{112,96},{128,112},... | collective-permute-start | bytes 12296 | tf_op jit(solution)/shard_map/ppermute | solution.py:85
  98.0 11.7 %collective-permute-start.3 = (f32[2,512]{0,1:T(8,128)S(1)}, f32[2,512]{0,1:T(8,128)S(1)}, u32[]{:S(2)}, u32[]{:S(2)}) collective-permute-start(f32[2,512]{0,1:T(8,128)S(1)} %concatenate.106), channel_id=1, source_target_pairs={{0,16},{16,32},{32,48},{48,64},{64,80},{80,96},{96,112},{112,128},... | collective-permute-start | bytes 12296 | tf_op jit(solution)/shard_map/ppermute | solution.py:84

commit v9 on v8

--- a/solution.py
+++ b/solution.py
@@ -5,6 +5,7 @@
 from jax.experimental.pallas import tpu as pltpu
 from jax.sharding import Mesh
 from jax.sharding import PartitionSpec as P
+
 
 TSTEP = 64
 COLS = ("cols_0", "cols_1")
@@ -14,9 +15,9 @@
 MOST = 32
 
 
-def wave_kernel(gt_ref, a_ref, o_ref):
+def dense_kernel(a_ref, d_ref):
     slots = a_ref.shape[0] - 16
-    width = gt_ref.shape[1]
+    width = d_ref.shape[0]
     lanes = a_ref.shape[1]
     code = a_ref[slots:slots + 16, :].astype(jnp.float32)
     start = (code[0:1] * CODE + code[1:2]).astype(jnp.int32)
@@ -35,24 +36,39 @@
         dense = jnp.where(((start >> bit) & 1) == 1, rolled, dense)
     if dense.shape[0] < width:
         dense = jnp.concatenate([dense, jnp.zeros((width - dense.shape[0], lanes), jnp.float32)], axis=0)
-    wave = jnp.dot(gt_ref[...], dense.astype(jnp.bfloat16), preferred_element_type=jnp.float32)
-    rows = wave.shape[0]
+    d_ref[...] = dense.astype(d_ref.dtype)
+
+
+def dense_slips(coded, width):
+    parts, height, lanes = coded.shape
+    return pl.pallas_call(
+        dense_kernel,
+        grid=(parts,),
+        in_specs=[pl.BlockSpec((None, height, lanes), lambda p: (p, 0, 0))],
+        out_specs=pl.BlockSpec((None, width, lanes), lambda p: (p, 0, 0)),
+        out_shape=jax.ShapeDtypeStruct((parts, width, lanes), jnp.bfloat16),
+    )(coded)
+
+
+def wave_kernel(gt_ref, d_ref, o_ref):
+    wave = jnp.dot(gt_ref[...], d_ref[...], preferred_element_type=jnp.float32)
+    rows, lanes = wave.shape
     o_ref[...] = jnp.max(wave.reshape(rows // TSTEP, TSTEP, lanes), axis=1)
 
 
-def wave_maxima(panel_t, coded):
-    parts, height, lanes = coded.shape
-    rows, width = panel_t.shape
+def wave_maxima(panel_t, dense):
+    parts, width, lanes = dense.shape
+    rows = panel_t.shape[0]
     return pl.pallas_call(
         wave_kernel,
         grid=(parts,),
         in_specs=[
             pl.BlockSpec((rows, width), lambda p: (0, 0)),
-            pl.BlockSpec((None, height, lanes), lambda p: (p, 0, 0)),
+            pl.BlockSpec((None, width, lanes), lambda p: (p, 0, 0)),
         ],
         out_specs=pl.BlockSpec((None, rows // TSTEP, lanes), lambda p: (p, 0, 0)),
         out_shape=jax.ShapeDtypeStruct((parts, rows // TSTEP, lanes), jnp.float32),
-    )(panel_t, coded)
+    )(panel_t, dense)
 
 
 def shifted(values, step, fill):
@@ -88,7 +104,7 @@
     return peak.T
 
 
-def local(greens, slip_values, rupture_ids, win_point):
+def step(greens, slip_values, rupture_ids, win_point):
     parts = lax.axis_size(SPLIT)
     shares = lax.axis_size(SHARE)
     own_sources, rows = greens.shape
@@ -120,10 +136,11 @@
     far = lax.ppermute(near, SHARE, [(i, (i + 1) % shares) for i in range(shares)])
     theirs = lax.ppermute(mine, "rows", [(i, i ^ 1) for i in range(count_rows)])
     coded = jnp.where(core == 0, jnp.concatenate([mine, theirs], axis=2), jnp.concatenate([theirs, mine], axis=2))
+    dense = dense_slips(coded, width)
     panel = jnp.where(side == 0, jnp.stack([near, far], axis=1), jnp.stack([far, near], axis=1))
     panel_t = panel.reshape(width, block).T
 
-    maxima = wave_maxima(panel_t, coded)
+    maxima = wave_maxima(panel_t, dense)
     maxima = lax.all_to_all(maxima, SPLIT, 0, 0, tiled=True)
     return point_peaks(maxima.reshape(-1, scen), win_point, MOST)
 
@@ -132,4 +149,4 @@
     split = Mesh(mesh.devices.reshape(mesh.shape["rows"], 8, 2), ("rows", "cols_0", "cols_1"))
     in_specs = (P(COLS, "rows"), P(COLS, None), P(COLS, None), P("rows"))
     out_specs = P(COLS, "rows")
-    return jax.shard_map(local, mesh=split, in_specs=in_specs, out_specs=out_specs, check_vma=False)
+    return jax.shard_map(step, mesh=split, in_specs=in_specs, out_specs=out_specs, check_vma=False)

time: 112 us -> 119 us (1.062)
  Pallas kernels: 9.6 us -> 15.8 us
    pallas_call x0 -> x1, Pallas kernels: none -> 6.94 us  [dense_slips(): pl.pallas_call(dense_kernel, grid=(parts,), in_specs=[pl.BlockSpec((None,...]
where the time goes in v9:
time: 119 us; the launch traced here: 117 us
  waiting for transfers between devices  61.4 us (52%)
  starting transfers between devices  25.1 us (21%)
  Pallas kernels  15.8 us (13%)
  other arithmetic  7.67 us (6%)
  local copies, waits for them, and re-layouts  7.12 us (6%)
    all_to_all x1, waiting for transfers between devices, step(): incoming = lax.all_to_all(outgoing, SPLIT, 0, 0, tiled=True)  31.4 us
    all_to_all x1, waiting for transfers between devices, step(): maxima = lax.all_to_all(maxima, SPLIT, 0, 0, tiled=True)  10.6 us
    all_to_all x1, starting transfers between devices, step(): incoming = lax.all_to_all(outgoing, SPLIT, 0, 0, tiled=True)  10.4 us
    ppermute x1, waiting for transfers between devices, step(): lax.ppermute(near, SHARE, [(i, (i + 1) % shares) for i in range(shares)])  9.89 us
    pallas_call x1, Pallas kernels, wave_maxima(): pl.pallas_call(wave_kernel, grid=(parts,), in_specs=[pl.BlockSpec((rows,...  8.9 us
    pallas_call x1, Pallas kernels, dense_slips(): pl.pallas_call(dense_kernel, grid=(parts,), in_specs=[pl.BlockSpec((None,...  6.94 us
    ppermute x1, waiting for transfers between devices, point_peaks(): lax.ppermute(to_right, 'rows', [(i, i + 1) for i in range(count - 1)])  6.04 us
    ppermute x1, starting transfers between devices, point_peaks(): lax.ppermute(to_left, 'rows', [(i + 1, i) for i in range(count - 1)])  3.91 us
  transfers between devices with their start and end apart: 6, of which 5 were waited for; matrix products, arithmetic and copies ran while one was open for 4% of the time, Pallas kernels for 0%

profile of v9, /device:TPU:6, one launch (start us, length us, event | category | flops | bytes accessed | tf_op | source)
XLA Modules:
  0.0 117.4 jit_solution(11493893008516157820)
XLA Ops:
  0.0 0.0 copy-start
  0.0 1.2 %fusion.1 = (bf16[1,512]{0,1:T(8,128)(2,1)S(1)}, bf16[1,512]{0,1:T(8,128)(2,1)S(1)}) fusion(s32[512,128]{1,0:T(8,128)} %param.6), kind=kLoop, calls=%fused_computation.18 | loop fusion | flops 7680 | bytes 4096 | tf_op jit(solution)/shard_map/convert.1
  1.2 1.1 fusion.6
  2.3 0.1 pad.35.clone
  2.4 0.1 fusion.9
  2.5 0.1 copy.22
  2.6 0.1 broadcast_in_dim.107
  2.7 0.0 copy-done
  2.7 0.3 copy.32
  3.0 0.3 copy.23
  3.3 0.1 broadcast_in_dim.108
  3.4 1.2 pad_maximum_fusion
  4.5 0.0 copy-start.1
  4.5 10.4 %all-to-all-start = ((bf16[8,68,1024]{2,1,0:T(8,128)(2,1)}), bf16[8,68,1024]{2,1,0:T(8,128)(2,1)S(1)}, u32[]{:S(2)}, u32[]{:S(2)}) async-start(bf16[8,68,1024]{2,1,0:T(8,128)(2,1)} %pad_maximum_fusion), calls=%async_computation | async-start | bytes 2359296 | tf_op jit(solution)/shard_map/all_to_all | solution.py:132
  15.0 0.0 copy-done.1
  15.0 0.1 fusion.12
  15.0 0.1 slice_bitcast_fusion.7
  15.1 31.4 %all-to-all-done = bf16[8,68,1024]{2,1,0:T(8,128)(2,1)S(1)} async-done(((bf16[8,68,1024]{2,1,0:T(8,128)(2,1)}), bf16[8,68,1024]{2,1,0:T(8,128)(2,1)S(1)}, u32[]{:S(2)}, u32[]{:S(2)}) %all-to-all-start) | async-done | bytes 1114144 | tf_op jit(solution)/shard_map/all_to_all | solution.py:132
  46.5 0.9 slice_bitcast_fusion.8
  47.5 3.5 %collective-permute-start = (bf16[8,32,1024]{2,1,0:T(8,128)(2,1)}, bf16[8,32,1024]{2,1,0:T(8,128)(2,1)S(1)}, u32[]{:S(2)}, u32[]{:S(2)}) collective-permute-start(bf16[8,32,1024]{2,1,0:T(8,128)(2,1)} %get-tuple-element.10), channel_id=1, source_target_pairs={{0,1},{1,0},{2,3},{3,2},{4,5},{5,4},{6,7},{7,6},{8,9},{9,8},{10,11... | collective-permute-start | bytes 1572872 | tf_op jit(solution)/shard_map/ppermute | solution.py:136
  51.0 0.4 reshape.107
  51.4 1.9 %collective-permute-start.1 = (bf16[8,144,256]{2,1,0:T(8,128)(2,1)S(1)}, bf16[8,144,256]{2,1,0:T(8,128)(2,1)S(1)}, u32[]{:S(2)}, u32[]{:S(2)}) collective-permute-start(bf16[8,144,256]{2,1,0:T(8,128)(2,1)S(1)} %reshape.107), channel_id=1, source_target_pairs={{0,16},{16,0},{32,48},{48,32},{64,80},{80,64},{96,112},{112,96},{1... | collective-permute-start | bytes 1769480 | tf_op jit(solution)/shard_map/ppermute | solution.py:137
  53.3 0.1 slice_bitcast_fusion.4
  53.4 0.1 slice_bitcast_fusion.5
  53.4 0.1 slice_bitcast_fusion.6
  53.5 9.9 %collective-permute-done = bf16[8,32,1024]{2,1,0:T(8,128)(2,1)S(1)} collective-permute-done((bf16[8,32,1024]{2,1,0:T(8,128)(2,1)}, bf16[8,32,1024]{2,1,0:T(8,128)(2,1)S(1)}, u32[]{:S(2)}, u32[]{:S(2)}) %collective-permute-start) | collective-permute-done | bytes 524320 | tf_op jit(solution)/shard_map/ppermute | solution.py:136
  63.4 0.2 maximum_select_fusion.1
  63.6 0.1 copy.24
  63.7 1.3 %copy.25 = bf16[512,1024]{0,1:T(8,128)(2,1)} copy(bf16[512,1024]{1,0:T(8,128)(2,1)S(1)} %bitcast.81) | data formatting | bytes 2097152 | tf_op jit(solution)/shard_map/jit(_where)/select_n | solution.py:140
  65.0 0.0 collective-permute-done.1
  65.0 1.3 %maximum_select_fusion.a_ref = bf16[8,144,512]{2,1,0:T(8,128)(2,1)} fusion(bf16[8,144,256]{2,1,0:T(8,128)(2,1)S(1)} %collective-permute-done.1, bf16[8,144,256]{2,1,0:T(8,128)(2,1)S(1)} %reshape.107, pred[]{:T(512)S(6)} %eq.75), kind=kLoop, calls=%fused_computation.1 | loop fusion | flops 5308416 | bytes 2359297 | tf_op jit(solution)/shard_map/jit(_where)/select_n | solution.py:138
  66.3 6.9 %shard_map.46.d_ref = bf16[8,512,512]{2,1,0:T(8,128)(2,1)} custom-call(bf16[8,144,512]{2,1,0:T(8,128)(2,1)} %maximum_select_fusion.a_ref), custom_call_target="tpu_custom_call" | custom-call | tf_op jit(solution)/shard_map/pallas_call | solution.py:44
  73.3 8.9 %shard_map.47 = f32[8,16,512]{2,1,0:T(8,128)} custom-call(bf16[1024,512]{1,0:T(8,128)(2,1)} %bitcast.82, bf16[8,512,512]{2,1,0:T(8,128)(2,1)} %shard_map.46.d_ref), custom_call_target="tpu_custom_call" | custom-call | tf_op jit(solution)/shard_map/pallas_call | solution.py:62
  82.2 3.4 %all-to-all-start.1 = ((f32[8,16,512]{2,1,0:T(8,128)}), f32[8,16,512]{2,1,0:T(8,128)S(1)}, u32[]{:S(2)}, u32[]{:S(2)}) async-start(f32[8,16,512]{2,1,0:T(8,128)} %shard_map.47), calls=%async_computation.1 | async-start | bytes 524288 | tf_op jit(solution)/shard_map/all_to_all | solution.py:144
  85.6 0.6 fusion.11
  86.2 0.1 maximum_compare_fusion
  86.2 0.1 compare_bitcast_fusion.7
  86.3 10.6 %all-to-all-done.1 = f32[8,16,512]{2,1,0:T(8,128)S(1)} async-done(((f32[8,16,512]{2,1,0:T(8,128)}), f32[8,16,512]{2,1,0:T(8,128)S(1)}, u32[]{:S(2)}, u32[]{:S(2)}) %all-to-all-start.1) | async-done | bytes 262176 | tf_op jit(solution)/shard_map/all_to_all | solution.py:144
  97.0 0.1 copy.27
  97.1 0.1 fusion.10
  97.2 0.1 maximum_select_fusion.13
  97.4 0.1 slice.164
  97.6 0.1 slice.165
  97.7 0.1 slice.166
  97.9 0.0 copy-start.2
  97.9 0.1 slice.167
  98.1 0.4 copy-done.2
  98.5 0.6 slice_select_fusion
  99.2 3.9 %collective-permute-start.2 = (f32[2,512]{0,1:T(8,128)S(1)}, f32[2,512]{0,1:T(8,128)S(1)}, u32[]{:S(2)}, u32[]{:S(2)}) collective-permute-start(f32[2,512]{0,1:T(8,128)S(1)} %slice_select_fusion), channel_id=1, source_target_pairs={{16,0},{32,16},{48,32},{64,48},{80,64},{96,80},{112,96},{128,112},... | collective-permute-start | bytes 12296 | tf_op jit(solution)/shard_map/ppermute | solution.py:101
  103.1 0.1 maximum_select_fusion.7
  103.2 0.1 maximum_select_fusion.6
  103.4 0.1 maximum_select_fusion.5
  103.5 0.1 maximum_select_fusion.4
  103.7 0.1 slice.175
  103.8 0.6 concatenate.106
  104.4 1.9 %collective-permute-start.3 = (f32[2,512]{0,1:T(8,128)S(1)}, f32[2,512]{0,1:T(8,128)S(1)}, u32[]{:S(2)}, u32[]{:S(2)}) collective-permute-start(f32[2,512]{0,1:T(8,128)S(1)} %concatenate.106), channel_id=1, source_target_pairs={{0,16},{16,32},{32,48},{48,64},{64,80},{80,96},{96,112},{112,128},... | collective-permute-start | bytes 12296 | tf_op jit(solution)/shard_map/ppermute | solution.py:100
  106.3 3.4 %collective-permute-done.2 = f32[2,512]{0,1:T(8,128)S(1)} collective-permute-done((f32[2,512]{0,1:T(8,128)S(1)}, f32[2,512]{0,1:T(8,128)S(1)}, u32[]{:S(2)}, u32[]{:S(2)}) %collective-permute-start.2) | collective-permute-done | bytes 4128 | tf_op jit(solution)/shard_map/ppermute | solution.py:101
  109.7 0.3 slice_reduce_fusion.3
  110.0 6.0 %collective-permute-done.3 = f32[2,512]{0,1:T(8,128)S(1)} collective-permute-done((f32[2,512]{0,1:T(8,128)S(1)}, f32[2,512]{0,1:T(8,128)S(1)}, u32[]{:S(2)}, u32[]{:S(2)}) %collective-permute-start.3) | collective-permute-done | bytes 4128 | tf_op jit(solution)/shard_map/ppermute | solution.py:100
  116.1 0.3 slice_reduce_fusion.2
  116.4 1.0 fusion.2
  (7 shorter events, 0.2 us)
Async XLA Ops:
  0.0 2.7 %copy-start = (bf16[32,8192]{1,0:T(8,128)(2,1)S(1)}, bf16[32,8192]{1,0:T(8,128)(2,1)}, u32[]{:S(2)}) copy-start(bf16[32,8192]{1,0:T(8,128)(2,1)} %param.4) | copy-start | bytes 1572868
  4.5 10.5 %copy-start.1 = (s32[128]{0:T(128)S(1)}, s32[128]{0:T(128)}, u32[]{:S(2)}) copy-start(s32[128]{0:T(128)} %param.7) | copy-start | bytes 1540
  4.5 42.0 %all-to-all-start = ((bf16[8,68,1024]{2,1,0:T(8,128)(2,1)}), bf16[8,68,1024]{2,1,0:T(8,128)(2,1)S(1)}, u32[]{:S(2)}, u32[]{:S(2)}) async-start(bf16[8,68,1024]{2,1,0:T(8,128)(2,1)} %pad_maximum_fusion), calls=%async_computation | async-start | bytes 2359296 | tf_op jit(solution)/shard_map/all_to_all | solution.py:132
  47.5 15.9 %collective-permute-start = (bf16[8,32,1024]{2,1,0:T(8,128)(2,1)}, bf16[8,32,1024]{2,1,0:T(8,128)(2,1)S(1)}, u32[]{:S(2)}, u32[]{:S(2)}) collective-permute-start(bf16[8,32,1024]{2,1,0:T(8,128)(2,1)} %get-tuple-element.10), channel_id=1, source_target_pairs={{0,1},{1,0},{2,3},{3,2},{4,5},{5,4},{6,7},{7,6},{8,9},{9,8},{10,11... | collective-permute-start | bytes 1572872 | tf_op jit(solution)/shard_map/ppermute | solution.py:136
  51.4 13.7 %collective-permute-start.1 = (bf16[8,144,256]{2,1,0:T(8,128)(2,1)S(1)}, bf16[8,144,256]{2,1,0:T(8,128)(2,1)S(1)}, u32[]{:S(2)}, u32[]{:S(2)}) collective-permute-start(bf16[8,144,256]{2,1,0:T(8,128)(2,1)S(1)} %reshape.107), channel_id=1, source_target_pairs={{0,16},{16,0},{32,48},{48,32},{64,80},{80,64},{96,112},{112,96},{1... | collective-permute-start | bytes 1769480 | tf_op jit(solution)/shard_map/ppermute | solution.py:137
  82.2 14.8 %all-to-all-start.1 = ((f32[8,16,512]{2,1,0:T(8,128)}), f32[8,16,512]{2,1,0:T(8,128)S(1)}, u32[]{:S(2)}, u32[]{:S(2)}) async-start(f32[8,16,512]{2,1,0:T(8,128)} %shard_map.47), calls=%async_computation.1 | async-start | bytes 524288 | tf_op jit(solution)/shard_map/all_to_all | solution.py:144
  97.9 0.7 copy-start.2
  99.2 10.5 %collective-permute-start.2 = (f32[2,512]{0,1:T(8,128)S(1)}, f32[2,512]{0,1:T(8,128)S(1)}, u32[]{:S(2)}, u32[]{:S(2)}) collective-permute-start(f32[2,512]{0,1:T(8,128)S(1)} %slice_select_fusion), channel_id=1, source_target_pairs={{16,0},{32,16},{48,32},{64,48},{80,64},{96,80},{112,96},{128,112},... | collective-permute-start | bytes 12296 | tf_op jit(solution)/shard_map/ppermute | solution.py:101
  104.4 11.7 %collective-permute-start.3 = (f32[2,512]{0,1:T(8,128)S(1)}, f32[2,512]{0,1:T(8,128)S(1)}, u32[]{:S(2)}, u32[]{:S(2)}) collective-permute-start(f32[2,512]{0,1:T(8,128)S(1)} %concatenate.106), channel_id=1, source_target_pairs={{0,16},{16,32},{32,48},{48,64},{64,80},{80,96},{96,112},{112,128},... | collective-permute-start | bytes 12296 | tf_op jit(solution)/shard_map/ppermute | solution.py:100

commit v10 on v9

--- a/solution.py
+++ b/solution.py
@@ -51,9 +51,13 @@
 
 
 def wave_kernel(gt_ref, d_ref, o_ref):
-    wave = jnp.dot(gt_ref[...], d_ref[...], preferred_element_type=jnp.float32)
-    rows, lanes = wave.shape
-    o_ref[...] = jnp.max(wave.reshape(rows // TSTEP, TSTEP, lanes), axis=1)
+    dense = d_ref[...]
+    rows = gt_ref.shape[0]
+    group = min(8, rows // TSTEP)
+    for first in range(0, rows // TSTEP, group):
+        wave = jnp.dot(gt_ref[first * TSTEP:(first + group) * TSTEP, :], dense, preferred_element_type=jnp.float32)
+        peaks = [jnp.max(wave[w * TSTEP:(w + 1) * TSTEP], axis=0, keepdims=True) for w in range(group)]
+        o_ref[first:first + group, :] = jnp.concatenate(peaks, axis=0)
 
 
 def wave_maxima(panel_t, dense):

time: 119 us -> 119 us (level)
  no operation moved by 1% of the time
where the time goes in v10:
time: 119 us; the launch traced here: 117 us
  waiting for transfers between devices  61.4 us (52%)
  starting transfers between devices  25.1 us (21%)
  Pallas kernels  15.9 us (13%)
  other arithmetic  7.67 us (6%)
  local copies, waits for them, and re-layouts  7.12 us (6%)
    all_to_all x1, waiting for transfers between devices, step(): incoming = lax.all_to_all(outgoing, SPLIT, 0, 0, tiled=True)  31.4 us
    all_to_all x1, waiting for transfers between devices, step(): maxima = lax.all_to_all(maxima, SPLIT, 0, 0, tiled=True)  10.6 us
    all_to_all x1, starting transfers between devices, step(): incoming = lax.all_to_all(outgoing, SPLIT, 0, 0, tiled=True)  10.4 us
    ppermute x1, waiting for transfers between devices, step(): lax.ppermute(near, SHARE, [(i, (i + 1) % shares) for i in range(shares)])  9.89 us
    pallas_call x1, Pallas kernels, wave_maxima(): pl.pallas_call(wave_kernel, grid=(parts,), in_specs=[pl.BlockSpec((rows,...  8.93 us
    pallas_call x1, Pallas kernels, dense_slips(): pl.pallas_call(dense_kernel, grid=(parts,), in_specs=[pl.BlockSpec((None,...  6.94 us
    ppermute x1, waiting for transfers between devices, point_peaks(): lax.ppermute(to_right, 'rows', [(i, i + 1) for i in range(count - 1)])  6.05 us
    ppermute x1, starting transfers between devices, point_peaks(): lax.ppermute(to_left, 'rows', [(i + 1, i) for i in range(count - 1)])  3.9 us
  transfers between devices with their start and end apart: 6, of which 5 were waited for; matrix products, arithmetic and copies ran while one was open for 4% of the time, Pallas kernels for 0%

profile of v10, /device:TPU:6, one launch (start us, length us, event | category | flops | bytes accessed | tf_op | source)
XLA Modules:
  0.0 117.5 jit_solution(5084260377568725615)
XLA Ops:
  0.0 0.0 copy-start
  0.0 1.2 %fusion.1 = (bf16[1,512]{0,1:T(8,128)(2,1)S(1)}, bf16[1,512]{0,1:T(8,128)(2,1)S(1)}) fusion(s32[512,128]{1,0:T(8,128)} %param.6), kind=kLoop, calls=%fused_computation.18 | loop fusion | flops 7680 | bytes 4096 | tf_op jit(solution)/shard_map/convert.1
  1.2 1.1 fusion.6
  2.3 0.1 pad.35.clone
  2.4 0.1 fusion.9
  2.5 0.1 copy.22
  2.6 0.1 broadcast_in_dim.107
  2.7 0.0 copy-done
  2.7 0.3 copy.32
  3.0 0.3 copy.23
  3.3 0.1 broadcast_in_dim.108
  3.4 1.2 pad_maximum_fusion
  4.5 0.0 copy-start.1
  4.5 10.4 %all-to-all-start = ((bf16[8,68,1024]{2,1,0:T(8,128)(2,1)}), bf16[8,68,1024]{2,1,0:T(8,128)(2,1)S(1)}, u32[]{:S(2)}, u32[]{:S(2)}) async-start(bf16[8,68,1024]{2,1,0:T(8,128)(2,1)} %pad_maximum_fusion), calls=%async_computation | async-start | bytes 2359296 | tf_op jit(solution)/shard_map/all_to_all | solution.py:136
  15.0 0.0 copy-done.1
  15.0 0.1 fusion.12
  15.0 0.1 slice_bitcast_fusion.7
  15.1 31.4 %all-to-all-done = bf16[8,68,1024]{2,1,0:T(8,128)(2,1)S(1)} async-done(((bf16[8,68,1024]{2,1,0:T(8,128)(2,1)}), bf16[8,68,1024]{2,1,0:T(8,128)(2,1)S(1)}, u32[]{:S(2)}, u32[]{:S(2)}) %all-to-all-start) | async-done | bytes 1114144 | tf_op jit(solution)/shard_map/all_to_all | solution.py:136
  46.5 0.9 slice_bitcast_fusion.8
  47.5 3.5 %collective-permute-start = (bf16[8,32,1024]{2,1,0:T(8,128)(2,1)}, bf16[8,32,1024]{2,1,0:T(8,128)(2,1)S(1)}, u32[]{:S(2)}, u32[]{:S(2)}) collective-permute-start(bf16[8,32,1024]{2,1,0:T(8,128)(2,1)} %get-tuple-element.10), channel_id=1, source_target_pairs={{0,1},{1,0},{2,3},{3,2},{4,5},{5,4},{6,7},{7,6},{8,9},{9,8},{10,11... | collective-permute-start | bytes 1572872 | tf_op jit(solution)/shard_map/ppermute | solution.py:140
  51.0 0.4 reshape.107
  51.4 1.9 %collective-permute-start.1 = (bf16[8,144,256]{2,1,0:T(8,128)(2,1)S(1)}, bf16[8,144,256]{2,1,0:T(8,128)(2,1)S(1)}, u32[]{:S(2)}, u32[]{:S(2)}) collective-permute-start(bf16[8,144,256]{2,1,0:T(8,128)(2,1)S(1)} %reshape.107), channel_id=1, source_target_pairs={{0,16},{16,0},{32,48},{48,32},{64,80},{80,64},{96,112},{112,96},{1... | collective-permute-start | bytes 1769480 | tf_op jit(solution)/shard_map/ppermute | solution.py:141
  53.3 0.1 slice_bitcast_fusion.4
  53.4 0.1 slice_bitcast_fusion.5
  53.4 0.1 slice_bitcast_fusion.6
  53.5 9.9 %collective-permute-done = bf16[8,32,1024]{2,1,0:T(8,128)(2,1)S(1)} collective-permute-done((bf16[8,32,1024]{2,1,0:T(8,128)(2,1)}, bf16[8,32,1024]{2,1,0:T(8,128)(2,1)S(1)}, u32[]{:S(2)}, u32[]{:S(2)}) %collective-permute-start) | collective-permute-done | bytes 524320 | tf_op jit(solution)/shard_map/ppermute | solution.py:140
  63.4 0.2 maximum_select_fusion.1
  63.6 0.1 copy.24
  63.7 1.3 %copy.25 = bf16[512,1024]{0,1:T(8,128)(2,1)} copy(bf16[512,1024]{1,0:T(8,128)(2,1)S(1)} %bitcast.81) | data formatting | bytes 2097152 | tf_op jit(solution)/shard_map/jit(_where)/select_n | solution.py:144
  65.0 0.0 collective-permute-done.1
  65.0 1.3 %maximum_select_fusion.a_ref = bf16[8,144,512]{2,1,0:T(8,128)(2,1)} fusion(bf16[8,144,256]{2,1,0:T(8,128)(2,1)S(1)} %collective-permute-done.1, bf16[8,144,256]{2,1,0:T(8,128)(2,1)S(1)} %reshape.107, pred[]{:T(512)S(6)} %eq.75), kind=kLoop, calls=%fused_computation.1 | loop fusion | flops 5308416 | bytes 2359297 | tf_op jit(solution)/shard_map/jit(_where)/select_n | solution.py:142
  66.3 6.9 %shard_map.46.d_ref = bf16[8,512,512]{2,1,0:T(8,128)(2,1)} custom-call(bf16[8,144,512]{2,1,0:T(8,128)(2,1)} %maximum_select_fusion.a_ref), custom_call_target="tpu_custom_call" | custom-call | tf_op jit(solution)/shard_map/pallas_call | solution.py:44
  73.3 8.9 %shard_map.47 = f32[8,16,512]{2,1,0:T(8,128)} custom-call(bf16[1024,512]{1,0:T(8,128)(2,1)} %bitcast.82, bf16[8,512,512]{2,1,0:T(8,128)(2,1)} %shard_map.46.d_ref), custom_call_target="tpu_custom_call" | custom-call | tf_op jit(solution)/shard_map/pallas_call | solution.py:66
  82.2 3.4 %all-to-all-start.1 = ((f32[8,16,512]{2,1,0:T(8,128)}), f32[8,16,512]{2,1,0:T(8,128)S(1)}, u32[]{:S(2)}, u32[]{:S(2)}) async-start(f32[8,16,512]{2,1,0:T(8,128)} %shard_map.47), calls=%async_computation.1 | async-start | bytes 524288 | tf_op jit(solution)/shard_map/all_to_all | solution.py:148
  85.6 0.6 fusion.11
  86.2 0.1 maximum_compare_fusion
  86.3 0.1 compare_bitcast_fusion.7
  86.3 10.6 %all-to-all-done.1 = f32[8,16,512]{2,1,0:T(8,128)S(1)} async-done(((f32[8,16,512]{2,1,0:T(8,128)}), f32[8,16,512]{2,1,0:T(8,128)S(1)}, u32[]{:S(2)}, u32[]{:S(2)}) %all-to-all-start.1) | async-done | bytes 262176 | tf_op jit(solution)/shard_map/all_to_all | solution.py:148
  97.0 0.1 copy.27
  97.1 0.1 fusion.10
  97.3 0.1 maximum_select_fusion.13
  97.4 0.1 slice.164
  97.6 0.1 slice.165
  97.8 0.1 slice.166
  97.9 0.0 copy-start.2
  97.9 0.1 slice.167
  98.1 0.4 copy-done.2
  98.6 0.6 slice_select_fusion
  99.2 3.9 %collective-permute-start.2 = (f32[2,512]{0,1:T(8,128)S(1)}, f32[2,512]{0,1:T(8,128)S(1)}, u32[]{:S(2)}, u32[]{:S(2)}) collective-permute-start(f32[2,512]{0,1:T(8,128)S(1)} %slice_select_fusion), channel_id=1, source_target_pairs={{16,0},{32,16},{48,32},{64,48},{80,64},{96,80},{112,96},{128,112},... | collective-permute-start | bytes 12296 | tf_op jit(solution)/shard_map/ppermute | solution.py:105
  103.1 0.1 maximum_select_fusion.7
  103.3 0.1 maximum_select_fusion.6
  103.4 0.1 maximum_select_fusion.5
  103.5 0.1 maximum_select_fusion.4
  103.7 0.1 slice.175
  103.8 0.6 concatenate.106
  104.4 1.9 %collective-permute-start.3 = (f32[2,512]{0,1:T(8,128)S(1)}, f32[2,512]{0,1:T(8,128)S(1)}, u32[]{:S(2)}, u32[]{:S(2)}) collective-permute-start(f32[2,512]{0,1:T(8,128)S(1)} %concatenate.106), channel_id=1, source_target_pairs={{0,16},{16,32},{32,48},{48,64},{64,80},{80,96},{96,112},{112,128},... | collective-permute-start | bytes 12296 | tf_op jit(solution)/shard_map/ppermute | solution.py:104
  106.3 3.4 %collective-permute-done.2 = f32[2,512]{0,1:T(8,128)S(1)} collective-permute-done((f32[2,512]{0,1:T(8,128)S(1)}, f32[2,512]{0,1:T(8,128)S(1)}, u32[]{:S(2)}, u32[]{:S(2)}) %collective-permute-start.2) | collective-permute-done | bytes 4128 | tf_op jit(solution)/shard_map/ppermute | solution.py:105
  109.8 0.3 slice_reduce_fusion.3
  110.1 6.0 %collective-permute-done.3 = f32[2,512]{0,1:T(8,128)S(1)} collective-permute-done((f32[2,512]{0,1:T(8,128)S(1)}, f32[2,512]{0,1:T(8,128)S(1)}, u32[]{:S(2)}, u32[]{:S(2)}) %collective-permute-start.3) | collective-permute-done | bytes 4128 | tf_op jit(solution)/shard_map/ppermute | solution.py:104
  116.1 0.3 slice_reduce_fusion.2
  116.4 1.0 fusion.2
  (7 shorter events, 0.2 us)
Async XLA Ops:
  0.0 2.7 %copy-start = (bf16[32,8192]{1,0:T(8,128)(2,1)S(1)}, bf16[32,8192]{1,0:T(8,128)(2,1)}, u32[]{:S(2)}) copy-start(bf16[32,8192]{1,0:T(8,128)(2,1)} %param.4) | copy-start | bytes 1572868
  4.5 10.5 %copy-start.1 = (s32[128]{0:T(128)S(1)}, s32[128]{0:T(128)}, u32[]{:S(2)}) copy-start(s32[128]{0:T(128)} %param.7) | copy-start | bytes 1540
  4.5 42.0 %all-to-all-start = ((bf16[8,68,1024]{2,1,0:T(8,128)(2,1)}), bf16[8,68,1024]{2,1,0:T(8,128)(2,1)S(1)}, u32[]{:S(2)}, u32[]{:S(2)}) async-start(bf16[8,68,1024]{2,1,0:T(8,128)(2,1)} %pad_maximum_fusion), calls=%async_computation | async-start | bytes 2359296 | tf_op jit(solution)/shard_map/all_to_all | solution.py:136
  47.5 15.9 %collective-permute-start = (bf16[8,32,1024]{2,1,0:T(8,128)(2,1)}, bf16[8,32,1024]{2,1,0:T(8,128)(2,1)S(1)}, u32[]{:S(2)}, u32[]{:S(2)}) collective-permute-start(bf16[8,32,1024]{2,1,0:T(8,128)(2,1)} %get-tuple-element.10), channel_id=1, source_target_pairs={{0,1},{1,0},{2,3},{3,2},{4,5},{5,4},{6,7},{7,6},{8,9},{9,8},{10,11... | collective-permute-start | bytes 1572872 | tf_op jit(solution)/shard_map/ppermute | solution.py:140
  51.4 13.7 %collective-permute-start.1 = (bf16[8,144,256]{2,1,0:T(8,128)(2,1)S(1)}, bf16[8,144,256]{2,1,0:T(8,128)(2,1)S(1)}, u32[]{:S(2)}, u32[]{:S(2)}) collective-permute-start(bf16[8,144,256]{2,1,0:T(8,128)(2,1)S(1)} %reshape.107), channel_id=1, source_target_pairs={{0,16},{16,0},{32,48},{48,32},{64,80},{80,64},{96,112},{112,96},{1... | collective-permute-start | bytes 1769480 | tf_op jit(solution)/shard_map/ppermute | solution.py:141
  82.2 14.8 %all-to-all-start.1 = ((f32[8,16,512]{2,1,0:T(8,128)}), f32[8,16,512]{2,1,0:T(8,128)S(1)}, u32[]{:S(2)}, u32[]{:S(2)}) async-start(f32[8,16,512]{2,1,0:T(8,128)} %shard_map.47), calls=%async_computation.1 | async-start | bytes 524288 | tf_op jit(solution)/shard_map/all_to_all | solution.py:148
  97.9 0.7 copy-start.2
  99.2 10.5 %collective-permute-start.2 = (f32[2,512]{0,1:T(8,128)S(1)}, f32[2,512]{0,1:T(8,128)S(1)}, u32[]{:S(2)}, u32[]{:S(2)}) collective-permute-start(f32[2,512]{0,1:T(8,128)S(1)} %slice_select_fusion), channel_id=1, source_target_pairs={{16,0},{32,16},{48,32},{64,48},{80,64},{96,80},{112,96},{128,112},... | collective-permute-start | bytes 12296 | tf_op jit(solution)/shard_map/ppermute | solution.py:105
  104.4 11.7 %collective-permute-start.3 = (f32[2,512]{0,1:T(8,128)S(1)}, f32[2,512]{0,1:T(8,128)S(1)}, u32[]{:S(2)}, u32[]{:S(2)}) collective-permute-start(f32[2,512]{0,1:T(8,128)S(1)} %concatenate.106), channel_id=1, source_target_pairs={{0,16},{16,32},{32,48},{48,64},{64,80},{80,96},{96,112},{112,128},... | collective-permute-start | bytes 12296 | tf_op jit(solution)/shard_map/ppermute | solution.py:104

commit v11 on v9

--- a/solution.py
+++ b/solution.py
@@ -50,13 +50,32 @@
     )(coded)
 
 
-def wave_kernel(gt_ref, d_ref, o_ref):
-    wave = jnp.dot(gt_ref[...], d_ref[...], preferred_element_type=jnp.float32)
+def near_kernel(gt_ref, d_ref, o_ref):
+    o_ref[...] = jnp.dot(gt_ref[...], d_ref[...], preferred_element_type=jnp.float32)
+
+
+def near_waves(panel_t, dense):
+    parts, width, lanes = dense.shape
+    rows = panel_t.shape[0]
+    return pl.pallas_call(
+        near_kernel,
+        grid=(parts,),
+        in_specs=[
+            pl.BlockSpec((rows, width), lambda p: (0, 0)),
+            pl.BlockSpec((None, width, lanes), lambda p: (p, 0, 0)),
+        ],
+        out_specs=pl.BlockSpec((None, rows, lanes), lambda p: (p, 0, 0)),
+        out_shape=jax.ShapeDtypeStruct((parts, rows, lanes), jnp.float32),
+    )(panel_t, dense)
+
+
+def wave_kernel(gt_ref, d_ref, w_ref, o_ref):
+    wave = w_ref[...] + jnp.dot(gt_ref[...], d_ref[...], preferred_element_type=jnp.float32)
     rows, lanes = wave.shape
     o_ref[...] = jnp.max(wave.reshape(rows // TSTEP, TSTEP, lanes), axis=1)
 
 
-def wave_maxima(panel_t, dense):
+def wave_maxima(panel_t, dense, partial):
     parts, width, lanes = dense.shape
     rows = panel_t.shape[0]
     return pl.pallas_call(
@@ -65,10 +84,11 @@
         in_specs=[
             pl.BlockSpec((rows, width), lambda p: (0, 0)),
             pl.BlockSpec((None, width, lanes), lambda p: (p, 0, 0)),
+            pl.BlockSpec((None, rows, lanes), lambda p: (p, 0, 0)),
         ],
         out_specs=pl.BlockSpec((None, rows // TSTEP, lanes), lambda p: (p, 0, 0)),
         out_shape=jax.ShapeDtypeStruct((parts, rows // TSTEP, lanes), jnp.float32),
-    )(panel_t, dense)
+    )(panel_t, dense, partial)
 
 
 def shifted(values, step, fill):
@@ -137,10 +157,11 @@
     theirs = lax.ppermute(mine, "rows", [(i, i ^ 1) for i in range(count_rows)])
     coded = jnp.where(core == 0, jnp.concatenate([mine, theirs], axis=2), jnp.concatenate([theirs, mine], axis=2))
     dense = dense_slips(coded, width)
-    panel = jnp.where(side == 0, jnp.stack([near, far], axis=1), jnp.stack([far, near], axis=1))
-    panel_t = panel.reshape(width, block).T
-
-    maxima = wave_maxima(panel_t, dense)
+    dense = dense.reshape(parts, parts, shares, own_sources, scen)
+    dense_near = jnp.where(side == 0, dense[:, :, 0], dense[:, :, 1]).reshape(parts, width // shares, scen)
+    dense_far = jnp.where(side == 0, dense[:, :, 1], dense[:, :, 0]).reshape(parts, width // shares, scen)
+    partial = near_waves(near.reshape(width // shares, block).T, dense_near)
+    maxima = wave_maxima(far.reshape(width // shares, block).T, dense_far, partial)
     maxima = lax.all_to_all(maxima, SPLIT, 0, 0, tiled=True)
     return point_peaks(maxima.reshape(-1, scen), win_point, MOST)
 

time: 119 us -> 132 us (1.11)
  Pallas kernels: 15.8 us -> 26.8 us
  other arithmetic: 7.67 us -> 12 us
    pallas_call x0 -> x1, Pallas kernels: none -> 9.33 us  [near_waves(): pl.pallas_call(near_kernel, grid=(parts,), in_specs=[pl.BlockSpec((rows,...]
    select_n x1, other arithmetic: 0.17 us -> 4.46 us  [step(): jnp.where(side == 0, dense[:, :, 0], dense[:, :, 1])]
    reshape x0 -> x2, local copies, waits for them, and re-layouts: none -> 1.99 us  [the longest x1 1 us: step(): partial = near_waves(near.reshape(width // shares, block).T, dense_near)]
    pallas_call x1, Pallas kernels: 8.9 us -> 10.5 us  [wave_maxima(): pl.pallas_call(wave_kernel, grid=(parts,), in_specs=[pl.BlockSpec((rows,...]
    select_n x2 -> x0, local copies, waits for them, and re-layouts: 1.43 us -> none  [step(): jnp.where(side == 0, jnp.stack([near, far], axis=1), jnp.stack([far, near...]
where the time goes in v11:
time: 132 us; the launch traced here: 131 us
  waiting for transfers between devices  60.2 us (46%)
  Pallas kernels  26.8 us (20%)
  starting transfers between devices  24.9 us (19%)
  other arithmetic  12 us (9%)
  local copies, waits for them, and re-layouts  6.48 us (5%)
    all_to_all x1, waiting for transfers between devices, step(): incoming = lax.all_to_all(outgoing, SPLIT, 0, 0, tiled=True)  31.4 us
    all_to_all x1, waiting for transfers between devices, step(): maxima = lax.all_to_all(maxima, SPLIT, 0, 0, tiled=True)  10.7 us
    pallas_call x1, Pallas kernels, wave_maxima(): pl.pallas_call(wave_kernel, grid=(parts,), in_specs=[pl.BlockSpec((rows,...  10.5 us
    all_to_all x1, starting transfers between devices, step(): incoming = lax.all_to_all(outgoing, SPLIT, 0, 0, tiled=True)  10.3 us
    pallas_call x1, Pallas kernels, near_waves(): pl.pallas_call(near_kernel, grid=(parts,), in_specs=[pl.BlockSpec((rows,...  9.33 us
    ppermute x1, waiting for transfers between devices, step(): lax.ppermute(near, SHARE, [(i, (i + 1) % shares) for i in range(shares)])  8.68 us
    pallas_call x1, Pallas kernels, dense_slips(): pl.pallas_call(dense_kernel, grid=(parts,), in_specs=[pl.BlockSpec((None,...  6.94 us
    ppermute x1, waiting for transfers between devices, point_peaks(): lax.ppermute(to_right, 'rows', [(i, i + 1) for i in range(count - 1)])  6.04 us
  transfers between devices with their start and end apart: 6, of which 5 were waited for; matrix products, arithmetic and copies ran while one was open for 4% of the time, Pallas kernels for 0%

profile of v11, /device:TPU:6, one launch (start us, length us, event | category | flops | bytes accessed | tf_op | source)
XLA Modules:
  0.0 130.7 jit_solution(12510209296903668163)
XLA Ops:
  0.0 0.0 copy-start
  0.0 1.2 fusion.1
  1.2 1.1 fusion.6
  2.3 0.1 pad.31.clone
  2.4 0.1 fusion.9
  2.5 0.1 copy.26
  2.6 0.1 broadcast_in_dim.107
  2.7 0.0 copy-done
  2.7 0.3 copy.40
  3.0 0.3 copy.27
  3.3 0.1 broadcast_in_dim.108
  3.4 0.0 copy-start.1
  3.4 1.1 pad_maximum_fusion
  4.5 10.3 %all-to-all-start = ((bf16[8,68,1024]{2,1,0:T(8,128)(2,1)}), bf16[8,68,1024]{2,1,0:T(8,128)(2,1)S(1)}, u32[]{:S(2)}, u32[]{:S(2)}) async-start(bf16[8,68,1024]{2,1,0:T(8,128)(2,1)} %pad_maximum_fusion), calls=%async_computation | async-start | bytes 2359296 | tf_op jit(solution)/shard_map/all_to_all | solution.py:152
  14.8 0.0 copy-done.1
  14.9 0.1 fusion.12
  14.9 0.1 slice_bitcast_fusion.9
  15.0 31.4 %all-to-all-done = bf16[8,68,1024]{2,1,0:T(8,128)(2,1)S(1)} async-done(((bf16[8,68,1024]{2,1,0:T(8,128)(2,1)}), bf16[8,68,1024]{2,1,0:T(8,128)(2,1)S(1)}, u32[]{:S(2)}, u32[]{:S(2)}) %all-to-all-start) | async-done | bytes 1114144 | tf_op jit(solution)/shard_map/all_to_all | solution.py:152
  46.5 3.5 %collective-permute-start = (bf16[8,32,1024]{2,1,0:T(8,128)(2,1)S(1)}, bf16[8,32,1024]{2,1,0:T(8,128)(2,1)S(1)}, u32[]{:S(2)}, u32[]{:S(2)}) collective-permute-start(bf16[8,32,1024]{2,1,0:T(8,128)(2,1)S(1)} %slice.171), channel_id=1, source_target_pairs={{0,1},{1,0},{2,3},{3,2},{4,5},{5,4},{6,7},{7,6},{8,9},{9,8},{10,11... | collective-permute-start | bytes 1572872 | tf_op jit(solution)/shard_map/ppermute | solution.py:156
  50.0 0.4 reshape.122
  50.4 1.9 %collective-permute-start.1 = (bf16[8,144,256]{2,1,0:T(8,128)(2,1)S(1)}, bf16[8,144,256]{2,1,0:T(8,128)(2,1)S(1)}, u32[]{:S(2)}, u32[]{:S(2)}) collective-permute-start(bf16[8,144,256]{2,1,0:T(8,128)(2,1)S(1)} %reshape.122), channel_id=1, source_target_pairs={{0,16},{16,0},{32,48},{48,32},{64,80},{80,64},{96,112},{112,96},{1... | collective-permute-start | bytes 1769480 | tf_op jit(solution)/shard_map/ppermute | solution.py:157
  52.3 0.1 slice_bitcast_fusion.6
  52.4 0.1 slice_bitcast_fusion.7
  52.4 0.1 slice_bitcast_fusion.8
  52.5 1.0 copy.31
  53.5 8.7 %collective-permute-done = bf16[8,32,1024]{2,1,0:T(8,128)(2,1)S(1)} collective-permute-done((bf16[8,32,1024]{2,1,0:T(8,128)(2,1)S(1)}, bf16[8,32,1024]{2,1,0:T(8,128)(2,1)S(1)}, u32[]{:S(2)}, u32[]{:S(2)}) %collective-permute-start) | collective-permute-done | bytes 524320 | tf_op jit(solution)/shard_map/ppermute | solution.py:156
  62.2 1.0 copy.28
  63.2 0.0 collective-permute-done.1
  63.2 1.3 maximum_select_fusion.a_ref
  64.5 6.9 %shard_map.46 = bf16[8,512,512]{2,1,0:T(8,128)(2,1)} custom-call(bf16[8,144,512]{2,1,0:T(8,128)(2,1)} %maximum_select_fusion.a_ref), custom_call_target="tpu_custom_call" | custom-call | tf_op jit(solution)/shard_map/pallas_call | solution.py:44
  71.4 4.5 %broadcast_select_fusion = (bf16[8,8,1,32,512]{4,3,1,0,2:T(8,128)(2,1)}, bf16[8,8,1,32,512]{4,3,1,0,2:T(8,128)(2,1)}) fusion(pred[]{:T(512)S(6)} %eq.75, bf16[8,8,2,32,512]{4,3,2,1,0:T(8,128)(2,1)} %bitcast.95), kind=kLoop, calls=%fused_computation.2 | loop fusion | flops 2097152 | bytes 8388609 | tf_op jit(solution)/shard_map/jit(_where)/select_n | solution.py:161
  75.9 9.3 %shard_map.47.w_ref = f32[8,1024,512]{2,1,0:T(8,128)} custom-call(bf16[1024,256]{1,0:T(8,128)(2,1)} %bitcast.102, bf16[8,256,512]{2,1,0:T(8,128)(2,1)} %bitcast.97), custom_call_target="tpu_custom_call" | custom-call | tf_op jit(solution)/shard_map/pallas_call | solution.py:60
  85.2 10.5 %shard_map.48 = f32[8,16,512]{2,1,0:T(8,128)} custom-call(bf16[1024,256]{1,0:T(8,128)(2,1)} %bitcast.103, bf16[8,256,512]{2,1,0:T(8,128)(2,1)} %bitcast.96, f32[8,1024,512]{2,1,0:T(8,128)} %shard_map.47.w_ref), custom_call_target="tpu_custom_call" | custom-call | tf_op jit(solution)/shard_map/pallas_call | solution.py:81
  95.8 3.4 %all-to-all-start.1 = ((f32[8,16,512]{2,1,0:T(8,128)}), f32[8,16,512]{2,1,0:T(8,128)S(1)}, u32[]{:S(2)}, u32[]{:S(2)}) async-start(f32[8,16,512]{2,1,0:T(8,128)} %shard_map.48), calls=%async_computation.1 | async-start | bytes 524288 | tf_op jit(solution)/shard_map/all_to_all | solution.py:165
  99.2 0.6 fusion.11
  99.8 0.1 maximum_compare_fusion
  99.8 0.1 compare_bitcast_fusion.7
  99.9 10.7 %all-to-all-done.1 = f32[8,16,512]{2,1,0:T(8,128)S(1)} async-done(((f32[8,16,512]{2,1,0:T(8,128)}), f32[8,16,512]{2,1,0:T(8,128)S(1)}, u32[]{:S(2)}, u32[]{:S(2)}) %all-to-all-start.1) | async-done | bytes 262176 | tf_op jit(solution)/shard_map/all_to_all | solution.py:165
  110.6 0.1 copy.33
  110.7 0.1 fusion.10
  110.9 0.1 maximum_select_fusion.12
  111.0 0.1 slice.176
  111.2 0.0 copy-start.2
  111.2 0.1 slice.177
  111.4 0.1 slice.178
  111.5 0.1 slice.179
  111.7 0.1 copy-done.2
  111.8 0.6 slice_select_fusion
  112.5 3.9 %collective-permute-start.2 = (f32[2,512]{0,1:T(8,128)S(1)}, f32[2,512]{0,1:T(8,128)S(1)}, u32[]{:S(2)}, u32[]{:S(2)}) collective-permute-start(f32[2,512]{0,1:T(8,128)S(1)} %slice_select_fusion), channel_id=1, source_target_pairs={{16,0},{32,16},{48,32},{64,48},{80,64},{96,80},{112,96},{128,112},... | collective-permute-start | bytes 12296 | tf_op jit(solution)/shard_map/ppermute | solution.py:121
  116.4 0.1 maximum_select_fusion.6
  116.5 0.1 maximum_select_fusion.5
  116.7 0.1 maximum_select_fusion.4
  116.8 0.1 maximum_select_fusion.3
  116.9 0.1 slice.187
  117.1 0.6 concatenate.106
  117.7 1.9 %collective-permute-start.3 = (f32[2,512]{0,1:T(8,128)S(1)}, f32[2,512]{0,1:T(8,128)S(1)}, u32[]{:S(2)}, u32[]{:S(2)}) collective-permute-start(f32[2,512]{0,1:T(8,128)S(1)} %concatenate.106), channel_id=1, source_target_pairs={{0,16},{16,32},{32,48},{48,64},{64,80},{80,96},{96,112},{112,128},... | collective-permute-start | bytes 12296 | tf_op jit(solution)/shard_map/ppermute | solution.py:120
  119.6 3.4 %collective-permute-done.2 = f32[2,512]{0,1:T(8,128)S(1)} collective-permute-done((f32[2,512]{0,1:T(8,128)S(1)}, f32[2,512]{0,1:T(8,128)S(1)}, u32[]{:S(2)}, u32[]{:S(2)}) %collective-permute-start.2) | collective-permute-done | bytes 4128 | tf_op jit(solution)/shard_map/ppermute | solution.py:121
  123.0 0.3 slice_reduce_fusion.3
  123.3 6.0 %collective-permute-done.3 = f32[2,512]{0,1:T(8,128)S(1)} collective-permute-done((f32[2,512]{0,1:T(8,128)S(1)}, f32[2,512]{0,1:T(8,128)S(1)}, u32[]{:S(2)}, u32[]{:S(2)}) %collective-permute-start.3) | collective-permute-done | bytes 4128 | tf_op jit(solution)/shard_map/ppermute | solution.py:120
  129.4 0.3 slice_reduce_fusion.2
  129.7 1.0 fusion.2
  (8 shorter events, 0.2 us)
Async XLA Ops:
  0.0 2.7 %copy-start = (bf16[32,8192]{1,0:T(8,128)(2,1)S(1)}, bf16[32,8192]{1,0:T(8,128)(2,1)}, u32[]{:S(2)}) copy-start(bf16[32,8192]{1,0:T(8,128)(2,1)} %param.4) | copy-start | bytes 1572868
  3.4 11.5 %copy-start.1 = (s32[128]{0:T(128)S(1)}, s32[128]{0:T(128)}, u32[]{:S(2)}) copy-start(s32[128]{0:T(128)} %param.7) | copy-start | bytes 1540
  4.5 41.9 %all-to-all-start = ((bf16[8,68,1024]{2,1,0:T(8,128)(2,1)}), bf16[8,68,1024]{2,1,0:T(8,128)(2,1)S(1)}, u32[]{:S(2)}, u32[]{:S(2)}) async-start(bf16[8,68,1024]{2,1,0:T(8,128)(2,1)} %pad_maximum_fusion), calls=%async_computation | async-start | bytes 2359296 | tf_op jit(solution)/shard_map/all_to_all | solution.py:152
  46.5 15.7 %collective-permute-start = (bf16[8,32,1024]{2,1,0:T(8,128)(2,1)S(1)}, bf16[8,32,1024]{2,1,0:T(8,128)(2,1)S(1)}, u32[]{:S(2)}, u32[]{:S(2)}) collective-permute-start(bf16[8,32,1024]{2,1,0:T(8,128)(2,1)S(1)} %slice.171), channel_id=1, source_target_pairs={{0,1},{1,0},{2,3},{3,2},{4,5},{5,4},{6,7},{7,6},{8,9},{9,8},{10,11... | collective-permute-start | bytes 1572872 | tf_op jit(solution)/shard_map/ppermute | solution.py:156
  50.4 12.8 %collective-permute-start.1 = (bf16[8,144,256]{2,1,0:T(8,128)(2,1)S(1)}, bf16[8,144,256]{2,1,0:T(8,128)(2,1)S(1)}, u32[]{:S(2)}, u32[]{:S(2)}) collective-permute-start(bf16[8,144,256]{2,1,0:T(8,128)(2,1)S(1)} %reshape.122), channel_id=1, source_target_pairs={{0,16},{16,0},{32,48},{48,32},{64,80},{80,64},{96,112},{112,96},{1... | collective-permute-start | bytes 1769480 | tf_op jit(solution)/shard_map/ppermute | solution.py:157
  95.8 14.8 %all-to-all-start.1 = ((f32[8,16,512]{2,1,0:T(8,128)}), f32[8,16,512]{2,1,0:T(8,128)S(1)}, u32[]{:S(2)}, u32[]{:S(2)}) async-start(f32[8,16,512]{2,1,0:T(8,128)} %shard_map.48), calls=%async_computation.1 | async-start | bytes 524288 | tf_op jit(solution)/shard_map/all_to_all | solution.py:165
  111.2 0.7 copy-start.2
  112.5 10.5 %collective-permute-start.2 = (f32[2,512]{0,1:T(8,128)S(1)}, f32[2,512]{0,1:T(8,128)S(1)}, u32[]{:S(2)}, u32[]{:S(2)}) collective-permute-start(f32[2,512]{0,1:T(8,128)S(1)} %slice_select_fusion), channel_id=1, source_target_pairs={{16,0},{32,16},{48,32},{64,48},{80,64},{96,80},{112,96},{128,112},... | collective-permute-start | bytes 12296 | tf_op jit(solution)/shard_map/ppermute | solution.py:121
  117.7 11.7 %collective-permute-start.3 = (f32[2,512]{0,1:T(8,128)S(1)}, f32[2,512]{0,1:T(8,128)S(1)}, u32[]{:S(2)}, u32[]{:S(2)}) collective-permute-start(f32[2,512]{0,1:T(8,128)S(1)} %concatenate.106), channel_id=1, source_target_pairs={{0,16},{16,32},{32,48},{48,64},{64,80},{80,96},{96,112},{112,128},... | collective-permute-start | bytes 12296 | tf_op jit(solution)/shard_map/ppermute | solution.py:120

commit v12 on v8

--- a/solution.py
+++ b/solution.py
@@ -106,16 +106,14 @@
     half = scen // 2
     mine = lax.dynamic_slice_in_dim(coded, core * half, half, axis=1)
     height = mine.shape[0]
-    outgoing = jnp.concatenate(
-        [
-            greens.reshape(own_sources, parts, block).transpose(1, 0, 2),
-            jnp.broadcast_to(mine.reshape(1, -1, block), (parts, height * half // block, block)),
-        ],
-        axis=1,
-    )
-    incoming = lax.all_to_all(outgoing, SPLIT, 0, 0, tiled=True)
-    near = incoming[:, :own_sources]
-    mine = incoming[:, own_sources:].reshape(parts, height, half)
+    greens_part = greens.reshape(own_sources, parts, block).transpose(1, 0, 2).reshape(parts, own_sources * block)
+    slips_part = jnp.broadcast_to(mine.reshape(1, height * half), (parts, height * half))
+    message = own_sources * block + height * half
+    lanes = message // 16 if message % (16 * 128) == 0 else message
+    outgoing = jnp.concatenate([greens_part, slips_part], axis=1).reshape(parts, message // lanes, lanes)
+    incoming = lax.all_to_all(outgoing, SPLIT, 0, 0, tiled=True).reshape(parts, message)
+    near = incoming[:, : own_sources * block].reshape(parts, own_sources, block)
+    mine = incoming[:, own_sources * block:].reshape(parts, height, half)
     count_rows = lax.axis_size("rows")
     far = lax.ppermute(near, SHARE, [(i, (i + 1) % shares) for i in range(shares)])
     theirs = lax.ppermute(mine, "rows", [(i, i ^ 1) for i in range(count_rows)])

time: 112 us -> 110 us (0.982)
  other arithmetic: 7.61 us -> 4.7 us
  local copies, waits for them, and re-layouts: 7.04 us -> 8.54 us
  waiting for transfers between devices: 61.4 us -> 60.1 us
    unnamed x7 -> x14, local copies, waits for them, and re-layouts: 0.75 us -> 3.82 us
    all_to_all x1, waiting for transfers between devices: 31.4 us -> 30 us  [local(): lax.all_to_all(outgoing, SPLIT, 0, 0, tiled=True).reshape(parts, message)]
where the time goes in v12:
time: 110 us; the launch traced here: 108 us
  waiting for transfers between devices  60.1 us (55%)
  starting transfers between devices  25.1 us (23%)
  Pallas kernels  9.6 us (9%)
  local copies, waits for them, and re-layouts  8.54 us (8%)
  other arithmetic  4.7 us (4%)
    all_to_all x1, waiting for transfers between devices, local(): lax.all_to_all(outgoing, SPLIT, 0, 0, tiled=True).reshape(parts, message)  30 us
    all_to_all x1, waiting for transfers between devices, local(): maxima = lax.all_to_all(maxima, SPLIT, 0, 0, tiled=True)  10.6 us
    all_to_all x1, starting transfers between devices, local(): lax.all_to_all(outgoing, SPLIT, 0, 0, tiled=True).reshape(parts, message)  10.4 us
    ppermute x1, waiting for transfers between devices, local(): lax.ppermute(near, SHARE, [(i, (i + 1) % shares) for i in range(shares)])  9.98 us
    pallas_call x1, Pallas kernels, wave_maxima(): pl.pallas_call(wave_kernel, grid=(parts,), in_specs=[pl.BlockSpec((rows,...  9.6 us
    ppermute x1, waiting for transfers between devices, point_peaks(): lax.ppermute(to_right, 'rows', [(i, i + 1) for i in range(count - 1)])  6.04 us
    ppermute x1, starting transfers between devices, point_peaks(): lax.ppermute(to_left, 'rows', [(i + 1, i) for i in range(count - 1)])  3.91 us
    unnamed x14, local copies, waits for them, and re-layouts  3.82 us
  transfers between devices with their start and end apart: 6, of which 5 were waited for; matrix products, arithmetic and copies ran while one was open for 4% of the time, Pallas kernels for 0%

profile of v12, /device:TPU:6, one launch (start us, length us, event | category | flops | bytes accessed | tf_op | source)
XLA Modules:
  0.0 108.4 jit_solution(9019651226576694432)
XLA Ops:
  0.0 0.0 copy-start
  0.0 0.0 copy-start.1
  0.0 1.4 %copy.32 = bf16[4,8,8,1024]{3,2,1,0:T(8,128)(2,1)S(1)} copy(bf16[4,8,8,1024]{3,1,2,0:T(8,128)(2,1)} %bitcast.121) | data formatting | bytes 1048576
  1.4 0.0 copy-done
  1.4 0.2 fusion.1
  1.6 0.0 copy-done.1
  1.7 0.1 pad.35.clone
  1.8 0.1 fusion.9
  1.9 0.1 copy.23
  2.0 0.1 copy.33
  2.1 0.2 pad_maximum_fusion
  2.3 1.2 %copy.43 = bf16[1,8,16,4352]{3,2,1,0:T(8,128)(2,1)} copy(bf16[1,8,16,4352]{3,1,2,0:T(8,128)(2,1)S(1)} %bitcast.102) | data formatting | bytes 2228224
  3.5 0.0 copy-start.2
  3.5 10.4 %all-to-all-start = ((bf16[8,16,4352]{2,1,0:T(8,128)(2,1)}), bf16[8,16,4352]{2,1,0:T(8,128)(2,1)S(1)}, u32[]{:S(2)}, u32[]{:S(2)}) async-start(bf16[8,16,4352]{2,1,0:T(8,128)(2,1)} %bitcast.95), calls=%async_computation | async-start | bytes 2228224 | tf_op jit(solution)/shard_map/all_to_all | solution.py:114
  13.9 0.0 copy-done.2
  13.9 0.1 fusion.12
  14.0 0.1 slice_bitcast_fusion.7
  14.1 30.0 %all-to-all-done = bf16[8,16,4352]{2,1,0:T(8,128)(2,1)S(1)} async-done(((bf16[8,16,4352]{2,1,0:T(8,128)(2,1)}), bf16[8,16,4352]{2,1,0:T(8,128)(2,1)S(1)}, u32[]{:S(2)}, u32[]{:S(2)}) %all-to-all-start) | async-done | bytes 1114144 | tf_op jit(solution)/shard_map/all_to_all | solution.py:114
  44.1 0.3 copy.35
  44.5 0.3 copy.45
  44.8 3.5 %collective-permute-start = (bf16[8,32,1024]{2,1,0:T(8,128)(2,1)S(1)}, bf16[8,32,1024]{2,1,0:T(8,128)(2,1)S(1)}, u32[]{:S(2)}, u32[]{:S(2)}) collective-permute-start(bf16[8,32,1024]{2,1,0:T(8,128)(2,1)S(1)} %bitcast.116), channel_id=1, source_target_pairs={{0,1},{1,0},{2,3},{3,2},{4,5},{5,4},{6,7},{7,6},{8,9},{9,8},{10,11... | collective-permute-start | bytes 1572872 | tf_op jit(solution)/shard_map/ppermute | solution.py:118
  48.3 0.1 copy.44
  48.4 1.9 %collective-permute-start.1 = (bf16[8,144,256]{2,1,0:T(8,128)(2,1)S(1)}, bf16[8,144,256]{2,1,0:T(8,128)(2,1)S(1)}, u32[]{:S(2)}, u32[]{:S(2)}) collective-permute-start(bf16[8,144,256]{2,1,0:T(8,128)(2,1)S(1)} %bitcast.108), channel_id=1, source_target_pairs={{0,16},{16,0},{32,48},{48,32},{64,80},{80,64},{96,112},{112,96},{1... | collective-permute-start | bytes 1769480 | tf_op jit(solution)/shard_map/ppermute | solution.py:119
  50.4 0.1 slice_bitcast_fusion.4
  50.4 0.1 slice_bitcast_fusion.5
  50.5 0.1 slice_bitcast_fusion.6
  50.6 10.0 %collective-permute-done = bf16[8,32,1024]{2,1,0:T(8,128)(2,1)S(1)} collective-permute-done((bf16[8,32,1024]{2,1,0:T(8,128)(2,1)S(1)}, bf16[8,32,1024]{2,1,0:T(8,128)(2,1)S(1)}, u32[]{:S(2)}, u32[]{:S(2)}) %collective-permute-start) | collective-permute-done | bytes 524320 | tf_op jit(solution)/shard_map/ppermute | solution.py:118
  60.6 0.2 maximum_select_fusion.1
  60.7 0.1 copy.24
  60.8 1.4 %copy.25 = bf16[512,1024]{0,1:T(8,128)(2,1)} copy(bf16[512,1024]{1,0:T(8,128)(2,1)S(1)} %bitcast.107) | data formatting | bytes 2097152 | tf_op jit(solution)/shard_map/jit(_where)/select_n | solution.py:121
  62.2 0.0 collective-permute-done.1
  62.2 1.3 %maximum_select_fusion.a_ref = bf16[8,144,512]{2,1,0:T(8,128)(2,1)} fusion(bf16[8,144,256]{2,1,0:T(8,128)(2,1)S(1)} %collective-permute-done.1, bf16[8,144,256]{2,1,0:T(8,128)(2,1)S(1)} %bitcast.109, pred[]{:T(512)S(6)} %eq.75), kind=kLoop, calls=%fused_computation | loop fusion | flops 5308416 | bytes 2359297 | tf_op jit(solution)/shard_map/jit(_where)/select_n | solution.py:120
  63.5 9.6 %shard_map.46 = f32[8,16,512]{2,1,0:T(8,128)} custom-call(bf16[1024,512]{1,0:T(8,128)(2,1)} %bitcast.106, bf16[8,144,512]{2,1,0:T(8,128)(2,1)} %maximum_select_fusion.a_ref), custom_call_target="tpu_custom_call" | custom-call | tf_op jit(solution)/shard_map/pallas_call | solution.py:46
  73.1 3.4 %all-to-all-start.1 = ((f32[8,16,512]{2,1,0:T(8,128)}), f32[8,16,512]{2,1,0:T(8,128)S(1)}, u32[]{:S(2)}, u32[]{:S(2)}) async-start(f32[8,16,512]{2,1,0:T(8,128)} %shard_map.46), calls=%async_computation.1 | async-start | bytes 524288 | tf_op jit(solution)/shard_map/all_to_all | solution.py:125
  76.5 0.6 fusion.11
  77.1 0.1 maximum_compare_fusion
  77.2 0.1 compare_bitcast_fusion.7
  77.3 10.6 %all-to-all-done.1 = f32[8,16,512]{2,1,0:T(8,128)S(1)} async-done(((f32[8,16,512]{2,1,0:T(8,128)}), f32[8,16,512]{2,1,0:T(8,128)S(1)}, u32[]{:S(2)}, u32[]{:S(2)}) %all-to-all-start.1) | async-done | bytes 262176 | tf_op jit(solution)/shard_map/all_to_all | solution.py:125
  87.9 0.1 copy.27
  88.0 0.1 fusion.10
  88.2 0.1 maximum_select_fusion.13
  88.3 0.1 slice.164
  88.5 0.1 slice.165
  88.7 0.1 slice.166
  88.8 0.0 copy-start.3
  88.8 0.1 slice.167
  89.0 0.4 copy-done.3
  89.5 0.6 slice_select_fusion
  90.1 3.9 %collective-permute-start.2 = (f32[2,512]{0,1:T(8,128)S(1)}, f32[2,512]{0,1:T(8,128)S(1)}, u32[]{:S(2)}, u32[]{:S(2)}) collective-permute-start(f32[2,512]{0,1:T(8,128)S(1)} %slice_select_fusion), channel_id=1, source_target_pairs={{16,0},{32,16},{48,32},{64,48},{80,64},{96,80},{112,96},{128,112},... | collective-permute-start | bytes 12296 | tf_op jit(solution)/shard_map/ppermute | solution.py:85
  94.0 0.1 maximum_select_fusion.7
  94.2 0.1 maximum_select_fusion.6
  94.3 0.1 maximum_select_fusion.5
  94.5 0.1 maximum_select_fusion.4
  94.6 0.1 slice.175
  94.7 0.6 concatenate.106
  95.3 1.9 %collective-permute-start.3 = (f32[2,512]{0,1:T(8,128)S(1)}, f32[2,512]{0,1:T(8,128)S(1)}, u32[]{:S(2)}, u32[]{:S(2)}) collective-permute-start(f32[2,512]{0,1:T(8,128)S(1)} %concatenate.106), channel_id=1, source_target_pairs={{0,16},{16,32},{32,48},{48,64},{64,80},{80,96},{96,112},{112,128},... | collective-permute-start | bytes 12296 | tf_op jit(solution)/shard_map/ppermute | solution.py:84
  97.3 3.4 %collective-permute-done.2 = f32[2,512]{0,1:T(8,128)S(1)} collective-permute-done((f32[2,512]{0,1:T(8,128)S(1)}, f32[2,512]{0,1:T(8,128)S(1)}, u32[]{:S(2)}, u32[]{:S(2)}) %collective-permute-start.2) | collective-permute-done | bytes 4128 | tf_op jit(solution)/shard_map/ppermute | solution.py:85
  100.7 0.3 slice_reduce_fusion.3
  101.0 6.0 %collective-permute-done.3 = f32[2,512]{0,1:T(8,128)S(1)} collective-permute-done((f32[2,512]{0,1:T(8,128)S(1)}, f32[2,512]{0,1:T(8,128)S(1)}, u32[]{:S(2)}, u32[]{:S(2)}) %collective-permute-start.3) | collective-permute-done | bytes 4128 | tf_op jit(solution)/shard_map/ppermute | solution.py:84
  107.0 0.3 slice_reduce_fusion.2
  107.3 1.0 fusion.2
  (10 shorter events, 0.3 us)
Async XLA Ops:
  0.0 1.4 %copy-start = (s32[512,128]{1,0:T(8,128)S(1)}, s32[512,128]{1,0:T(8,128)}, u32[]{:S(2)}) copy-start(s32[512,128]{1,0:T(8,128)} %param.6) | copy-start | bytes 786436
  0.0 1.6 %copy-start.1 = (bf16[512,128]{1,0:T(8,128)(2,1)S(1)}, bf16[512,128]{1,0:T(8,128)(2,1)}, u32[]{:S(2)}) copy-start(bf16[512,128]{1,0:T(8,128)(2,1)} %param.5) | copy-start | bytes 393220
  3.5 10.5 %copy-start.2 = (s32[128]{0:T(128)S(1)}, s32[128]{0:T(128)}, u32[]{:S(2)}) copy-start(s32[128]{0:T(128)} %param.7) | copy-start | bytes 1540
  3.5 40.6 %all-to-all-start = ((bf16[8,16,4352]{2,1,0:T(8,128)(2,1)}), bf16[8,16,4352]{2,1,0:T(8,128)(2,1)S(1)}, u32[]{:S(2)}, u32[]{:S(2)}) async-start(bf16[8,16,4352]{2,1,0:T(8,128)(2,1)} %bitcast.95), calls=%async_computation | async-start | bytes 2228224 | tf_op jit(solution)/shard_map/all_to_all | solution.py:114
  44.8 15.7 %collective-permute-start = (bf16[8,32,1024]{2,1,0:T(8,128)(2,1)S(1)}, bf16[8,32,1024]{2,1,0:T(8,128)(2,1)S(1)}, u32[]{:S(2)}, u32[]{:S(2)}) collective-permute-start(bf16[8,32,1024]{2,1,0:T(8,128)(2,1)S(1)} %bitcast.116), channel_id=1, source_target_pairs={{0,1},{1,0},{2,3},{3,2},{4,5},{5,4},{6,7},{7,6},{8,9},{9,8},{10,11... | collective-permute-start | bytes 1572872 | tf_op jit(solution)/shard_map/ppermute | solution.py:118
  48.4 13.7 %collective-permute-start.1 = (bf16[8,144,256]{2,1,0:T(8,128)(2,1)S(1)}, bf16[8,144,256]{2,1,0:T(8,128)(2,1)S(1)}, u32[]{:S(2)}, u32[]{:S(2)}) collective-permute-start(bf16[8,144,256]{2,1,0:T(8,128)(2,1)S(1)} %bitcast.108), channel_id=1, source_target_pairs={{0,16},{16,0},{32,48},{48,32},{64,80},{80,64},{96,112},{112,96},{1... | collective-permute-start | bytes 1769480 | tf_op jit(solution)/shard_map/ppermute | solution.py:119
  73.1 14.8 %all-to-all-start.1 = ((f32[8,16,512]{2,1,0:T(8,128)}), f32[8,16,512]{2,1,0:T(8,128)S(1)}, u32[]{:S(2)}, u32[]{:S(2)}) async-start(f32[8,16,512]{2,1,0:T(8,128)} %shard_map.46), calls=%async_computation.1 | async-start | bytes 524288 | tf_op jit(solution)/shard_map/all_to_all | solution.py:125
  88.8 0.7 copy-start.3
  90.1 10.6 %collective-permute-start.2 = (f32[2,512]{0,1:T(8,128)S(1)}, f32[2,512]{0,1:T(8,128)S(1)}, u32[]{:S(2)}, u32[]{:S(2)}) collective-permute-start(f32[2,512]{0,1:T(8,128)S(1)} %slice_select_fusion), channel_id=1, source_target_pairs={{16,0},{32,16},{48,32},{64,48},{80,64},{96,80},{112,96},{128,112},... | collective-permute-start | bytes 12296 | tf_op jit(solution)/shard_map/ppermute | solution.py:85
  95.3 11.7 %collective-permute-start.3 = (f32[2,512]{0,1:T(8,128)S(1)}, f32[2,512]{0,1:T(8,128)S(1)}, u32[]{:S(2)}, u32[]{:S(2)}) collective-permute-start(f32[2,512]{0,1:T(8,128)S(1)} %concatenate.106), channel_id=1, source_target_pairs={{0,16},{16,32},{32,48},{48,64},{64,80},{80,96},{96,112},{112,128},... | collective-permute-start | bytes 12296 | tf_op jit(solution)/shard_map/ppermute | solution.py:84

commit v13 on v12

--- a/solution.py
+++ b/solution.py
@@ -96,24 +96,34 @@
     scen = slip_values.shape[0]
     block = rows // parts
 
+    core = lax.rem(lax.axis_index("rows"), 2)
+    side = lax.axis_index(SHARE)
+    half = scen // 2
+    slots = slip_values.shape[1]
     listed = rupture_ids >= 0
     values = jnp.where(listed, slip_values, jnp.zeros_like(slip_values))
     starts = jnp.maximum(rupture_ids[:, 0], 0)
+    values = lax.dynamic_slice_in_dim(values, core * half, half, axis=0)
+    starts = lax.dynamic_slice_in_dim(starts, core * half, half)
     code = jnp.stack([starts // CODE, starts % CODE]).astype(jnp.bfloat16)
-    coded = jnp.concatenate([values.T, code, jnp.zeros((14, scen), jnp.bfloat16)], axis=0)
-    core = lax.rem(lax.axis_index("rows"), 2)
-    side = lax.axis_index(SHARE)
-    half = scen // 2
-    mine = lax.dynamic_slice_in_dim(coded, core * half, half, axis=1)
-    height = mine.shape[0]
     greens_part = greens.reshape(own_sources, parts, block).transpose(1, 0, 2).reshape(parts, own_sources * block)
-    slips_part = jnp.broadcast_to(mine.reshape(1, height * half), (parts, height * half))
-    message = own_sources * block + height * half
-    lanes = message // 16 if message % (16 * 128) == 0 else message
-    outgoing = jnp.concatenate([greens_part, slips_part], axis=1).reshape(parts, message // lanes, lanes)
+    slip_part = jnp.concatenate([values.reshape(-1), code.reshape(-1)])
+    used = own_sources * block + slip_part.shape[0]
+    message = -(-used // (16 * 128)) * (16 * 128)
+    outgoing = jnp.concatenate(
+        [
+            greens_part,
+            jnp.broadcast_to(slip_part[None], (parts, slip_part.shape[0])),
+            jnp.zeros((parts, message - used), jnp.bfloat16),
+        ],
+        axis=1,
+    ).reshape(parts, 16, message // 16)
     incoming = lax.all_to_all(outgoing, SPLIT, 0, 0, tiled=True).reshape(parts, message)
     near = incoming[:, : own_sources * block].reshape(parts, own_sources, block)
-    mine = incoming[:, own_sources * block:].reshape(parts, height, half)
+    got = incoming[:, own_sources * block: used]
+    got_values = got[:, : half * slots].reshape(parts, half, slots).transpose(0, 2, 1)
+    got_code = got[:, half * slots:].reshape(parts, 2, half)
+    mine = jnp.concatenate([got_values, got_code, jnp.zeros((parts, 14, half), jnp.bfloat16)], axis=1)
     count_rows = lax.axis_size("rows")
     far = lax.ppermute(near, SHARE, [(i, (i + 1) % shares) for i in range(shares)])
     theirs = lax.ppermute(mine, "rows", [(i, i ^ 1) for i in range(count_rows)])

time: 110 us -> 114 us (1.036); the launches traced: 108 us -> 114 us
  waiting for transfers between devices: 60.1 us -> 63.3 us
  other arithmetic: 4.7 us -> 6.54 us
    ppermute x1, waiting for transfers between devices: 9.98 us -> 12.5 us  [local(): lax.ppermute(near, SHARE, [(i, (i + 1) % shares) for i in range(shares)])]
    unnamed x14 -> x11, local copies, waits for them, and re-layouts: 3.82 us -> 3.49 us
where the time goes in v13:
time: 114 us
  waiting for transfers between devices  63.3 us (56%)
  starting transfers between devices  25.6 us (22%)
  Pallas kernels  9.6 us (8%)
  local copies, waits for them, and re-layouts  8.32 us (7%)
  other arithmetic  6.54 us (6%)
    all_to_all x1, waiting for transfers between devices, local(): lax.all_to_all(outgoing, SPLIT, 0, 0, tiled=True).reshape(parts, message)  29.3 us
    ppermute x1, waiting for transfers between devices, local(): lax.ppermute(near, SHARE, [(i, (i + 1) % shares) for i in range(shares)])  12.5 us
    all_to_all x1, waiting for transfers between devices, local(): maxima = lax.all_to_all(maxima, SPLIT, 0, 0, tiled=True)  11.1 us
    all_to_all x1, starting transfers between devices, local(): lax.all_to_all(outgoing, SPLIT, 0, 0, tiled=True).reshape(parts, message)  10.4 us
    pallas_call x1, Pallas kernels, wave_maxima(): pl.pallas_call(wave_kernel, grid=(parts,), in_specs=[pl.BlockSpec((rows,...  9.6 us
    ppermute x1, waiting for transfers between devices, point_peaks(): lax.ppermute(to_right, 'rows', [(i, i + 1) for i in range(count - 1)])  7.01 us
    ppermute x1, starting transfers between devices, point_peaks(): lax.ppermute(to_left, 'rows', [(i + 1, i) for i in range(count - 1)])  4.36 us
    unnamed x11, local copies, waits for them, and re-layouts  3.49 us
  transfers between devices with their start and end apart: 6, of which 5 were waited for; matrix products, arithmetic and copies ran while one was open for 4% of the time, Pallas kernels for 0%

profile of v13, /device:TPU:6, one launch (start us, length us, event | category | flops | bytes accessed | tf_op | source)
XLA Modules:
  0.0 113.6 jit_solution(16466371223297862968)
XLA Ops:
  0.0 1.0 fusion.1
  1.1 0.9 fusion.3
  2.0 1.3 %copy.32 = bf16[4,8,8,1024]{3,2,1,0:T(8,128)(2,1)S(1)} copy(bf16[4,8,8,1024]{3,1,2,0:T(8,128)(2,1)} %bitcast.105) | data formatting | bytes 1048576
  3.4 0.3 maximum_maximum_fusion
  3.7 1.1 copy.43
  4.8 0.0 copy-start
  4.8 10.4 %all-to-all-start = ((bf16[8,16,4224]{2,1,0:T(8,128)(2,1)}), bf16[8,16,4224]{2,1,0:T(8,128)(2,1)S(1)}, u32[]{:S(2)}, u32[]{:S(2)}) async-start(bf16[8,16,4224]{2,1,0:T(8,128)(2,1)} %bitcast.78), calls=%async_computation | async-start | bytes 2162688 | tf_op jit(solution)/shard_map/all_to_all | solution.py:121
  15.3 0.0 copy-done
  15.3 0.1 fusion.8
  15.4 0.1 slice_bitcast_fusion.8
  15.4 29.3 %all-to-all-done = bf16[8,16,4224]{2,1,0:T(8,128)(2,1)S(1)} async-done(((bf16[8,16,4224]{2,1,0:T(8,128)(2,1)}), bf16[8,16,4224]{2,1,0:T(8,128)(2,1)S(1)}, u32[]{:S(2)}, u32[]{:S(2)}) %all-to-all-start) | async-done | bytes 1081376 | tf_op jit(solution)/shard_map/all_to_all | solution.py:121
  44.7 0.2 copy.35
  44.9 0.1 slice_bitcast_fusion
  45.0 0.1 copy.44
  45.1 0.2 copy.25
  45.3 0.1 pad_maximum_fusion
  45.4 1.9 %collective-permute-start.1 = (bf16[8,144,256]{2,1,0:T(8,128)(2,1)S(1)}, bf16[8,144,256]{2,1,0:T(8,128)(2,1)S(1)}, u32[]{:S(2)}, u32[]{:S(2)}) collective-permute-start(bf16[8,144,256]{2,1,0:T(8,128)(2,1)S(1)} %pad_maximum_fusion), channel_id=1, source_target_pairs={{0,16},{16,0},{32,48},{48,32},{64,80},{80,64},{96,112},{112,96},{1... | collective-permute-start | bytes 1769480 | tf_op jit(solution)/shard_map/ppermute | solution.py:129
  47.3 0.3 copy.45
  47.6 3.5 %collective-permute-start = (bf16[8,32,1024]{2,1,0:T(8,128)(2,1)S(1)}, bf16[8,32,1024]{2,1,0:T(8,128)(2,1)S(1)}, u32[]{:S(2)}, u32[]{:S(2)}) collective-permute-start(bf16[8,32,1024]{2,1,0:T(8,128)(2,1)S(1)} %bitcast.98), channel_id=1, source_target_pairs={{0,1},{1,0},{2,3},{3,2},{4,5},{5,4},{6,7},{7,6},{8,9},{9,8},{10,11... | collective-permute-start | bytes 1572872 | tf_op jit(solution)/shard_map/ppermute | solution.py:128
  51.1 0.1 slice_bitcast_fusion.7
  51.2 0.1 slice_bitcast_fusion.6
  51.2 0.1 slice_bitcast_fusion.5
  51.3 12.5 %collective-permute-done = bf16[8,32,1024]{2,1,0:T(8,128)(2,1)S(1)} collective-permute-done((bf16[8,32,1024]{2,1,0:T(8,128)(2,1)S(1)}, bf16[8,32,1024]{2,1,0:T(8,128)(2,1)S(1)}, u32[]{:S(2)}, u32[]{:S(2)}) %collective-permute-start) | collective-permute-done | bytes 524320 | tf_op jit(solution)/shard_map/ppermute | solution.py:128
  63.8 0.2 maximum_select_fusion.1
  64.0 0.1 copy.23
  64.1 1.4 %copy.24 = bf16[512,1024]{0,1:T(8,128)(2,1)} copy(bf16[512,1024]{1,0:T(8,128)(2,1)S(1)} %bitcast.93) | data formatting | bytes 2097152 | tf_op jit(solution)/shard_map/jit(_where)/select_n | solution.py:131
  65.4 0.0 collective-permute-done.1
  65.4 1.3 %maximum_select_fusion.a_ref = bf16[8,144,512]{2,1,0:T(8,128)(2,1)} fusion(bf16[8,144,256]{2,1,0:T(8,128)(2,1)S(1)} %collective-permute-done.1, bf16[8,14,256]{2,1,0:T(8,128)(2,1)S(1)} %broadcast_in_dim.110, bf16[8,2,256]{2,1,0:T(2,128)(2,1)S(1)} %reshape.75, bf16[8,128,256]{2,1,0:T(8,128)(2,1)S(1)} %bitcast.87, pred[]{:T(512)S(6)} %eq.75), kind=kLoop, calls=%fused_computation | loop fusion | flops 10027008 | bytes 2359297 | tf_op jit(solution)/shard_map/jit(_where)/select_n | solution.py:130
  66.8 9.6 %shard_map.46 = f32[8,16,512]{2,1,0:T(8,128)} custom-call(bf16[1024,512]{1,0:T(8,128)(2,1)} %bitcast.92, bf16[8,144,512]{2,1,0:T(8,128)(2,1)} %maximum_select_fusion.a_ref), custom_call_target="tpu_custom_call" | custom-call | tf_op jit(solution)/shard_map/pallas_call | solution.py:46
  76.4 3.4 %all-to-all-start.1 = ((f32[8,16,512]{2,1,0:T(8,128)}), f32[8,16,512]{2,1,0:T(8,128)S(1)}, u32[]{:S(2)}, u32[]{:S(2)}) async-start(f32[8,16,512]{2,1,0:T(8,128)} %shard_map.46), calls=%async_computation.1 | async-start | bytes 524288 | tf_op jit(solution)/shard_map/all_to_all | solution.py:135
  79.8 0.6 fusion.7
  80.4 0.1 maximum_compare_fusion
  80.5 0.1 compare_bitcast_fusion.7
  80.6 11.1 %all-to-all-done.1 = f32[8,16,512]{2,1,0:T(8,128)S(1)} async-done(((f32[8,16,512]{2,1,0:T(8,128)}), f32[8,16,512]{2,1,0:T(8,128)S(1)}, u32[]{:S(2)}, u32[]{:S(2)}) %all-to-all-start.1) | async-done | bytes 262176 | tf_op jit(solution)/shard_map/all_to_all | solution.py:135
  91.7 0.1 copy.27
  91.8 0.1 fusion.6
  92.0 0.1 maximum_select_fusion.13
  92.1 0.1 slice.172
  92.3 0.1 slice.173
  92.4 0.1 slice.174
  92.6 0.0 copy-start.1
  92.6 0.1 slice.175
  92.8 0.4 copy-done.1
  93.2 0.7 slice_select_fusion
  93.9 4.4 %collective-permute-start.2 = (f32[2,512]{0,1:T(8,128)S(1)}, f32[2,512]{0,1:T(8,128)S(1)}, u32[]{:S(2)}, u32[]{:S(2)}) collective-permute-start(f32[2,512]{0,1:T(8,128)S(1)} %slice_select_fusion), channel_id=1, source_target_pairs={{16,0},{32,16},{48,32},{64,48},{80,64},{96,80},{112,96},{128,112},... | collective-permute-start | bytes 12296 | tf_op jit(solution)/shard_map/ppermute | solution.py:85
  98.3 0.1 maximum_select_fusion.7
  98.4 0.1 maximum_select_fusion.6
  98.6 0.1 maximum_select_fusion.5
  98.7 0.1 maximum_select_fusion.4
  98.8 0.1 slice.183
  99.0 0.7 concatenate.109
  99.6 1.9 %collective-permute-start.3 = (f32[2,512]{0,1:T(8,128)S(1)}, f32[2,512]{0,1:T(8,128)S(1)}, u32[]{:S(2)}, u32[]{:S(2)}) collective-permute-start(f32[2,512]{0,1:T(8,128)S(1)} %concatenate.109), channel_id=1, source_target_pairs={{0,16},{16,32},{32,48},{48,64},{64,80},{80,96},{96,112},{112,128},... | collective-permute-start | bytes 12296 | tf_op jit(solution)/shard_map/ppermute | solution.py:84
  101.6 3.4 %collective-permute-done.2 = f32[2,512]{0,1:T(8,128)S(1)} collective-permute-done((f32[2,512]{0,1:T(8,128)S(1)}, f32[2,512]{0,1:T(8,128)S(1)}, u32[]{:S(2)}, u32[]{:S(2)}) %collective-permute-start.2) | collective-permute-done | bytes 4128 | tf_op jit(solution)/shard_map/ppermute | solution.py:85
  105.0 0.3 slice_reduce_fusion.3
  105.3 7.0 %collective-permute-done.3 = f32[2,512]{0,1:T(8,128)S(1)} collective-permute-done((f32[2,512]{0,1:T(8,128)S(1)}, f32[2,512]{0,1:T(8,128)S(1)}, u32[]{:S(2)}, u32[]{:S(2)}) %collective-permute-start.3) | collective-permute-done | bytes 4128 | tf_op jit(solution)/shard_map/ppermute | solution.py:84
  112.3 0.3 slice_reduce_fusion.2
  112.6 1.0 fusion
  (16 shorter events, 0.2 us)
Async XLA Ops:
  4.8 10.5 %copy-start = (s32[128]{0:T(128)S(1)}, s32[128]{0:T(128)}, u32[]{:S(2)}) copy-start(s32[128]{0:T(128)} %param.7) | copy-start | bytes 1540
  4.8 39.9 %all-to-all-start = ((bf16[8,16,4224]{2,1,0:T(8,128)(2,1)}), bf16[8,16,4224]{2,1,0:T(8,128)(2,1)S(1)}, u32[]{:S(2)}, u32[]{:S(2)}) async-start(bf16[8,16,4224]{2,1,0:T(8,128)(2,1)} %bitcast.78), calls=%async_computation | async-start | bytes 2162688 | tf_op jit(solution)/shard_map/all_to_all | solution.py:121
  45.4 20.1 %collective-permute-start.1 = (bf16[8,144,256]{2,1,0:T(8,128)(2,1)S(1)}, bf16[8,144,256]{2,1,0:T(8,128)(2,1)S(1)}, u32[]{:S(2)}, u32[]{:S(2)}) collective-permute-start(bf16[8,144,256]{2,1,0:T(8,128)(2,1)S(1)} %pad_maximum_fusion), channel_id=1, source_target_pairs={{0,16},{16,0},{32,48},{48,32},{64,80},{80,64},{96,112},{112,96},{1... | collective-permute-start | bytes 1769480 | tf_op jit(solution)/shard_map/ppermute | solution.py:129
  47.6 16.2 %collective-permute-start = (bf16[8,32,1024]{2,1,0:T(8,128)(2,1)S(1)}, bf16[8,32,1024]{2,1,0:T(8,128)(2,1)S(1)}, u32[]{:S(2)}, u32[]{:S(2)}) collective-permute-start(bf16[8,32,1024]{2,1,0:T(8,128)(2,1)S(1)} %bitcast.98), channel_id=1, source_target_pairs={{0,1},{1,0},{2,3},{3,2},{4,5},{5,4},{6,7},{7,6},{8,9},{9,8},{10,11... | collective-permute-start | bytes 1572872 | tf_op jit(solution)/shard_map/ppermute | solution.py:128
  76.4 15.3 %all-to-all-start.1 = ((f32[8,16,512]{2,1,0:T(8,128)}), f32[8,16,512]{2,1,0:T(8,128)S(1)}, u32[]{:S(2)}, u32[]{:S(2)}) async-start(f32[8,16,512]{2,1,0:T(8,128)} %shard_map.46), calls=%async_computation.1 | async-start | bytes 524288 | tf_op jit(solution)/shard_map/all_to_all | solution.py:135
  92.6 0.7 copy-start.1
  93.9 11.1 %collective-permute-start.2 = (f32[2,512]{0,1:T(8,128)S(1)}, f32[2,512]{0,1:T(8,128)S(1)}, u32[]{:S(2)}, u32[]{:S(2)}) collective-permute-start(f32[2,512]{0,1:T(8,128)S(1)} %slice_select_fusion), channel_id=1, source_target_pairs={{16,0},{32,16},{48,32},{64,48},{80,64},{96,80},{112,96},{128,112},... | collective-permute-start | bytes 12296 | tf_op jit(solution)/shard_map/ppermute | solution.py:85
  99.6 12.7 %collective-permute-start.3 = (f32[2,512]{0,1:T(8,128)S(1)}, f32[2,512]{0,1:T(8,128)S(1)}, u32[]{:S(2)}, u32[]{:S(2)}) collective-permute-start(f32[2,512]{0,1:T(8,128)S(1)} %concatenate.109), channel_id=1, source_target_pairs={{0,16},{16,32},{32,48},{48,64},{64,80},{80,96},{96,112},{112,128},... | collective-permute-start | bytes 12296 | tf_op jit(solution)/shard_map/ppermute | solution.py:84

commit v14 on v12

--- a/solution.py
+++ b/solution.py
@@ -100,7 +100,7 @@
     values = jnp.where(listed, slip_values, jnp.zeros_like(slip_values))
     starts = jnp.maximum(rupture_ids[:, 0], 0)
     code = jnp.stack([starts // CODE, starts % CODE]).astype(jnp.bfloat16)
-    coded = jnp.concatenate([values.T, code, jnp.zeros((14, scen), jnp.bfloat16)], axis=0)
+    coded = jnp.concatenate([values.T, code], axis=0)
     core = lax.rem(lax.axis_index("rows"), 2)
     side = lax.axis_index(SHARE)
     half = scen // 2
@@ -108,16 +108,19 @@
     height = mine.shape[0]
     greens_part = greens.reshape(own_sources, parts, block).transpose(1, 0, 2).reshape(parts, own_sources * block)
     slips_part = jnp.broadcast_to(mine.reshape(1, height * half), (parts, height * half))
-    message = own_sources * block + height * half
-    lanes = message // 16 if message % (16 * 128) == 0 else message
-    outgoing = jnp.concatenate([greens_part, slips_part], axis=1).reshape(parts, message // lanes, lanes)
+    used = own_sources * block + height * half
+    message = -(-used // (16 * 128)) * (16 * 128)
+    outgoing = jnp.concatenate(
+        [greens_part, slips_part, jnp.zeros((parts, message - used), jnp.bfloat16)], axis=1
+    ).reshape(parts, 16, message // 16)
     incoming = lax.all_to_all(outgoing, SPLIT, 0, 0, tiled=True).reshape(parts, message)
     near = incoming[:, : own_sources * block].reshape(parts, own_sources, block)
-    mine = incoming[:, own_sources * block:].reshape(parts, height, half)
+    mine = incoming[:, own_sources * block: used].reshape(parts, height, half)
     count_rows = lax.axis_size("rows")
     far = lax.ppermute(near, SHARE, [(i, (i + 1) % shares) for i in range(shares)])
     theirs = lax.ppermute(mine, "rows", [(i, i ^ 1) for i in range(count_rows)])
     coded = jnp.where(core == 0, jnp.concatenate([mine, theirs], axis=2), jnp.concatenate([theirs, mine], axis=2))
+    coded = jnp.pad(coded, ((0, 0), (0, 16 - (height - slip_values.shape[1])), (0, 0)))
     panel = jnp.where(side == 0, jnp.stack([near, far], axis=1), jnp.stack([far, near], axis=1))
     panel_t = panel.reshape(width, block).T
 

time: 110 us -> 109 us (level)
    pad x0 -> x1, local copies, waits for them, and re-layouts: none -> 1.14 us  [local(): jnp.pad(coded, ((0, 0), (0, 16 - (height - slip_values.shape[1])), (0, 0)))]
    unnamed x14 -> x12, local copies, waits for them, and re-layouts: 3.82 us -> 3.41 us
where the time goes in v14:
time: 109 us; the launch traced here: 108 us
  waiting for transfers between devices  59.3 us (54%)
  starting transfers between devices  25.1 us (23%)
  Pallas kernels  9.6 us (9%)
  local copies, waits for them, and re-layouts  9.45 us (9%)
  other arithmetic  3.85 us (4%)
    all_to_all x1, waiting for transfers between devices, local(): lax.all_to_all(outgoing, SPLIT, 0, 0, tiled=True).reshape(parts, message)  29.3 us
    all_to_all x1, waiting for transfers between devices, local(): maxima = lax.all_to_all(maxima, SPLIT, 0, 0, tiled=True)  10.6 us
    all_to_all x1, starting transfers between devices, local(): lax.all_to_all(outgoing, SPLIT, 0, 0, tiled=True).reshape(parts, message)  10.4 us
    ppermute x1, waiting for transfers between devices, local(): lax.ppermute(near, SHARE, [(i, (i + 1) % shares) for i in range(shares)])  9.95 us
    pallas_call x1, Pallas kernels, wave_maxima(): pl.pallas_call(wave_kernel, grid=(parts,), in_specs=[pl.BlockSpec((rows,...  9.6 us
    ppermute x1, waiting for transfers between devices, point_peaks(): lax.ppermute(to_right, 'rows', [(i, i + 1) for i in range(count - 1)])  6.04 us
    ppermute x1, starting transfers between devices, point_peaks(): lax.ppermute(to_left, 'rows', [(i + 1, i) for i in range(count - 1)])  3.91 us
    ppermute x1, starting transfers between devices, local(): lax.ppermute(near, SHARE, [(i, (i + 1) % shares) for i in range(shares)])  3.48 us
  transfers between devices with their start and end apart: 6, of which 5 were waited for; matrix products, arithmetic and copies ran while one was open for 4% of the time, Pallas kernels for 0%

profile of v14, /device:TPU:6, one launch (start us, length us, event | category | flops | bytes accessed | tf_op | source)
XLA Modules:
  0.0 107.7 jit_solution(3933718939732053571)
XLA Ops:
  0.0 0.0 copy-start
  0.0 0.0 copy-start.1
  0.0 1.4 %copy.39 = bf16[4,8,8,1024]{3,2,1,0:T(8,128)(2,1)S(1)} copy(bf16[4,8,8,1024]{3,1,2,0:T(8,128)(2,1)} %bitcast.115) | data formatting | bytes 1048576
  1.4 0.0 copy-done
  1.4 0.2 fusion.1
  1.6 0.0 copy-done.1
  1.7 0.1 fusion.8
  1.8 0.1 copy.26
  2.0 0.3 maximum_maximum_fusion
  2.3 1.1 %copy.47 = bf16[1,8,16,4224]{3,2,1,0:T(8,128)(2,1)} copy(bf16[1,8,16,4224]{3,1,2,0:T(8,128)(2,1)S(1)} %bitcast.97) | data formatting | bytes 2162688
  3.4 0.0 copy-start.2
  3.4 10.4 %all-to-all-start = ((bf16[8,16,4224]{2,1,0:T(8,128)(2,1)}), bf16[8,16,4224]{2,1,0:T(8,128)(2,1)S(1)}, u32[]{:S(2)}, u32[]{:S(2)}) async-start(bf16[8,16,4224]{2,1,0:T(8,128)(2,1)} %bitcast.91), calls=%async_computation | async-start | bytes 2162688 | tf_op jit(solution)/shard_map/all_to_all | solution.py:116
  13.9 0.0 copy-done.2
  13.9 0.1 fusion.11
  14.0 0.1 slice_bitcast_fusion.7
  14.0 29.3 %all-to-all-done = bf16[8,16,4224]{2,1,0:T(8,128)(2,1)S(1)} async-done(((bf16[8,16,4224]{2,1,0:T(8,128)(2,1)}), bf16[8,16,4224]{2,1,0:T(8,128)(2,1)S(1)}, u32[]{:S(2)}, u32[]{:S(2)}) %all-to-all-start) | async-done | bytes 1081376 | tf_op jit(solution)/shard_map/all_to_all | solution.py:116
  43.3 0.2 copy.41
  43.5 0.3 copy.48
  43.8 3.5 %collective-permute-start = (bf16[8,32,1024]{2,1,0:T(8,128)(2,1)S(1)}, bf16[8,32,1024]{2,1,0:T(8,128)(2,1)S(1)}, u32[]{:S(2)}, u32[]{:S(2)}) collective-permute-start(bf16[8,32,1024]{2,1,0:T(8,128)(2,1)S(1)} %bitcast.110), channel_id=1, source_target_pairs={{0,1},{1,0},{2,3},{3,2},{4,5},{5,4},{6,7},{7,6},{8,9},{9,8},{10,11... | collective-permute-start | bytes 1572872 | tf_op jit(solution)/shard_map/ppermute | solution.py:120
  47.3 0.1 slice_bitcast_fusion.4
  47.4 1.9 %collective-permute-start.1 = (bf16[8,130,256]{2,0,1:T(8,128)(2,1)S(1)}, bf16[8,130,256]{2,0,1:T(8,128)(2,1)S(1)}, u32[]{:S(2)}, u32[]{:S(2)}) collective-permute-start(bf16[8,130,256]{2,0,1:T(8,128)(2,1)S(1)} %bitcast.107), channel_id=1, source_target_pairs={{0,16},{16,0},{32,48},{48,32},{64,80},{80,64},{96,112},{112,96},{1... | collective-permute-start | bytes 1597448 | tf_op jit(solution)/shard_map/ppermute | solution.py:121
  49.4 0.1 slice_bitcast_fusion.5
  49.4 0.1 slice_bitcast_fusion.6
  49.5 0.1 copy.29
  49.6 10.0 %collective-permute-done = bf16[8,32,1024]{2,1,0:T(8,128)(2,1)S(1)} collective-permute-done((bf16[8,32,1024]{2,1,0:T(8,128)(2,1)S(1)}, bf16[8,32,1024]{2,1,0:T(8,128)(2,1)S(1)}, u32[]{:S(2)}, u32[]{:S(2)}) %collective-permute-start) | collective-permute-done | bytes 524320 | tf_op jit(solution)/shard_map/ppermute | solution.py:120
  59.6 0.2 maximum_select_fusion.1
  59.8 0.1 copy.27
  59.9 1.4 %copy.28 = bf16[512,1024]{0,1:T(8,128)(2,1)} copy(bf16[512,1024]{1,0:T(8,128)(2,1)S(1)} %bitcast.102) | data formatting | bytes 2097152 | tf_op jit(solution)/shard_map/jit(_where)/select_n | solution.py:124
  61.2 0.0 collective-permute-done.1
  61.2 0.1 copy.30
  61.3 0.3 maximum_select_fusion
  61.6 1.1 %pad.24.a_ref = bf16[8,144,512]{2,1,0:T(8,128)(2,1)} pad(bf16[8,130,512]{2,1,0:T(8,128)(2,1)S(1)} %maximum_select_fusion, bf16[]{:T(256)} %constant.63.clone.1), padding=0_0x0_14x0_0 | pad | bytes 2244610 | tf_op jit(solution)/shard_map/jit(_pad)/pad | solution.py:123
  62.8 9.6 %shard_map.46 = f32[8,16,512]{2,1,0:T(8,128)} custom-call(bf16[1024,512]{1,0:T(8,128)(2,1)} %bitcast.101, bf16[8,144,512]{2,1,0:T(8,128)(2,1)} %pad.24.a_ref), custom_call_target="tpu_custom_call" | custom-call | tf_op jit(solution)/shard_map/pallas_call | solution.py:46
  72.4 3.4 %all-to-all-start.1 = ((f32[8,16,512]{2,1,0:T(8,128)}), f32[8,16,512]{2,1,0:T(8,128)S(1)}, u32[]{:S(2)}, u32[]{:S(2)}) async-start(f32[8,16,512]{2,1,0:T(8,128)} %shard_map.46), calls=%async_computation.1 | async-start | bytes 524288 | tf_op jit(solution)/shard_map/all_to_all | solution.py:128
  75.8 0.6 fusion.10
  76.4 0.1 maximum_compare_fusion
  76.5 0.1 compare_bitcast_fusion.7
  76.6 10.6 %all-to-all-done.1 = f32[8,16,512]{2,1,0:T(8,128)S(1)} async-done(((f32[8,16,512]{2,1,0:T(8,128)}), f32[8,16,512]{2,1,0:T(8,128)S(1)}, u32[]{:S(2)}, u32[]{:S(2)}) %all-to-all-start.1) | async-done | bytes 262176 | tf_op jit(solution)/shard_map/all_to_all | solution.py:128
  87.2 0.1 copy.34
  87.3 0.1 fusion.9
  87.5 0.1 maximum_select_fusion.13
  87.6 0.1 slice.164
  87.8 0.1 slice.165
  88.0 0.1 slice.166
  88.1 0.0 copy-start.3
  88.1 0.1 slice.167
  88.3 0.4 copy-done.3
  88.8 0.6 slice_select_fusion
  89.4 3.9 %collective-permute-start.2 = (f32[2,512]{0,1:T(8,128)S(1)}, f32[2,512]{0,1:T(8,128)S(1)}, u32[]{:S(2)}, u32[]{:S(2)}) collective-permute-start(f32[2,512]{0,1:T(8,128)S(1)} %slice_select_fusion), channel_id=1, source_target_pairs={{16,0},{32,16},{48,32},{64,48},{80,64},{96,80},{112,96},{128,112},... | collective-permute-start | bytes 12296 | tf_op jit(solution)/shard_map/ppermute | solution.py:85
  93.3 0.1 maximum_select_fusion.7
  93.5 0.1 maximum_select_fusion.6
  93.6 0.1 maximum_select_fusion.5
  93.7 0.1 maximum_select_fusion.4
  93.9 0.1 slice.175
  94.0 0.6 concatenate.106
  94.6 1.9 %collective-permute-start.3 = (f32[2,512]{0,1:T(8,128)S(1)}, f32[2,512]{0,1:T(8,128)S(1)}, u32[]{:S(2)}, u32[]{:S(2)}) collective-permute-start(f32[2,512]{0,1:T(8,128)S(1)} %concatenate.106), channel_id=1, source_target_pairs={{0,16},{16,32},{32,48},{48,64},{64,80},{80,96},{96,112},{112,128},... | collective-permute-start | bytes 12296 | tf_op jit(solution)/shard_map/ppermute | solution.py:84
  96.5 3.4 %collective-permute-done.2 = f32[2,512]{0,1:T(8,128)S(1)} collective-permute-done((f32[2,512]{0,1:T(8,128)S(1)}, f32[2,512]{0,1:T(8,128)S(1)}, u32[]{:S(2)}, u32[]{:S(2)}) %collective-permute-start.2) | collective-permute-done | bytes 4128 | tf_op jit(solution)/shard_map/ppermute | solution.py:85
  100.0 0.3 slice_reduce_fusion.3
  100.3 6.0 %collective-permute-done.3 = f32[2,512]{0,1:T(8,128)S(1)} collective-permute-done((f32[2,512]{0,1:T(8,128)S(1)}, f32[2,512]{0,1:T(8,128)S(1)}, u32[]{:S(2)}, u32[]{:S(2)}) %collective-permute-start.3) | collective-permute-done | bytes 4128 | tf_op jit(solution)/shard_map/ppermute | solution.py:84
  106.3 0.3 slice_reduce_fusion.2
  106.6 1.0 fusion.2
  (12 shorter events, 0.3 us)
Async XLA Ops:
  0.0 1.4 %copy-start = (s32[512,128]{1,0:T(8,128)S(1)}, s32[512,128]{1,0:T(8,128)}, u32[]{:S(2)}) copy-start(s32[512,128]{1,0:T(8,128)} %param.6) | copy-start | bytes 786436
  0.0 1.6 %copy-start.1 = (bf16[512,128]{1,0:T(8,128)(2,1)S(1)}, bf16[512,128]{1,0:T(8,128)(2,1)}, u32[]{:S(2)}) copy-start(bf16[512,128]{1,0:T(8,128)(2,1)} %param.5) | copy-start | bytes 393220
  3.4 10.5 %copy-start.2 = (s32[128]{0:T(128)S(1)}, s32[128]{0:T(128)}, u32[]{:S(2)}) copy-start(s32[128]{0:T(128)} %param.7) | copy-start | bytes 1540
  3.4 39.9 %all-to-all-start = ((bf16[8,16,4224]{2,1,0:T(8,128)(2,1)}), bf16[8,16,4224]{2,1,0:T(8,128)(2,1)S(1)}, u32[]{:S(2)}, u32[]{:S(2)}) async-start(bf16[8,16,4224]{2,1,0:T(8,128)(2,1)} %bitcast.91), calls=%async_computation | async-start | bytes 2162688 | tf_op jit(solution)/shard_map/all_to_all | solution.py:116
  43.8 15.7 %collective-permute-start = (bf16[8,32,1024]{2,1,0:T(8,128)(2,1)S(1)}, bf16[8,32,1024]{2,1,0:T(8,128)(2,1)S(1)}, u32[]{:S(2)}, u32[]{:S(2)}) collective-permute-start(bf16[8,32,1024]{2,1,0:T(8,128)(2,1)S(1)} %bitcast.110), channel_id=1, source_target_pairs={{0,1},{1,0},{2,3},{3,2},{4,5},{5,4},{6,7},{7,6},{8,9},{9,8},{10,11... | collective-permute-start | bytes 1572872 | tf_op jit(solution)/shard_map/ppermute | solution.py:120
  47.4 13.8 %collective-permute-start.1 = (bf16[8,130,256]{2,0,1:T(8,128)(2,1)S(1)}, bf16[8,130,256]{2,0,1:T(8,128)(2,1)S(1)}, u32[]{:S(2)}, u32[]{:S(2)}) collective-permute-start(bf16[8,130,256]{2,0,1:T(8,128)(2,1)S(1)} %bitcast.107), channel_id=1, source_target_pairs={{0,16},{16,0},{32,48},{48,32},{64,80},{80,64},{96,112},{112,96},{1... | collective-permute-start | bytes 1597448 | tf_op jit(solution)/shard_map/ppermute | solution.py:121
  72.4 14.8 %all-to-all-start.1 = ((f32[8,16,512]{2,1,0:T(8,128)}), f32[8,16,512]{2,1,0:T(8,128)S(1)}, u32[]{:S(2)}, u32[]{:S(2)}) async-start(f32[8,16,512]{2,1,0:T(8,128)} %shard_map.46), calls=%async_computation.1 | async-start | bytes 524288 | tf_op jit(solution)/shard_map/all_to_all | solution.py:128
  88.1 0.7 copy-start.3
  89.4 10.5 %collective-permute-start.2 = (f32[2,512]{0,1:T(8,128)S(1)}, f32[2,512]{0,1:T(8,128)S(1)}, u32[]{:S(2)}, u32[]{:S(2)}) collective-permute-start(f32[2,512]{0,1:T(8,128)S(1)} %slice_select_fusion), channel_id=1, source_target_pairs={{16,0},{32,16},{48,32},{64,48},{80,64},{96,80},{112,96},{128,112},... | collective-permute-start | bytes 12296 | tf_op jit(solution)/shard_map/ppermute | solution.py:85
  94.6 11.7 %collective-permute-start.3 = (f32[2,512]{0,1:T(8,128)S(1)}, f32[2,512]{0,1:T(8,128)S(1)}, u32[]{:S(2)}, u32[]{:S(2)}) collective-permute-start(f32[2,512]{0,1:T(8,128)S(1)} %concatenate.106), channel_id=1, source_target_pairs={{0,16},{16,32},{32,48},{48,64},{64,80},{80,96},{96,112},{112,128},... | collective-permute-start | bytes 12296 | tf_op jit(solution)/shard_map/ppermute | solution.py:84

commit v15 on v14

--- a/solution.py
+++ b/solution.py
@@ -16,7 +16,7 @@
 
 def wave_kernel(gt_ref, a_ref, o_ref):
     slots = a_ref.shape[0] - 16
-    width = gt_ref.shape[1]
+    width = gt_ref.shape[0]
     lanes = a_ref.shape[1]
     code = a_ref[slots:slots + 16, :].astype(jnp.float32)
     start = (code[0:1] * CODE + code[1:2]).astype(jnp.int32)
@@ -35,24 +35,26 @@
         dense = jnp.where(((start >> bit) & 1) == 1, rolled, dense)
     if dense.shape[0] < width:
         dense = jnp.concatenate([dense, jnp.zeros((width - dense.shape[0], lanes), jnp.float32)], axis=0)
-    wave = jnp.dot(gt_ref[...], dense.astype(jnp.bfloat16), preferred_element_type=jnp.float32)
+    wave = lax.dot_general(
+        gt_ref[...], dense.astype(jnp.bfloat16), (((0,), (0,)), ((), ())), preferred_element_type=jnp.float32
+    )
     rows = wave.shape[0]
     o_ref[...] = jnp.max(wave.reshape(rows // TSTEP, TSTEP, lanes), axis=1)
 
 
-def wave_maxima(panel_t, coded):
+def wave_maxima(panel, coded):
     parts, height, lanes = coded.shape
-    rows, width = panel_t.shape
+    width, rows = panel.shape
     return pl.pallas_call(
         wave_kernel,
         grid=(parts,),
         in_specs=[
-            pl.BlockSpec((rows, width), lambda p: (0, 0)),
+            pl.BlockSpec((width, rows), lambda p: (0, 0)),
             pl.BlockSpec((None, height, lanes), lambda p: (p, 0, 0)),
         ],
         out_specs=pl.BlockSpec((None, rows // TSTEP, lanes), lambda p: (p, 0, 0)),
         out_shape=jax.ShapeDtypeStruct((parts, rows // TSTEP, lanes), jnp.float32),
-    )(panel_t, coded)
+    )(panel, coded)
 
 
 def shifted(values, step, fill):
@@ -122,9 +124,7 @@
     coded = jnp.where(core == 0, jnp.concatenate([mine, theirs], axis=2), jnp.concatenate([theirs, mine], axis=2))
     coded = jnp.pad(coded, ((0, 0), (0, 16 - (height - slip_values.shape[1])), (0, 0)))
     panel = jnp.where(side == 0, jnp.stack([near, far], axis=1), jnp.stack([far, near], axis=1))
-    panel_t = panel.reshape(width, block).T
-
-    maxima = wave_maxima(panel_t, coded)
+    maxima = wave_maxima(panel.reshape(width, block), coded)
     maxima = lax.all_to_all(maxima, SPLIT, 0, 0, tiled=True)
     return point_peaks(maxima.reshape(-1, scen), win_point, MOST)
 

time: 109 us -> 109 us (level)
  local copies, waits for them, and re-layouts: 9.45 us -> 8.3 us
    select_n x2 -> x0, local copies, waits for them, and re-layouts: 1.44 us -> none  [local(): jnp.where(side == 0, jnp.stack([near, far], axis=1), jnp.stack([far, near...]
    unnamed x12 -> x11, local copies, waits for them, and re-layouts: 3.41 us -> 3.12 us
where the time goes in v15:
time: 109 us; the launch traced here: 107 us
  waiting for transfers between devices  59 us (54%)
  starting transfers between devices  25.1 us (23%)
  Pallas kernels  9.89 us (9%)
  local copies, waits for them, and re-layouts  8.3 us (8%)
  other arithmetic  4.75 us (4%)
    all_to_all x1, waiting for transfers between devices, local(): lax.all_to_all(outgoing, SPLIT, 0, 0, tiled=True).reshape(parts, message)  29.3 us
    all_to_all x1, waiting for transfers between devices, local(): maxima = lax.all_to_all(maxima, SPLIT, 0, 0, tiled=True)  10.6 us
    all_to_all x1, starting transfers between devices, local(): lax.all_to_all(outgoing, SPLIT, 0, 0, tiled=True).reshape(parts, message)  10.4 us
    pallas_call x1, Pallas kernels, wave_maxima(): pl.pallas_call(wave_kernel, grid=(parts,), in_specs=[pl.BlockSpec((width,...  9.89 us
    ppermute x1, waiting for transfers between devices, local(): lax.ppermute(near, SHARE, [(i, (i + 1) % shares) for i in range(shares)])  9.65 us
    ppermute x1, waiting for transfers between devices, point_peaks(): lax.ppermute(to_right, 'rows', [(i, i + 1) for i in range(count - 1)])  6.05 us
    ppermute x1, starting transfers between devices, point_peaks(): lax.ppermute(to_left, 'rows', [(i + 1, i) for i in range(count - 1)])  3.9 us
    ppermute x1, starting transfers between devices, local(): lax.ppermute(near, SHARE, [(i, (i + 1) % shares) for i in range(shares)])  3.48 us
  transfers between devices with their start and end apart: 6, of which 5 were waited for; matrix products, arithmetic and copies ran while one was open for 4% of the time, Pallas kernels for 0%

profile of v15, /device:TPU:6, one launch (start us, length us, event | category | flops | bytes accessed | tf_op | source)
XLA Modules:
  0.0 107.4 jit_solution(10494444223556910415)
XLA Ops:
  0.0 0.0 copy-start
  0.0 0.0 copy-start.1
  0.0 1.4 %copy.41 = bf16[4,8,8,1024]{3,2,1,0:T(8,128)(2,1)S(1)} copy(bf16[4,8,8,1024]{3,1,2,0:T(8,128)(2,1)} %bitcast.105) | data formatting | bytes 1048576
  1.4 0.0 copy-done
  1.4 0.2 fusion.1
  1.6 0.0 copy-done.1
  1.7 0.1 fusion.8
  1.8 0.1 copy.27
  2.0 0.3 maximum_maximum_fusion
  2.3 1.1 %copy.45 = bf16[1,8,16,4224]{3,2,1,0:T(8,128)(2,1)} copy(bf16[1,8,16,4224]{3,1,2,0:T(8,128)(2,1)S(1)} %bitcast.91) | data formatting | bytes 2162688
  3.4 0.0 copy-start.2
  3.4 10.4 %all-to-all-start = ((bf16[8,16,4224]{2,1,0:T(8,128)(2,1)}), bf16[8,16,4224]{2,1,0:T(8,128)(2,1)S(1)}, u32[]{:S(2)}, u32[]{:S(2)}) async-start(bf16[8,16,4224]{2,1,0:T(8,128)(2,1)} %bitcast.84), calls=%async_computation | async-start | bytes 2162688 | tf_op jit(solution)/shard_map/all_to_all | solution.py:118
  13.9 0.0 copy-done.2
  13.9 0.1 fusion.11
  14.0 0.1 slice_bitcast_fusion.7
  14.0 29.3 %all-to-all-done = bf16[8,16,4224]{2,1,0:T(8,128)(2,1)S(1)} async-done(((bf16[8,16,4224]{2,1,0:T(8,128)(2,1)}), bf16[8,16,4224]{2,1,0:T(8,128)(2,1)S(1)}, u32[]{:S(2)}, u32[]{:S(2)}) %all-to-all-start) | async-done | bytes 1081376 | tf_op jit(solution)/shard_map/all_to_all | solution.py:118
  43.3 0.2 copy.43
  43.5 0.3 copy.28
  43.8 3.5 %collective-permute-start = (bf16[8,32,1024]{2,1,0:T(8,128)(2,1)S(1)}, bf16[8,32,1024]{2,1,0:T(8,128)(2,1)S(1)}, u32[]{:S(2)}, u32[]{:S(2)}) collective-permute-start(bf16[8,32,1024]{2,1,0:T(8,128)(2,1)S(1)} %copy.28), channel_id=1, source_target_pairs={{0,1},{1,0},{2,3},{3,2},{4,5},{5,4},{6,7},{7,6},{8,9},{9,8},{10,11... | collective-permute-start | bytes 1572872 | tf_op jit(solution)/shard_map/ppermute | solution.py:122
  47.3 0.1 slice_bitcast_fusion.4
  47.4 1.9 %collective-permute-start.1 = (bf16[8,130,256]{2,0,1:T(8,128)(2,1)S(1)}, bf16[8,130,256]{2,0,1:T(8,128)(2,1)S(1)}, u32[]{:S(2)}, u32[]{:S(2)}) collective-permute-start(bf16[8,130,256]{2,0,1:T(8,128)(2,1)S(1)} %bitcast.100), channel_id=1, source_target_pairs={{0,16},{16,0},{32,48},{48,32},{64,80},{80,64},{96,112},{112,96},{1... | collective-permute-start | bytes 1597448 | tf_op jit(solution)/shard_map/ppermute | solution.py:123
  49.4 0.1 slice_bitcast_fusion.5
  49.4 0.1 slice_bitcast_fusion.6
  49.5 0.1 copy.31
  49.6 0.3 copy.29
  49.9 9.7 %collective-permute-done = bf16[8,32,1024]{2,1,0:T(8,128)(2,1)S(1)} collective-permute-done((bf16[8,32,1024]{2,1,0:T(8,128)(2,1)S(1)}, bf16[8,32,1024]{2,1,0:T(8,128)(2,1)S(1)}, u32[]{:S(2)}, u32[]{:S(2)}) %collective-permute-start) | collective-permute-done | bytes 524320 | tf_op jit(solution)/shard_map/ppermute | solution.py:122
  59.6 1.1 maximum_select_fusion.1
  60.7 0.0 collective-permute-done.1
  60.7 0.1 copy.32
  60.8 0.3 maximum_select_fusion
  61.1 1.1 %pad.24.a_ref = bf16[8,144,512]{2,1,0:T(8,128)(2,1)} pad(bf16[8,130,512]{2,1,0:T(8,128)(2,1)S(1)} %maximum_select_fusion, bf16[]{:T(256)} %constant.63.clone.1), padding=0_0x0_14x0_0 | pad | bytes 2244610 | tf_op jit(solution)/shard_map/jit(_pad)/pad | solution.py:125
  62.2 9.9 %shard_map.46 = f32[8,16,512]{2,1,0:T(8,128)} custom-call(bf16[512,1024]{1,0:T(8,128)(2,1)} %bitcast.95, bf16[8,144,512]{2,1,0:T(8,128)(2,1)} %pad.24.a_ref), custom_call_target="tpu_custom_call" | custom-call | tf_op jit(solution)/shard_map/pallas_call | solution.py:48
  72.1 3.4 %all-to-all-start.1 = ((f32[8,16,512]{2,1,0:T(8,128)}), f32[8,16,512]{2,1,0:T(8,128)S(1)}, u32[]{:S(2)}, u32[]{:S(2)}) async-start(f32[8,16,512]{2,1,0:T(8,128)} %shard_map.46), calls=%async_computation.1 | async-start | bytes 524288 | tf_op jit(solution)/shard_map/all_to_all | solution.py:128
  75.5 0.6 fusion.10
  76.1 0.1 maximum_compare_fusion
  76.2 0.1 compare_bitcast_fusion.7
  76.3 10.6 %all-to-all-done.1 = f32[8,16,512]{2,1,0:T(8,128)S(1)} async-done(((f32[8,16,512]{2,1,0:T(8,128)}), f32[8,16,512]{2,1,0:T(8,128)S(1)}, u32[]{:S(2)}, u32[]{:S(2)}) %all-to-all-start.1) | async-done | bytes 262176 | tf_op jit(solution)/shard_map/all_to_all | solution.py:128
  86.9 0.1 copy.36
  87.1 0.1 fusion.9
  87.2 0.1 maximum_select_fusion.13
  87.3 0.1 slice.164
  87.5 0.1 slice.165
  87.7 0.1 slice.166
  87.8 0.0 copy-start.3
  87.9 0.1 slice.167
  88.0 0.4 copy-done.3
  88.5 0.6 slice_select_fusion
  89.1 3.9 %collective-permute-start.2 = (f32[2,512]{0,1:T(8,128)S(1)}, f32[2,512]{0,1:T(8,128)S(1)}, u32[]{:S(2)}, u32[]{:S(2)}) collective-permute-start(f32[2,512]{0,1:T(8,128)S(1)} %slice_select_fusion), channel_id=1, source_target_pairs={{16,0},{32,16},{48,32},{64,48},{80,64},{96,80},{112,96},{128,112},... | collective-permute-start | bytes 12296 | tf_op jit(solution)/shard_map/ppermute | solution.py:87
  93.1 0.1 maximum_select_fusion.7
  93.2 0.1 maximum_select_fusion.6
  93.3 0.1 maximum_select_fusion.5
  93.5 0.1 maximum_select_fusion.4
  93.6 0.1 slice.175
  93.7 0.6 concatenate.106
  94.3 1.9 %collective-permute-start.3 = (f32[2,512]{0,1:T(8,128)S(1)}, f32[2,512]{0,1:T(8,128)S(1)}, u32[]{:S(2)}, u32[]{:S(2)}) collective-permute-start(f32[2,512]{0,1:T(8,128)S(1)} %concatenate.106), channel_id=1, source_target_pairs={{0,16},{16,32},{32,48},{48,64},{64,80},{80,96},{96,112},{112,128},... | collective-permute-start | bytes 12296 | tf_op jit(solution)/shard_map/ppermute | solution.py:86
  96.3 3.4 %collective-permute-done.2 = f32[2,512]{0,1:T(8,128)S(1)} collective-permute-done((f32[2,512]{0,1:T(8,128)S(1)}, f32[2,512]{0,1:T(8,128)S(1)}, u32[]{:S(2)}, u32[]{:S(2)}) %collective-permute-start.2) | collective-permute-done | bytes 4128 | tf_op jit(solution)/shard_map/ppermute | solution.py:87
  99.7 0.3 slice_reduce_fusion.3
  100.0 6.0 %collective-permute-done.3 = f32[2,512]{0,1:T(8,128)S(1)} collective-permute-done((f32[2,512]{0,1:T(8,128)S(1)}, f32[2,512]{0,1:T(8,128)S(1)}, u32[]{:S(2)}, u32[]{:S(2)}) %collective-permute-start.3) | collective-permute-done | bytes 4128 | tf_op jit(solution)/shard_map/ppermute | solution.py:86
  106.0 0.3 slice_reduce_fusion.2
  106.3 1.0 fusion.2
  (12 shorter events, 0.3 us)
Async XLA Ops:
  0.0 1.4 %copy-start = (s32[512,128]{1,0:T(8,128)S(1)}, s32[512,128]{1,0:T(8,128)}, u32[]{:S(2)}) copy-start(s32[512,128]{1,0:T(8,128)} %param.6) | copy-start | bytes 786436
  0.0 1.6 %copy-start.1 = (bf16[512,128]{1,0:T(8,128)(2,1)S(1)}, bf16[512,128]{1,0:T(8,128)(2,1)}, u32[]{:S(2)}) copy-start(bf16[512,128]{1,0:T(8,128)(2,1)} %param.5) | copy-start | bytes 393220
  3.4 10.5 %copy-start.2 = (s32[128]{0:T(128)S(1)}, s32[128]{0:T(128)}, u32[]{:S(2)}) copy-start(s32[128]{0:T(128)} %param.7) | copy-start | bytes 1540
  3.4 39.9 %all-to-all-start = ((bf16[8,16,4224]{2,1,0:T(8,128)(2,1)}), bf16[8,16,4224]{2,1,0:T(8,128)(2,1)S(1)}, u32[]{:S(2)}, u32[]{:S(2)}) async-start(bf16[8,16,4224]{2,1,0:T(8,128)(2,1)} %bitcast.84), calls=%async_computation | async-start | bytes 2162688 | tf_op jit(solution)/shard_map/all_to_all | solution.py:118
  43.8 15.7 %collective-permute-start = (bf16[8,32,1024]{2,1,0:T(8,128)(2,1)S(1)}, bf16[8,32,1024]{2,1,0:T(8,128)(2,1)S(1)}, u32[]{:S(2)}, u32[]{:S(2)}) collective-permute-start(bf16[8,32,1024]{2,1,0:T(8,128)(2,1)S(1)} %copy.28), channel_id=1, source_target_pairs={{0,1},{1,0},{2,3},{3,2},{4,5},{5,4},{6,7},{7,6},{8,9},{9,8},{10,11... | collective-permute-start | bytes 1572872 | tf_op jit(solution)/shard_map/ppermute | solution.py:122
  47.4 13.2 %collective-permute-start.1 = (bf16[8,130,256]{2,0,1:T(8,128)(2,1)S(1)}, bf16[8,130,256]{2,0,1:T(8,128)(2,1)S(1)}, u32[]{:S(2)}, u32[]{:S(2)}) collective-permute-start(bf16[8,130,256]{2,0,1:T(8,128)(2,1)S(1)} %bitcast.100), channel_id=1, source_target_pairs={{0,16},{16,0},{32,48},{48,32},{64,80},{80,64},{96,112},{112,96},{1... | collective-permute-start | bytes 1597448 | tf_op jit(solution)/shard_map/ppermute | solution.py:123
  72.1 14.8 %all-to-all-start.1 = ((f32[8,16,512]{2,1,0:T(8,128)}), f32[8,16,512]{2,1,0:T(8,128)S(1)}, u32[]{:S(2)}, u32[]{:S(2)}) async-start(f32[8,16,512]{2,1,0:T(8,128)} %shard_map.46), calls=%async_computation.1 | async-start | bytes 524288 | tf_op jit(solution)/shard_map/all_to_all | solution.py:128
  87.8 0.7 copy-start.3
  89.1 10.5 %collective-permute-start.2 = (f32[2,512]{0,1:T(8,128)S(1)}, f32[2,512]{0,1:T(8,128)S(1)}, u32[]{:S(2)}, u32[]{:S(2)}) collective-permute-start(f32[2,512]{0,1:T(8,128)S(1)} %slice_select_fusion), channel_id=1, source_target_pairs={{16,0},{32,16},{48,32},{64,48},{80,64},{96,80},{112,96},{128,112},... | collective-permute-start | bytes 12296 | tf_op jit(solution)/shard_map/ppermute | solution.py:87
  94.3 11.7 %collective-permute-start.3 = (f32[2,512]{0,1:T(8,128)S(1)}, f32[2,512]{0,1:T(8,128)S(1)}, u32[]{:S(2)}, u32[]{:S(2)}) collective-permute-start(f32[2,512]{0,1:T(8,128)S(1)} %concatenate.106), channel_id=1, source_target_pairs={{0,16},{16,32},{32,48},{48,64},{64,80},{80,96},{96,112},{112,128},... | collective-permute-start | bytes 12296 | tf_op jit(solution)/shard_map/ppermute | solution.py:86

commit v16 on v14

--- a/solution.py
+++ b/solution.py
@@ -15,10 +15,10 @@
 
 
 def wave_kernel(gt_ref, a_ref, o_ref):
-    slots = a_ref.shape[0] - 16
+    slots = a_ref.shape[0] - 2
     width = gt_ref.shape[1]
     lanes = a_ref.shape[1]
-    code = a_ref[slots:slots + 16, :].astype(jnp.float32)
+    code = a_ref[slots:slots + 2, :].astype(jnp.float32)
     start = (code[0:1] * CODE + code[1:2]).astype(jnp.int32)
     dense = a_ref[0:slots, :].astype(jnp.float32)
     reach = slots
@@ -120,7 +120,6 @@
     far = lax.ppermute(near, SHARE, [(i, (i + 1) % shares) for i in range(shares)])
     theirs = lax.ppermute(mine, "rows", [(i, i ^ 1) for i in range(count_rows)])
     coded = jnp.where(core == 0, jnp.concatenate([mine, theirs], axis=2), jnp.concatenate([theirs, mine], axis=2))
-    coded = jnp.pad(coded, ((0, 0), (0, 16 - (height - slip_values.shape[1])), (0, 0)))
     panel = jnp.where(side == 0, jnp.stack([near, far], axis=1), jnp.stack([far, near], axis=1))
     panel_t = panel.reshape(width, block).T
 

time: 109 us -> 109 us (level)
  local copies, waits for them, and re-layouts: 9.45 us -> 8.31 us
    pad x1 -> x0, local copies, waits for them, and re-layouts: 1.14 us -> none  [local(): jnp.pad(coded, ((0, 0), (0, 16 - (height - slip_values.shape[1])), (0, 0)))]
where the time goes in v16:
time: 109 us; the launch traced here: 108 us
  waiting for transfers between devices  59.3 us (54%)
  starting transfers between devices  25.1 us (23%)
  Pallas kernels  9.6 us (9%)
  local copies, waits for them, and re-layouts  8.31 us (8%)
  other arithmetic  4.85 us (4%)
    all_to_all x1, waiting for transfers between devices, local(): lax.all_to_all(outgoing, SPLIT, 0, 0, tiled=True).reshape(parts, message)  29.3 us
    all_to_all x1, waiting for transfers between devices, local(): maxima = lax.all_to_all(maxima, SPLIT, 0, 0, tiled=True)  10.6 us
    all_to_all x1, starting transfers between devices, local(): lax.all_to_all(outgoing, SPLIT, 0, 0, tiled=True).reshape(parts, message)  10.4 us
    ppermute x1, waiting for transfers between devices, local(): lax.ppermute(near, SHARE, [(i, (i + 1) % shares) for i in range(shares)])  9.95 us
    pallas_call x1, Pallas kernels, wave_maxima(): pl.pallas_call(wave_kernel, grid=(parts,), in_specs=[pl.BlockSpec((rows,...  9.6 us
    ppermute x1, waiting for transfers between devices, point_peaks(): lax.ppermute(to_right, 'rows', [(i, i + 1) for i in range(count - 1)])  6.04 us
    ppermute x1, starting transfers between devices, point_peaks(): lax.ppermute(to_left, 'rows', [(i + 1, i) for i in range(count - 1)])  3.91 us
    ppermute x1, starting transfers between devices, local(): lax.ppermute(near, SHARE, [(i, (i + 1) % shares) for i in range(shares)])  3.48 us
  transfers between devices with their start and end apart: 6, of which 5 were waited for; matrix products, arithmetic and copies ran while one was open for 4% of the time, Pallas kernels for 0%

profile of v16, /device:TPU:6, one launch (start us, length us, event | category | flops | bytes accessed | tf_op | source)
XLA Modules:
  0.0 107.5 jit_solution(2318500197262126135)
XLA Ops:
  0.0 0.0 copy-start
  0.0 0.0 copy-start.1
  0.0 1.4 %copy.39 = bf16[4,8,8,1024]{3,2,1,0:T(8,128)(2,1)S(1)} copy(bf16[4,8,8,1024]{3,1,2,0:T(8,128)(2,1)} %bitcast.115) | data formatting | bytes 1048576
  1.4 0.0 copy-done
  1.4 0.2 fusion.1
  1.6 0.0 copy-done.1
  1.7 0.1 fusion.8
  1.8 0.1 copy.26
  2.0 0.3 maximum_maximum_fusion
  2.3 1.1 %copy.47 = bf16[1,8,16,4224]{3,2,1,0:T(8,128)(2,1)} copy(bf16[1,8,16,4224]{3,1,2,0:T(8,128)(2,1)S(1)} %bitcast.97) | data formatting | bytes 2162688
  3.4 0.0 copy-start.2
  3.4 10.4 %all-to-all-start = ((bf16[8,16,4224]{2,1,0:T(8,128)(2,1)}), bf16[8,16,4224]{2,1,0:T(8,128)(2,1)S(1)}, u32[]{:S(2)}, u32[]{:S(2)}) async-start(bf16[8,16,4224]{2,1,0:T(8,128)(2,1)} %bitcast.91), calls=%async_computation | async-start | bytes 2162688 | tf_op jit(solution)/shard_map/all_to_all | solution.py:116
  13.9 0.0 copy-done.2
  13.9 0.1 fusion.11
  14.0 0.1 slice_bitcast_fusion.7
  14.0 29.3 %all-to-all-done = bf16[8,16,4224]{2,1,0:T(8,128)(2,1)S(1)} async-done(((bf16[8,16,4224]{2,1,0:T(8,128)(2,1)}), bf16[8,16,4224]{2,1,0:T(8,128)(2,1)S(1)}, u32[]{:S(2)}, u32[]{:S(2)}) %all-to-all-start) | async-done | bytes 1081376 | tf_op jit(solution)/shard_map/all_to_all | solution.py:116
  43.3 0.2 copy.41
  43.5 0.3 copy.48
  43.8 3.5 %collective-permute-start = (bf16[8,32,1024]{2,1,0:T(8,128)(2,1)S(1)}, bf16[8,32,1024]{2,1,0:T(8,128)(2,1)S(1)}, u32[]{:S(2)}, u32[]{:S(2)}) collective-permute-start(bf16[8,32,1024]{2,1,0:T(8,128)(2,1)S(1)} %bitcast.110), channel_id=1, source_target_pairs={{0,1},{1,0},{2,3},{3,2},{4,5},{5,4},{6,7},{7,6},{8,9},{9,8},{10,11... | collective-permute-start | bytes 1572872 | tf_op jit(solution)/shard_map/ppermute | solution.py:120
  47.3 0.1 slice_bitcast_fusion.4
  47.4 1.9 %collective-permute-start.1 = (bf16[8,130,256]{2,0,1:T(8,128)(2,1)S(1)}, bf16[8,130,256]{2,0,1:T(8,128)(2,1)S(1)}, u32[]{:S(2)}, u32[]{:S(2)}) collective-permute-start(bf16[8,130,256]{2,0,1:T(8,128)(2,1)S(1)} %bitcast.107), channel_id=1, source_target_pairs={{0,16},{16,0},{32,48},{48,32},{64,80},{80,64},{96,112},{112,96},{1... | collective-permute-start | bytes 1597448 | tf_op jit(solution)/shard_map/ppermute | solution.py:121
  49.4 0.1 slice_bitcast_fusion.5
  49.4 0.1 slice_bitcast_fusion.6
  49.5 0.1 copy.29
  49.6 10.0 %collective-permute-done = bf16[8,32,1024]{2,1,0:T(8,128)(2,1)S(1)} collective-permute-done((bf16[8,32,1024]{2,1,0:T(8,128)(2,1)S(1)}, bf16[8,32,1024]{2,1,0:T(8,128)(2,1)S(1)}, u32[]{:S(2)}, u32[]{:S(2)}) %collective-permute-start) | collective-permute-done | bytes 524320 | tf_op jit(solution)/shard_map/ppermute | solution.py:120
  59.6 0.2 maximum_select_fusion.1
  59.8 0.1 copy.27
  59.9 1.4 %copy.28 = bf16[512,1024]{0,1:T(8,128)(2,1)} copy(bf16[512,1024]{1,0:T(8,128)(2,1)S(1)} %bitcast.102) | data formatting | bytes 2097152 | tf_op jit(solution)/shard_map/jit(_where)/select_n | solution.py:123
  61.2 0.0 collective-permute-done.1
  61.2 0.1 copy.30
  61.3 1.3 %maximum_select_fusion.a_ref = bf16[8,130,512]{2,1,0:T(8,128)(2,1)} fusion(bf16[8,130,256]{2,1,0:T(8,128)(2,1)S(1)} %copy.30, bf16[8,130,256]{2,1,0:T(8,128)(2,1)S(1)} %copy.29, pred[]{:T(512)S(6)} %eq.75), kind=kLoop, calls=%fused_computation | loop fusion | flops 4792320 | bytes 2129921 | tf_op jit(solution)/shard_map/jit(_where)/select_n | solution.py:122
  62.6 9.6 %shard_map.46 = f32[8,16,512]{2,1,0:T(8,128)} custom-call(bf16[1024,512]{1,0:T(8,128)(2,1)} %bitcast.101, bf16[8,130,512]{2,1,0:T(8,128)(2,1)} %maximum_select_fusion.a_ref), custom_call_target="tpu_custom_call" | custom-call | tf_op jit(solution)/shard_map/pallas_call | solution.py:46
  72.2 3.4 %all-to-all-start.1 = ((f32[8,16,512]{2,1,0:T(8,128)}), f32[8,16,512]{2,1,0:T(8,128)S(1)}, u32[]{:S(2)}, u32[]{:S(2)}) async-start(f32[8,16,512]{2,1,0:T(8,128)} %shard_map.46), calls=%async_computation.1 | async-start | bytes 524288 | tf_op jit(solution)/shard_map/all_to_all | solution.py:127
  75.7 0.6 fusion.10
  76.2 0.1 maximum_compare_fusion
  76.3 0.1 compare_bitcast_fusion.7
  76.4 10.6 %all-to-all-done.1 = f32[8,16,512]{2,1,0:T(8,128)S(1)} async-done(((f32[8,16,512]{2,1,0:T(8,128)}), f32[8,16,512]{2,1,0:T(8,128)S(1)}, u32[]{:S(2)}, u32[]{:S(2)}) %all-to-all-start.1) | async-done | bytes 262176 | tf_op jit(solution)/shard_map/all_to_all | solution.py:127
  87.1 0.1 copy.34
  87.2 0.1 fusion.9
  87.3 0.1 maximum_select_fusion.13
  87.5 0.1 slice.164
  87.6 0.1 slice.165
  87.8 0.1 slice.166
  87.9 0.0 copy-start.3
  88.0 0.1 slice.167
  88.2 0.4 copy-done.3
  88.6 0.6 slice_select_fusion
  89.3 3.9 %collective-permute-start.2 = (f32[2,512]{0,1:T(8,128)S(1)}, f32[2,512]{0,1:T(8,128)S(1)}, u32[]{:S(2)}, u32[]{:S(2)}) collective-permute-start(f32[2,512]{0,1:T(8,128)S(1)} %slice_select_fusion), channel_id=1, source_target_pairs={{16,0},{32,16},{48,32},{64,48},{80,64},{96,80},{112,96},{128,112},... | collective-permute-start | bytes 12296 | tf_op jit(solution)/shard_map/ppermute | solution.py:85
  93.2 0.1 maximum_select_fusion.7
  93.3 0.1 maximum_select_fusion.6
  93.5 0.1 maximum_select_fusion.5
  93.6 0.1 maximum_select_fusion.4
  93.8 0.1 slice.175
  93.9 0.6 concatenate.106
  94.5 1.9 %collective-permute-start.3 = (f32[2,512]{0,1:T(8,128)S(1)}, f32[2,512]{0,1:T(8,128)S(1)}, u32[]{:S(2)}, u32[]{:S(2)}) collective-permute-start(f32[2,512]{0,1:T(8,128)S(1)} %concatenate.106), channel_id=1, source_target_pairs={{0,16},{16,32},{32,48},{48,64},{64,80},{80,96},{96,112},{112,128},... | collective-permute-start | bytes 12296 | tf_op jit(solution)/shard_map/ppermute | solution.py:84
  96.4 3.4 %collective-permute-done.2 = f32[2,512]{0,1:T(8,128)S(1)} collective-permute-done((f32[2,512]{0,1:T(8,128)S(1)}, f32[2,512]{0,1:T(8,128)S(1)}, u32[]{:S(2)}, u32[]{:S(2)}) %collective-permute-start.2) | collective-permute-done | bytes 4128 | tf_op jit(solution)/shard_map/ppermute | solution.py:85
  99.8 0.3 slice_reduce_fusion.3
  100.1 6.0 %collective-permute-done.3 = f32[2,512]{0,1:T(8,128)S(1)} collective-permute-done((f32[2,512]{0,1:T(8,128)S(1)}, f32[2,512]{0,1:T(8,128)S(1)}, u32[]{:S(2)}, u32[]{:S(2)}) %collective-permute-start.3) | collective-permute-done | bytes 4128 | tf_op jit(solution)/shard_map/ppermute | solution.py:84
  106.2 0.3 slice_reduce_fusion.2
  106.5 1.0 fusion.2
  (12 shorter events, 0.3 us)
Async XLA Ops:
  0.0 1.4 %copy-start = (s32[512,128]{1,0:T(8,128)S(1)}, s32[512,128]{1,0:T(8,128)}, u32[]{:S(2)}) copy-start(s32[512,128]{1,0:T(8,128)} %param.6) | copy-start | bytes 786436
  0.0 1.6 %copy-start.1 = (bf16[512,128]{1,0:T(8,128)(2,1)S(1)}, bf16[512,128]{1,0:T(8,128)(2,1)}, u32[]{:S(2)}) copy-start(bf16[512,128]{1,0:T(8,128)(2,1)} %param.5) | copy-start | bytes 393220
  3.4 10.5 %copy-start.2 = (s32[128]{0:T(128)S(1)}, s32[128]{0:T(128)}, u32[]{:S(2)}) copy-start(s32[128]{0:T(128)} %param.7) | copy-start | bytes 1540
  3.4 39.9 %all-to-all-start = ((bf16[8,16,4224]{2,1,0:T(8,128)(2,1)}), bf16[8,16,4224]{2,1,0:T(8,128)(2,1)S(1)}, u32[]{:S(2)}, u32[]{:S(2)}) async-start(bf16[8,16,4224]{2,1,0:T(8,128)(2,1)} %bitcast.91), calls=%async_computation | async-start | bytes 2162688 | tf_op jit(solution)/shard_map/all_to_all | solution.py:116
  43.8 15.7 %collective-permute-start = (bf16[8,32,1024]{2,1,0:T(8,128)(2,1)S(1)}, bf16[8,32,1024]{2,1,0:T(8,128)(2,1)S(1)}, u32[]{:S(2)}, u32[]{:S(2)}) collective-permute-start(bf16[8,32,1024]{2,1,0:T(8,128)(2,1)S(1)} %bitcast.110), channel_id=1, source_target_pairs={{0,1},{1,0},{2,3},{3,2},{4,5},{5,4},{6,7},{7,6},{8,9},{9,8},{10,11... | collective-permute-start | bytes 1572872 | tf_op jit(solution)/shard_map/ppermute | solution.py:120
  47.4 13.8 %collective-permute-start.1 = (bf16[8,130,256]{2,0,1:T(8,128)(2,1)S(1)}, bf16[8,130,256]{2,0,1:T(8,128)(2,1)S(1)}, u32[]{:S(2)}, u32[]{:S(2)}) collective-permute-start(bf16[8,130,256]{2,0,1:T(8,128)(2,1)S(1)} %bitcast.107), channel_id=1, source_target_pairs={{0,16},{16,0},{32,48},{48,32},{64,80},{80,64},{96,112},{112,96},{1... | collective-permute-start | bytes 1597448 | tf_op jit(solution)/shard_map/ppermute | solution.py:121
  72.2 14.8 %all-to-all-start.1 = ((f32[8,16,512]{2,1,0:T(8,128)}), f32[8,16,512]{2,1,0:T(8,128)S(1)}, u32[]{:S(2)}, u32[]{:S(2)}) async-start(f32[8,16,512]{2,1,0:T(8,128)} %shard_map.46), calls=%async_computation.1 | async-start | bytes 524288 | tf_op jit(solution)/shard_map/all_to_all | solution.py:127
  87.9 0.7 copy-start.3
  89.3 10.6 %collective-permute-start.2 = (f32[2,512]{0,1:T(8,128)S(1)}, f32[2,512]{0,1:T(8,128)S(1)}, u32[]{:S(2)}, u32[]{:S(2)}) collective-permute-start(f32[2,512]{0,1:T(8,128)S(1)} %slice_select_fusion), channel_id=1, source_target_pairs={{16,0},{32,16},{48,32},{64,48},{80,64},{96,80},{112,96},{128,112},... | collective-permute-start | bytes 12296 | tf_op jit(solution)/shard_map/ppermute | solution.py:85
  94.5 11.7 %collective-permute-start.3 = (f32[2,512]{0,1:T(8,128)S(1)}, f32[2,512]{0,1:T(8,128)S(1)}, u32[]{:S(2)}, u32[]{:S(2)}) collective-permute-start(f32[2,512]{0,1:T(8,128)S(1)} %concatenate.106), channel_id=1, source_target_pairs={{0,16},{16,32},{32,48},{48,64},{64,80},{80,96},{96,112},{112,128},... | collective-permute-start | bytes 12296 | tf_op jit(solution)/shard_map/ppermute | solution.py:84

commit v17 on v15

--- a/solution.py
+++ b/solution.py
@@ -15,10 +15,10 @@
 
 
 def wave_kernel(gt_ref, a_ref, o_ref):
-    slots = a_ref.shape[0] - 16
+    slots = a_ref.shape[0] - 2
     width = gt_ref.shape[0]
     lanes = a_ref.shape[1]
-    code = a_ref[slots:slots + 16, :].astype(jnp.float32)
+    code = a_ref[slots:slots + 2, :].astype(jnp.float32)
     start = (code[0:1] * CODE + code[1:2]).astype(jnp.int32)
     dense = a_ref[0:slots, :].astype(jnp.float32)
     reach = slots
@@ -122,7 +122,6 @@
     far = lax.ppermute(near, SHARE, [(i, (i + 1) % shares) for i in range(shares)])
     theirs = lax.ppermute(mine, "rows", [(i, i ^ 1) for i in range(count_rows)])
     coded = jnp.where(core == 0, jnp.concatenate([mine, theirs], axis=2), jnp.concatenate([theirs, mine], axis=2))
-    coded = jnp.pad(coded, ((0, 0), (0, 16 - (height - slip_values.shape[1])), (0, 0)))
     panel = jnp.where(side == 0, jnp.stack([near, far], axis=1), jnp.stack([far, near], axis=1))
     maxima = wave_maxima(panel.reshape(width, block), coded)
     maxima = lax.all_to_all(maxima, SPLIT, 0, 0, tiled=True)

time: 109 us -> 109 us (level)
  local copies, waits for them, and re-layouts: 8.3 us -> 7.16 us
    pad x1 -> x0, local copies, waits for them, and re-layouts: 1.14 us -> none  [local(): jnp.pad(coded, ((0, 0), (0, 16 - (height - slip_values.shape[1])), (0, 0)))]
where the time goes in v17:
time: 109 us; the launch traced here: 107 us
  waiting for transfers between devices  59 us (54%)
  starting transfers between devices  25.1 us (23%)
  Pallas kernels  9.89 us (9%)
  local copies, waits for them, and re-layouts  7.16 us (7%)
  other arithmetic  5.78 us (5%)
    all_to_all x1, waiting for transfers between devices, local(): lax.all_to_all(outgoing, SPLIT, 0, 0, tiled=True).reshape(parts, message)  29.3 us
    all_to_all x1, waiting for transfers between devices, local(): maxima = lax.all_to_all(maxima, SPLIT, 0, 0, tiled=True)  10.7 us
    all_to_all x1, starting transfers between devices, local(): lax.all_to_all(outgoing, SPLIT, 0, 0, tiled=True).reshape(parts, message)  10.4 us
    pallas_call x1, Pallas kernels, wave_maxima(): pl.pallas_call(wave_kernel, grid=(parts,), in_specs=[pl.BlockSpec((width,...  9.89 us
    ppermute x1, waiting for transfers between devices, local(): lax.ppermute(near, SHARE, [(i, (i + 1) % shares) for i in range(shares)])  9.65 us
    ppermute x1, waiting for transfers between devices, point_peaks(): lax.ppermute(to_right, 'rows', [(i, i + 1) for i in range(count - 1)])  6.04 us
    ppermute x1, starting transfers between devices, point_peaks(): lax.ppermute(to_left, 'rows', [(i + 1, i) for i in range(count - 1)])  3.9 us
    ppermute x1, starting transfers between devices, local(): lax.ppermute(near, SHARE, [(i, (i + 1) % shares) for i in range(shares)])  3.48 us
  transfers between devices with their start and end apart: 6, of which 5 were waited for; matrix products, arithmetic and copies ran while one was open for 4% of the time, Pallas kernels for 0%

profile of v17, /device:TPU:6, one launch (start us, length us, event | category | flops | bytes accessed | tf_op | source)
XLA Modules:
  0.0 107.3 jit_solution(5184191162588418785)
XLA Ops:
  0.0 0.0 copy-start
  0.0 0.0 copy-start.1
  0.0 1.4 %copy.41 = bf16[4,8,8,1024]{3,2,1,0:T(8,128)(2,1)S(1)} copy(bf16[4,8,8,1024]{3,1,2,0:T(8,128)(2,1)} %bitcast.105) | data formatting | bytes 1048576
  1.4 0.0 copy-done
  1.4 0.2 fusion.1
  1.6 0.0 copy-done.1
  1.7 0.1 fusion.8
  1.8 0.1 copy.27
  2.0 0.3 maximum_maximum_fusion
  2.3 1.1 %copy.45 = bf16[1,8,16,4224]{3,2,1,0:T(8,128)(2,1)} copy(bf16[1,8,16,4224]{3,1,2,0:T(8,128)(2,1)S(1)} %bitcast.91) | data formatting | bytes 2162688
  3.4 0.0 copy-start.2
  3.4 10.4 %all-to-all-start = ((bf16[8,16,4224]{2,1,0:T(8,128)(2,1)}), bf16[8,16,4224]{2,1,0:T(8,128)(2,1)S(1)}, u32[]{:S(2)}, u32[]{:S(2)}) async-start(bf16[8,16,4224]{2,1,0:T(8,128)(2,1)} %bitcast.84), calls=%async_computation | async-start | bytes 2162688 | tf_op jit(solution)/shard_map/all_to_all | solution.py:118
  13.9 0.0 copy-done.2
  13.9 0.1 fusion.11
  14.0 0.1 slice_bitcast_fusion.7
  14.0 29.3 %all-to-all-done = bf16[8,16,4224]{2,1,0:T(8,128)(2,1)S(1)} async-done(((bf16[8,16,4224]{2,1,0:T(8,128)(2,1)}), bf16[8,16,4224]{2,1,0:T(8,128)(2,1)S(1)}, u32[]{:S(2)}, u32[]{:S(2)}) %all-to-all-start) | async-done | bytes 1081376 | tf_op jit(solution)/shard_map/all_to_all | solution.py:118
  43.3 0.2 copy.43
  43.5 0.3 copy.28
  43.8 3.5 %collective-permute-start = (bf16[8,32,1024]{2,1,0:T(8,128)(2,1)S(1)}, bf16[8,32,1024]{2,1,0:T(8,128)(2,1)S(1)}, u32[]{:S(2)}, u32[]{:S(2)}) collective-permute-start(bf16[8,32,1024]{2,1,0:T(8,128)(2,1)S(1)} %copy.28), channel_id=1, source_target_pairs={{0,1},{1,0},{2,3},{3,2},{4,5},{5,4},{6,7},{7,6},{8,9},{9,8},{10,11... | collective-permute-start | bytes 1572872 | tf_op jit(solution)/shard_map/ppermute | solution.py:122
  47.3 0.1 slice_bitcast_fusion.4
  47.4 1.9 %collective-permute-start.1 = (bf16[8,130,256]{2,0,1:T(8,128)(2,1)S(1)}, bf16[8,130,256]{2,0,1:T(8,128)(2,1)S(1)}, u32[]{:S(2)}, u32[]{:S(2)}) collective-permute-start(bf16[8,130,256]{2,0,1:T(8,128)(2,1)S(1)} %bitcast.100), channel_id=1, source_target_pairs={{0,16},{16,0},{32,48},{48,32},{64,80},{80,64},{96,112},{112,96},{1... | collective-permute-start | bytes 1597448 | tf_op jit(solution)/shard_map/ppermute | solution.py:123
  49.4 0.1 slice_bitcast_fusion.5
  49.4 0.1 slice_bitcast_fusion.6
  49.5 0.1 copy.31
  49.6 0.3 copy.29
  49.9 9.7 %collective-permute-done = bf16[8,32,1024]{2,1,0:T(8,128)(2,1)S(1)} collective-permute-done((bf16[8,32,1024]{2,1,0:T(8,128)(2,1)S(1)}, bf16[8,32,1024]{2,1,0:T(8,128)(2,1)S(1)}, u32[]{:S(2)}, u32[]{:S(2)}) %collective-permute-start) | collective-permute-done | bytes 524320 | tf_op jit(solution)/shard_map/ppermute | solution.py:122
  59.6 1.1 %maximum_select_fusion.1 = bf16[8,2,32,1024]{3,2,1,0:T(8,128)(2,1)} fusion(bf16[8,1,32,1024]{3,2,1,0:T(8,128)(2,1)S(1)} %bitcast.104, bf16[8,1,32,1024]{3,2,1,0:T(8,128)(2,1)S(1)} %copy.29, pred[]{:T(512)S(6)} %eq.74), kind=kLoop, calls=%fused_computation.3 | loop fusion | flops 1572864 | bytes 2097153 | tf_op jit(solution)/shard_map/jit(_where)/select_n | solution.py:125
  60.7 0.0 collective-permute-done.1
  60.7 0.1 copy.32
  60.8 1.3 %maximum_select_fusion.a_ref = bf16[8,130,512]{2,1,0:T(8,128)(2,1)} fusion(bf16[8,130,256]{2,1,0:T(8,128)(2,1)S(1)} %copy.32, bf16[8,130,256]{2,1,0:T(8,128)(2,1)S(1)} %copy.31, pred[]{:T(512)S(6)} %eq.75), kind=kLoop, calls=%fused_computation | loop fusion | flops 4792320 | bytes 2129921 | tf_op jit(solution)/shard_map/jit(_where)/select_n | solution.py:124
  62.1 9.9 %shard_map.46 = f32[8,16,512]{2,1,0:T(8,128)} custom-call(bf16[512,1024]{1,0:T(8,128)(2,1)} %bitcast.95, bf16[8,130,512]{2,1,0:T(8,128)(2,1)} %maximum_select_fusion.a_ref), custom_call_target="tpu_custom_call" | custom-call | tf_op jit(solution)/shard_map/pallas_call | solution.py:48
  72.0 3.4 %all-to-all-start.1 = ((f32[8,16,512]{2,1,0:T(8,128)}), f32[8,16,512]{2,1,0:T(8,128)S(1)}, u32[]{:S(2)}, u32[]{:S(2)}) async-start(f32[8,16,512]{2,1,0:T(8,128)} %shard_map.46), calls=%async_computation.1 | async-start | bytes 524288 | tf_op jit(solution)/shard_map/all_to_all | solution.py:127
  75.4 0.6 fusion.10
  76.0 0.1 maximum_compare_fusion
  76.1 0.1 compare_bitcast_fusion.7
  76.2 10.7 %all-to-all-done.1 = f32[8,16,512]{2,1,0:T(8,128)S(1)} async-done(((f32[8,16,512]{2,1,0:T(8,128)}), f32[8,16,512]{2,1,0:T(8,128)S(1)}, u32[]{:S(2)}, u32[]{:S(2)}) %all-to-all-start.1) | async-done | bytes 262176 | tf_op jit(solution)/shard_map/all_to_all | solution.py:127
  86.8 0.1 copy.36
  86.9 0.1 fusion.9
  87.1 0.1 maximum_select_fusion.13
  87.2 0.1 slice.164
  87.4 0.1 slice.165
  87.6 0.1 slice.166
  87.7 0.0 copy-start.3
  87.8 0.1 slice.167
  87.9 0.4 copy-done.3
  88.4 0.6 slice_select_fusion
  89.0 3.9 %collective-permute-start.2 = (f32[2,512]{0,1:T(8,128)S(1)}, f32[2,512]{0,1:T(8,128)S(1)}, u32[]{:S(2)}, u32[]{:S(2)}) collective-permute-start(f32[2,512]{0,1:T(8,128)S(1)} %slice_select_fusion), channel_id=1, source_target_pairs={{16,0},{32,16},{48,32},{64,48},{80,64},{96,80},{112,96},{128,112},... | collective-permute-start | bytes 12296 | tf_op jit(solution)/shard_map/ppermute | solution.py:87
  92.9 0.1 maximum_select_fusion.7
  93.1 0.1 maximum_select_fusion.6
  93.2 0.1 maximum_select_fusion.5
  93.4 0.1 maximum_select_fusion.4
  93.5 0.1 slice.175
  93.6 0.6 concatenate.106
  94.2 1.9 %collective-permute-start.3 = (f32[2,512]{0,1:T(8,128)S(1)}, f32[2,512]{0,1:T(8,128)S(1)}, u32[]{:S(2)}, u32[]{:S(2)}) collective-permute-start(f32[2,512]{0,1:T(8,128)S(1)} %concatenate.106), channel_id=1, source_target_pairs={{0,16},{16,32},{32,48},{48,64},{64,80},{80,96},{96,112},{112,128},... | collective-permute-start | bytes 12296 | tf_op jit(solution)/shard_map/ppermute | solution.py:86
  96.2 3.4 %collective-permute-done.2 = f32[2,512]{0,1:T(8,128)S(1)} collective-permute-done((f32[2,512]{0,1:T(8,128)S(1)}, f32[2,512]{0,1:T(8,128)S(1)}, u32[]{:S(2)}, u32[]{:S(2)}) %collective-permute-start.2) | collective-permute-done | bytes 4128 | tf_op jit(solution)/shard_map/ppermute | solution.py:87
  99.6 0.3 slice_reduce_fusion.3
  99.9 6.0 %collective-permute-done.3 = f32[2,512]{0,1:T(8,128)S(1)} collective-permute-done((f32[2,512]{0,1:T(8,128)S(1)}, f32[2,512]{0,1:T(8,128)S(1)}, u32[]{:S(2)}, u32[]{:S(2)}) %collective-permute-start.3) | collective-permute-done | bytes 4128 | tf_op jit(solution)/shard_map/ppermute | solution.py:86
  105.9 0.3 slice_reduce_fusion.2
  106.2 1.0 fusion.2
  (12 shorter events, 0.3 us)
Async XLA Ops:
  0.0 1.4 %copy-start = (s32[512,128]{1,0:T(8,128)S(1)}, s32[512,128]{1,0:T(8,128)}, u32[]{:S(2)}) copy-start(s32[512,128]{1,0:T(8,128)} %param.6) | copy-start | bytes 786436
  0.0 1.6 %copy-start.1 = (bf16[512,128]{1,0:T(8,128)(2,1)S(1)}, bf16[512,128]{1,0:T(8,128)(2,1)}, u32[]{:S(2)}) copy-start(bf16[512,128]{1,0:T(8,128)(2,1)} %param.5) | copy-start | bytes 393220
  3.4 10.5 %copy-start.2 = (s32[128]{0:T(128)S(1)}, s32[128]{0:T(128)}, u32[]{:S(2)}) copy-start(s32[128]{0:T(128)} %param.7) | copy-start | bytes 1540
  3.4 39.9 %all-to-all-start = ((bf16[8,16,4224]{2,1,0:T(8,128)(2,1)}), bf16[8,16,4224]{2,1,0:T(8,128)(2,1)S(1)}, u32[]{:S(2)}, u32[]{:S(2)}) async-start(bf16[8,16,4224]{2,1,0:T(8,128)(2,1)} %bitcast.84), calls=%async_computation | async-start | bytes 2162688 | tf_op jit(solution)/shard_map/all_to_all | solution.py:118
  43.8 15.7 %collective-permute-start = (bf16[8,32,1024]{2,1,0:T(8,128)(2,1)S(1)}, bf16[8,32,1024]{2,1,0:T(8,128)(2,1)S(1)}, u32[]{:S(2)}, u32[]{:S(2)}) collective-permute-start(bf16[8,32,1024]{2,1,0:T(8,128)(2,1)S(1)} %copy.28), channel_id=1, source_target_pairs={{0,1},{1,0},{2,3},{3,2},{4,5},{5,4},{6,7},{7,6},{8,9},{9,8},{10,11... | collective-permute-start | bytes 1572872 | tf_op jit(solution)/shard_map/ppermute | solution.py:122
  47.4 13.2 %collective-permute-start.1 = (bf16[8,130,256]{2,0,1:T(8,128)(2,1)S(1)}, bf16[8,130,256]{2,0,1:T(8,128)(2,1)S(1)}, u32[]{:S(2)}, u32[]{:S(2)}) collective-permute-start(bf16[8,130,256]{2,0,1:T(8,128)(2,1)S(1)} %bitcast.100), channel_id=1, source_target_pairs={{0,16},{16,0},{32,48},{48,32},{64,80},{80,64},{96,112},{112,96},{1... | collective-permute-start | bytes 1597448 | tf_op jit(solution)/shard_map/ppermute | solution.py:123
  72.0 14.8 %all-to-all-start.1 = ((f32[8,16,512]{2,1,0:T(8,128)}), f32[8,16,512]{2,1,0:T(8,128)S(1)}, u32[]{:S(2)}, u32[]{:S(2)}) async-start(f32[8,16,512]{2,1,0:T(8,128)} %shard_map.46), calls=%async_computation.1 | async-start | bytes 524288 | tf_op jit(solution)/shard_map/all_to_all | solution.py:127
  87.7 0.7 copy-start.3
  89.0 10.5 %collective-permute-start.2 = (f32[2,512]{0,1:T(8,128)S(1)}, f32[2,512]{0,1:T(8,128)S(1)}, u32[]{:S(2)}, u32[]{:S(2)}) collective-permute-start(f32[2,512]{0,1:T(8,128)S(1)} %slice_select_fusion), channel_id=1, source_target_pairs={{16,0},{32,16},{48,32},{64,48},{80,64},{96,80},{112,96},{128,112},... | collective-permute-start | bytes 12296 | tf_op jit(solution)/shard_map/ppermute | solution.py:87
  94.2 11.7 %collective-permute-start.3 = (f32[2,512]{0,1:T(8,128)S(1)}, f32[2,512]{0,1:T(8,128)S(1)}, u32[]{:S(2)}, u32[]{:S(2)}) collective-permute-start(f32[2,512]{0,1:T(8,128)S(1)} %concatenate.106), channel_id=1, source_target_pairs={{0,16},{16,32},{32,48},{48,64},{64,80},{80,96},{96,112},{112,128},... | collective-permute-start | bytes 12296 | tf_op jit(solution)/shard_map/ppermute | solution.py:86
